TPU v7x, 128 devices: a whole 4x4x4 slice. The times are simulated.
128 devices in a mesh: dp: 32 (over y, x, core), proto: 4 (over z).
Axes of the slice: x: 4, y: 4, z: 4, core: 2. Of those that a mesh axis runs over, the one named last changes fastest.
Arguments:
- features: bfloat16 [16384, 2048], P('dp', 'proto'), may hold values from -8 to 8
- head_weight: bfloat16 [2048, 256], P('proto'), may hold values from -1 to 1
- prototypes: bfloat16 [256, 32768], P(None, 'proto'), may hold values from -1 to 1
Outputs:
- codes: bfloat16 [16384, 32768], P('dp', 'proto')
- proto_grad: float32 [256, 32768], P('dp', 'proto')
- head_grad: float32 [256, 2048], P('dp', 'proto')
All inputs are finite; a program needn't handle non-finite values.
Results may differ from a plain program's by a relative error of at most 0.009.
Values may be sent and summed in bfloat16 or wider, within the bound.
No kernel may reach another device: no remote copies, remote signals or barrier semaphores. Data moves between devices by JAX's collectives and lax.ppermute only.
A program may use at most 128 MiB of HBM per device.

v0:
```python
import math

import jax
import jax.numpy as jnp
from jax import lax
from jax.experimental import pallas as pl
from jax.sharding import Mesh
from jax.sharding import PartitionSpec as P

PROTOS = 32768
ITERS = 3


sink_eps = 0.05
soft_temp = 0.1

DP = ("y", "x", "core")
SIZES = {"y": 4, "x": 4, "core": 2, "z": 4}
F32 = jnp.float32
BF16 = jnp.bfloat16


def _shift(v, ax, k):
    n = SIZES[ax]
    return lax.ppermute(v, ax, [(i, (i + k) % n) for i in range(n)])


def _allsum(v, ax, dt=None):
    sent = v if dt is None else v.astype(dt)
    acc = v
    for k in range(1, SIZES[ax]):
        acc = acc + _shift(sent, ax, k).astype(v.dtype)
    return acc


def _allsum_dp(v):
    for ax in ("core", "x", "y"):
        v = _allsum(v, ax)
    return v


def _rs(a, ax, axis, dt=None):
    n = SIZES[ax]
    i = lax.axis_index(ax)
    acc = lax.dynamic_index_in_dim(a, i, axis, keepdims=False)
    for k in range(1, n):
        blk = lax.dynamic_index_in_dim(a, (i + k) % n, axis, keepdims=False)
        if dt is not None:
            blk = blk.astype(dt)
        acc = acc + _shift(blk, ax, k).astype(a.dtype)
    return acc


def _ag(v, ax):
    n = SIZES[ax]
    i = lax.axis_index(ax)
    parts = [v] + [_shift(v, ax, k) for k in range(1, n)]
    rel = jnp.stack(parts)
    idx = (i - jnp.arange(n)) % n
    return rel[idx]


def _rs_dp(part, dt):
    R, N = part.shape
    a = part.reshape(SIZES["y"], SIZES["x"], SIZES["core"], R // 32, N)
    a = _rs(a, "core", 2, dt)
    a = _rs(a, "x", 1, dt)
    a = _rs(a, "y", 0, dt)
    return a


def _score_kernel(u_ref, n_ref, s_ref, col_ref, rs_ref):
    j = pl.program_id(0)
    sc = jnp.dot(u_ref[...], n_ref[...], preferred_element_type=F32)
    s = jnp.exp(sc * (1.0 / soft_temp))
    s_ref[...] = s
    col_ref[...] = jnp.sum(s * s, axis=0, keepdims=True)

    @pl.when(j == 0)
    def _():
        rs_ref[...] = jnp.zeros_like(rs_ref)

    rs_ref[...] += jnp.sum(s, axis=1, keepdims=True)


def _scores(unit_b, normed, bp=1024):
    T, E = unit_b.shape
    Pn = normed.shape[1]
    soft, col, rs = pl.pallas_call(
        _score_kernel,
        grid=(Pn // bp,),
        in_specs=[pl.BlockSpec((T, E), lambda j: (0, 0)), pl.BlockSpec((E, bp), lambda j: (0, j))],
        out_specs=[
            pl.BlockSpec((T, bp), lambda j: (0, j)),
            pl.BlockSpec((1, bp), lambda j: (0, j)),
            pl.BlockSpec((T, 1), lambda j: (0, 0)),
        ],
        out_shape=[
            jax.ShapeDtypeStruct((T, Pn), F32),
            jax.ShapeDtypeStruct((1, Pn), F32),
            jax.ShapeDtypeStruct((T, 1), F32),
        ],
    )(unit_b, normed)
    return soft, col[0], rs[:, 0]


def _col_kernel(s_ref, r_ref, o_ref):
    s = s_ref[...]
    o_ref[...] = jnp.sum(s * s * r_ref[...], axis=0, keepdims=True)


def _colpass(soft, r, bp=1024):
    T, Pn = soft.shape
    return pl.pallas_call(
        _col_kernel,
        grid=(Pn // bp,),
        in_specs=[pl.BlockSpec((T, bp), lambda j: (0, j)), pl.BlockSpec((T, 1), lambda j: (0, 0))],
        out_specs=pl.BlockSpec((1, bp), lambda j: (0, j)),
        out_shape=jax.ShapeDtypeStruct((1, Pn), F32),
    )(soft, r.reshape(T, 1))[0]


def _row_kernel(s_ref, c_ref, o_ref):
    s = s_ref[...]
    o_ref[...] = jnp.sum(s * s * c_ref[...], axis=1, keepdims=True)


def _rowpass(soft, c, bt=64):
    T, Pn = soft.shape
    return pl.pallas_call(
        _row_kernel,
        grid=(T // bt,),
        in_specs=[pl.BlockSpec((bt, Pn), lambda i: (i, 0)), pl.BlockSpec((1, Pn), lambda i: (0, 0))],
        out_specs=pl.BlockSpec((bt, 1), lambda i: (i, 0)),
        out_shape=jax.ShapeDtypeStruct((T, 1), F32),
    )(soft, c.reshape(1, Pn))[:, 0]


def on_device(features, head_weight, prototypes):
    partial_proj = jnp.dot(features, head_weight, preferred_element_type=F32)
    T, E = partial_proj.shape
    nz = SIZES["z"]
    proj_blk = _rs(partial_proj.reshape(nz, T // nz, E), "z", 0)
    projected = _ag(proj_blk, "z").reshape(T, E)
    length = jnp.sqrt(jnp.sum(projected * projected, axis=1, keepdims=True) + 1e-06)
    unit = projected / length
    unit_b = unit.astype(BF16)
    proto_f = prototypes.astype(F32)
    normed = (proto_f / jnp.sqrt(jnp.sum(proto_f * proto_f, axis=0, keepdims=True) + 1e-06)).astype(BF16)
    soft, col0, soft_local = _scores(unit_b, normed)
    kern = soft * soft
    r = None
    soft_total = None
    for step in range(ITERS):
        colpart = col0 if r is None else _colpass(soft, r)
        c = 1.0 / _allsum_dp(colpart)
        rowpart = _rowpass(soft, c)
        if step == 0:
            both = _allsum(jnp.stack([rowpart, soft_local]), "z")
            row, soft_total = both[0], both[1]
        else:
            row = _allsum(rowpart, "z")
        r = 1.0 / row
    plan = kern * c[None, :] * r[:, None]
    probs = soft / soft_total[:, None]
    codes = (PROTOS * plan).astype(BF16)
    tokens_all = 32 * T
    factor = PROTOS / (soft_temp * math.sqrt(tokens_all))
    dscore = ((probs - plan) * factor).astype(BF16)
    half = dscore.shape[1] // 2
    pg = []
    for h in range(2):
        pg_part = lax.dot_general(
            unit_b, dscore[:, h * half:(h + 1) * half], (((0,), (0,)), ((), ())), preferred_element_type=F32
        )
        pg.append(_rs_dp(pg_part, BF16))
    proto_grad = jnp.concatenate(pg, axis=1)
    dunit_part = lax.dot_general(dscore, normed, (((1,), (1,)), ((), ())), preferred_element_type=F32)
    dunit = _allsum(dunit_part, "z", BF16)
    dproj = ((dunit - unit * jnp.sum(unit * dunit, axis=1, keepdims=True)) / length).astype(BF16)
    head_part = lax.dot_general(dproj, features, (((0,), (0,)), ((), ())), preferred_element_type=F32)
    head_grad = _rs_dp(head_part, BF16)
    return (codes, proto_grad, head_grad)


def solution(mesh):
    devs = mesh.devices.reshape(SIZES["y"], SIZES["x"], SIZES["core"], SIZES["z"])
    m4 = Mesh(devs, ("y", "x", "core", "z"))
    in_specs = (P(DP, "z"), P("z", None), P(None, "z"))
    out_specs = (P(DP, "z"), P(DP, "z"), P(DP, "z"))
    return jax.shard_map(on_device, mesh=m4, in_specs=in_specs, out_specs=out_specs, check_vma=False)
```

profile of v0, /device:TPU:6, one launch (start us, length us, event | category | flops | bytes accessed | tf_op | source)
XLA Modules:
  0.0 242.4 jit_solution(5316719602699539694)
XLA Ops:
  3.1 2.0 collective-permute-start
  5.1 3.6 %collective-permute-start.1 = (f32[128,256]{1,0:T(8,128)S(1)}, f32[128,256]{1,0:T(8,128)S(1)}, u32[]{:S(2)}, u32[]{:S(2)}) collective-permute-start(f32[128,256]{1,0:T(8,128)S(1)} %get-tuple-element.27), channel_id=1, source_target_pairs={{0,2},{1,3},{2,0},{3,1},{4,6},{5,7},{6,4},{7,5},{8,10},{9,11},{10,... | collective-permute-start | bytes 393224 | tf_op jit(solution)/shard_map/ppermute | solution.py:25
  9.7 3.1 %fusion = f32[8192]{0:T(1024)S(1)} fusion(bf16[256,8192]{1,0:T(8,128)(2,1)} %param.5), kind=kLoop, calls=%fused_computation.6 | loop fusion | flops 6283264 | bytes 4227072 | tf_op jit(solution)/shard_map/reduce_sum | solution.py:149
  12.8 2.9 %fusion.1.n_ref = bf16[256,8192]{1,0:T(8,128)(2,1)} fusion(bf16[256,8192]{1,0:T(8,128)(2,1)S(1)} %copy-done.1, f32[8192]{0:T(1024)S(1)} %add_sqrt_fusion), kind=kLoop, calls=%fused_computation.7 | loop fusion | flops 6291456 | bytes 8421376 | tf_op jit(solution)/shard_map/convert_element_type | solution.py:149
  16.9 1.6 collective-permute-start.4
  19.7 4.7 %collective-permute-done.3 = f32[128,256]{1,0:T(8,128)S(1)} collective-permute-done((f32[128,256]{1,0:T(8,128)S(1)}, f32[128,256]{1,0:T(8,128)S(1)}, u32[]{:S(2)}, u32[]{:S(2)}) %collective-permute-start.3) | collective-permute-done | bytes 131104 | tf_op jit(solution)/shard_map/ppermute | solution.py:25
  26.5 10.7 %shard_map.58 = (f32[512,8192]{1,0:T(8,128)}, f32[1,8192]{1,0:T(1,128)}, f32[512,1]{1,0:T(8,128)}) custom-call(bf16[512,256]{1,0:T(8,128)(2,1)} %get-tuple-element.9.u_ref, bf16[256,8192]{1,0:T(8,128)(2,1)} %fusion.1.n_ref), custom_call_target="tpu_custom_call" | custom-call | tf_op jit(solution)/shard_map/pallas_call | solution.py:89
  40.0 2.4 collective-permute-start.8
  43.5 1.9 collective-permute-done.8
  45.4 2.1 collective-permute-done.9
  47.5 1.6 collective-permute-start.10
  49.2 2.9 %collective-permute-start.11 = (f32[8192]{0:T(1024)S(1)}, f32[8192]{0:T(1024)S(1)}, u32[]{:S(2)}, u32[]{:S(2)}) collective-permute-start(f32[8192]{0:T(1024)S(1)} %add_add_fusion.2), channel_id=1, source_target_pairs={{0,64},{32,96},{64,0},{96,32},{1,65},{33,97},{65,1},{97,33},{2,66}... | collective-permute-start | bytes 98312 | tf_op jit(solution)/shard_map/ppermute | solution.py:25
  56.6 9.4 %shard_map.59 = f32[512,1]{1,0:T(8,128)} custom-call(f32[512,8192]{1,0:T(8,128)} %get-tuple-element.6.s_ref, f32[1,8192]{1,0:T(1,128)} %bitcast.161), custom_call_target="tpu_custom_call" | custom-call | tf_op jit(solution)/shard_map/pallas_call | solution.py:130
  68.0 3.3 %collective-permute-start.14 = (f32[2,512]{1,0:T(2,128)S(1)}, f32[2,512]{1,0:T(2,128)S(1)}, u32[]{:S(2)}, u32[]{:S(2)}) collective-permute-start(f32[2,512]{1,0:T(2,128)S(1)} %pad_maximum_fusion.2), channel_id=1, source_target_pairs={{0,2},{1,3},{2,0},{3,1},{4,6},{5,7},{6,4},{7,5},{8,10},{9,11},{10,... | collective-permute-start | bytes 12296 | tf_op jit(solution)/shard_map/ppermute | solution.py:25
  73.1 1.8 collective-permute-done.15
  75.8 9.3 %shard_map.60 = f32[1,8192]{1,0:T(1,128)} custom-call(f32[512,8192]{1,0:T(8,128)} %get-tuple-element.6.s_ref, f32[512,1]{1,0:T(8,128)} %copy.16.r_ref), custom_call_target="tpu_custom_call" | custom-call | tf_op jit(solution)/shard_map/pallas_call | solution.py:114
  89.3 1.9 collective-permute-done.17
  91.2 2.1 collective-permute-done.18
  94.1 3.8 %collective-permute-start.21 = (f32[8192]{0:T(1024)S(1)}, f32[8192]{0:T(1024)S(1)}, u32[]{:S(2)}, u32[]{:S(2)}) collective-permute-start(f32[8192]{0:T(1024)S(1)} %add_add_fusion.1), channel_id=1, source_target_pairs={{0,64},{32,96},{64,0},{96,32},{1,65},{33,97},{65,1},{97,33},{2,66}... | collective-permute-start | bytes 98312 | tf_op jit(solution)/shard_map/ppermute | solution.py:25
  100.2 1.7 collective-permute-done.22
  102.5 9.4 %shard_map.61 = f32[512,1]{1,0:T(8,128)} custom-call(f32[512,8192]{1,0:T(8,128)} %get-tuple-element.6.s_ref, f32[1,8192]{1,0:T(1,128)} %bitcast.162), custom_call_target="tpu_custom_call" | custom-call | tf_op jit(solution)/shard_map/pallas_call | solution.py:130
  113.1 2.7 %collective-permute-start.24 = (f32[512]{0:T(512)S(1)}, f32[512]{0:T(512)S(1)}, u32[]{:S(2)}, u32[]{:S(2)}) collective-permute-start(f32[512]{0:T(512)S(1)} %reduce.3), channel_id=1, source_target_pairs={{0,2},{1,3},{2,0},{3,1},{4,6},{5,7},{6,4},{7,5},{8,10},{9,11},{10,... | collective-permute-start | bytes 6152 | tf_op jit(solution)/shard_map/ppermute | solution.py:25
  115.8 1.5 collective-permute-start.25
  120.2 9.3 %shard_map.62 = f32[1,8192]{1,0:T(1,128)} custom-call(f32[512,8192]{1,0:T(8,128)} %get-tuple-element.6.s_ref, f32[512,1]{1,0:T(8,128)} %copy.17.r_ref), custom_call_target="tpu_custom_call" | custom-call | tf_op jit(solution)/shard_map/pallas_call | solution.py:114
  131.7 2.0 collective-permute-start.27
  135.8 3.2 %collective-permute-done.28 = f32[8192]{0:T(1024)S(1)} collective-permute-done((f32[8192]{0:T(1024)S(1)}, f32[8192]{0:T(1024)S(1)}, u32[]{:S(2)}, u32[]{:S(2)}) %collective-permute-start.28) | collective-permute-done | bytes 32800 | tf_op jit(solution)/shard_map/ppermute | solution.py:25
  139.8 2.7 %collective-permute-start.31 = (f32[8192]{0:T(1024)S(1)}, f32[8192]{0:T(1024)S(1)}, u32[]{:S(2)}, u32[]{:S(2)}) collective-permute-start(f32[8192]{0:T(1024)S(1)} %add_add_fusion), channel_id=1, source_target_pairs={{0,64},{32,96},{64,0},{96,32},{1,65},{33,97},{65,1},{97,33},{2,66}... | collective-permute-start | bytes 98312 | tf_op jit(solution)/shard_map/ppermute | solution.py:25
  147.1 9.4 %shard_map.63 = f32[512,1]{1,0:T(8,128)} custom-call(f32[512,8192]{1,0:T(8,128)} %get-tuple-element.6.s_ref, f32[1,8192]{1,0:T(1,128)} %bitcast.154), custom_call_target="tpu_custom_call" | custom-call | tf_op jit(solution)/shard_map/pallas_call | solution.py:130
  157.6 1.5 collective-permute-start.33
  159.1 2.7 %collective-permute-start.34 = (f32[512]{0:T(512)S(1)}, f32[512]{0:T(512)S(1)}, u32[]{:S(2)}, u32[]{:S(2)}) collective-permute-start(f32[512]{0:T(512)S(1)} %reduce.4), channel_id=1, source_target_pairs={{0,2},{1,3},{2,0},{3,1},{4,6},{5,7},{6,4},{7,5},{8,10},{9,11},{10,... | collective-permute-start | bytes 6152 | tf_op jit(solution)/shard_map/ppermute | solution.py:25
  162.5 1.7 collective-permute-done.34
  165.4 11.1 %multiply_convert_fusion = (bf16[512,8192]{1,0:T(8,128)(2,1)S(1)}, bf16[512,8192]{1,0:T(8,128)(2,1)}) fusion(f32[512,8192]{1,0:T(8,128)} %get-tuple-element.6.s_ref, f32[512]{0:T(512)S(1)} %bitcast.173, f32[512]{0:T(512)S(1)} %add_divide_fusion.3, f32[8192]{0:T(1024)S(1)} %copy-done.4), kind=kLoop, calls=%fused_computation.1 | loop fusion | flops 37748736 | bytes 33591296 | tf_op jit(solution)/shard_map/convert_element_type | solution.py:169
  176.6 2.4 fusion.47
  179.0 2.7 %collective-permute-start.51 = (bf16[512,256]{1,0:T(8,128)(2,1)S(1)}, bf16[512,256]{1,0:T(8,128)(2,1)S(1)}, u32[]{:S(2)}, u32[]{:S(2)}) collective-permute-start(bf16[512,256]{1,0:T(8,128)(2,1)S(1)} %get-tuple-element.36), channel_id=1, source_target_pairs={{0,2},{1,3},{2,0},{3,1},{4,6},{5,7},{6,4},{7,5},{8,10},{9,11},{10,... | collective-permute-start | bytes 786440 | tf_op jit(solution)/shard_map/ppermute | solution.py:25
  184.5 4.9 %collective-permute-done.50 = bf16[512,256]{1,0:T(8,128)(2,1)S(1)} collective-permute-done((bf16[512,256]{1,0:T(8,128)(2,1)S(1)}, bf16[512,256]{1,0:T(8,128)(2,1)S(1)}, u32[]{:S(2)}, u32[]{:S(2)}) %collective-permute-start.50) | collective-permute-done | bytes 262176 | tf_op jit(solution)/shard_map/ppermute | solution.py:25
  196.9 1.9 collective-permute-done.55
  200.8 2.7 %collective-permute-start.58 = (bf16[8,512]{1,0:T(8,128)(2,1)S(1)}, bf16[8,512]{1,0:T(8,128)(2,1)S(1)}, u32[]{:S(2)}, u32[]{:S(2)}) collective-permute-start(bf16[8,512]{1,0:T(8,128)(2,1)S(1)} %get-tuple-element.33), channel_id=1, source_target_pairs={{0,64},{32,96},{64,0},{96,32},{1,65},{33,97},{65,1},{97,33},{2,66}... | collective-permute-start | bytes 24584 | tf_op jit(solution)/shard_map/ppermute | solution.py:25
  204.4 1.6 collective-permute-done.58
  208.2 2.0 collective-permute-start.37
  211.6 3.3 %collective-permute-start.44 = (bf16[4,8,4096]{2,1,0:T(8,128)(2,1)S(1)}, bf16[4,8,4096]{2,1,0:T(8,128)(2,1)S(1)}, u32[]{:S(2)}, u32[]{:S(2)}) collective-permute-start(bf16[4,8,4096]{2,1,0:T(8,128)(2,1)S(1)} %get-tuple-element.16), channel_id=1, source_target_pairs={{0,8},{8,16},{16,24},{24,0},{1,9},{9,17},{17,25},{25,1},{2,10},{10... | collective-permute-start | bytes 786440 | tf_op jit(solution)/shard_map/ppermute | solution.py:25
  216.2 4.4 %collective-permute-done.37 = bf16[4,8,4096]{2,1,0:T(8,128)(2,1)S(1)} collective-permute-done((bf16[4,8,4096]{2,1,0:T(8,128)(2,1)S(1)}, bf16[4,8,4096]{2,1,0:T(8,128)(2,1)S(1)}, u32[]{:S(2)}, u32[]{:S(2)}) %collective-permute-start.37) | collective-permute-done | bytes 262176 | tf_op jit(solution)/shard_map/ppermute | solution.py:25
  220.6 1.5 collective-permute-start.46
  222.1 5.0 %collective-permute-done.39 = bf16[4,8,4096]{2,1,0:T(8,128)(2,1)S(1)} collective-permute-done((bf16[4,8,4096]{2,1,0:T(8,128)(2,1)S(1)}, bf16[4,8,4096]{2,1,0:T(8,128)(2,1)S(1)}, u32[]{:S(2)}, u32[]{:S(2)}) %collective-permute-start.39) | collective-permute-done | bytes 262176 | tf_op jit(solution)/shard_map/ppermute | solution.py:25
  227.4 2.8 %collective-permute-start.41 = (bf16[8,4096]{1,0:T(8,128)(2,1)S(1)}, bf16[8,4096]{1,0:T(8,128)(2,1)S(1)}, u32[]{:S(2)}, u32[]{:S(2)}) collective-permute-start(bf16[8,4096]{1,0:T(8,128)(2,1)S(1)} %get-tuple-element.21), channel_id=1, source_target_pairs={{0,64},{32,96},{64,0},{96,32},{1,65},{33,97},{65,1},{97,33},{2,66}... | collective-permute-start | bytes 196616 | tf_op jit(solution)/shard_map/ppermute | solution.py:25
  231.5 2.3 collective-permute-done.46
  234.0 1.9 collective-permute-start.47
  236.8 1.8 collective-permute-start.49
  239.5 2.1 collective-permute-done.48
  (147 shorter events, 68.0 us)
Async XLA Ops:
  3.1 12.6 %collective-permute-start = (f32[128,256]{1,0:T(8,128)S(1)}, f32[128,256]{1,0:T(8,128)S(1)}, u32[]{:S(2)}, u32[]{:S(2)}) collective-permute-start(f32[128,256]{1,0:T(8,128)S(1)} %get-tuple-element.25), channel_id=1, source_target_pairs={{0,1},{1,2},{2,3},{3,0},{4,5},{5,6},{6,7},{7,4},{8,9},{9,10},{10,1... | collective-permute-start | bytes 393224 | tf_op jit(solution)/shard_map/ppermute | solution.py:25
  5.1 10.6 %collective-permute-start.1 = (f32[128,256]{1,0:T(8,128)S(1)}, f32[128,256]{1,0:T(8,128)S(1)}, u32[]{:S(2)}, u32[]{:S(2)}) collective-permute-start(f32[128,256]{1,0:T(8,128)S(1)} %get-tuple-element.27), channel_id=1, source_target_pairs={{0,2},{1,3},{2,0},{3,1},{4,6},{5,7},{6,4},{7,5},{8,10},{9,11},{10,... | collective-permute-start | bytes 393224 | tf_op jit(solution)/shard_map/ppermute | solution.py:25
  8.7 7.1 %collective-permute-start.2 = (f32[128,256]{1,0:T(8,128)S(1)}, f32[128,256]{1,0:T(8,128)S(1)}, u32[]{:S(2)}, u32[]{:S(2)}) collective-permute-start(f32[128,256]{1,0:T(8,128)S(1)} %get-tuple-element.26), channel_id=1, source_target_pairs={{0,3},{1,0},{2,1},{3,2},{4,7},{5,4},{6,5},{7,6},{8,11},{9,8},{10,9... | collective-permute-start | bytes 393224 | tf_op jit(solution)/shard_map/ppermute | solution.py:25
  15.8 8.7 %collective-permute-start.3 = (f32[128,256]{1,0:T(8,128)S(1)}, f32[128,256]{1,0:T(8,128)S(1)}, u32[]{:S(2)}, u32[]{:S(2)}) collective-permute-start(f32[128,256]{1,0:T(8,128)S(1)} %fusion.25), channel_id=1, source_target_pairs={{0,1},{1,2},{2,3},{3,0},{4,5},{5,6},{6,7},{7,4},{8,9},{9,10},{10,1... | collective-permute-start | bytes 393224 | tf_op jit(solution)/shard_map/ppermute | solution.py:25
  16.9 7.6 %collective-permute-start.4 = (f32[128,256]{1,0:T(8,128)S(1)}, f32[128,256]{1,0:T(8,128)S(1)}, u32[]{:S(2)}, u32[]{:S(2)}) collective-permute-start(f32[128,256]{1,0:T(8,128)S(1)} %fusion.25), channel_id=1, source_target_pairs={{0,2},{1,3},{2,0},{3,1},{4,6},{5,7},{6,4},{7,5},{8,10},{9,11},{10,... | collective-permute-start | bytes 393224 | tf_op jit(solution)/shard_map/ppermute | solution.py:25
  18.4 6.4 %collective-permute-start.5 = (f32[128,256]{1,0:T(8,128)S(1)}, f32[128,256]{1,0:T(8,128)S(1)}, u32[]{:S(2)}, u32[]{:S(2)}) collective-permute-start(f32[128,256]{1,0:T(8,128)S(1)} %fusion.25), channel_id=1, source_target_pairs={{0,3},{1,0},{2,1},{3,2},{4,7},{5,4},{6,5},{7,6},{8,11},{9,8},{10,9... | collective-permute-start | bytes 393224 | tf_op jit(solution)/shard_map/ppermute | solution.py:25
  39.5 4.0 %collective-permute-start.7 = (f32[8192]{0:T(1024)S(1)}, f32[8192]{0:T(1024)S(1)}, u32[]{:S(2)}, u32[]{:S(2)}) collective-permute-start(f32[8192]{0:T(1024)S(1)} %add.394), channel_id=1, source_target_pairs={{0,8},{8,16},{16,24},{24,0},{1,9},{9,17},{17,25},{25,1},{2,10},{10... | collective-permute-start | bytes 98312 | tf_op jit(solution)/shard_map/ppermute | solution.py:25
  40.0 5.4 %collective-permute-start.8 = (f32[8192]{0:T(1024)S(1)}, f32[8192]{0:T(1024)S(1)}, u32[]{:S(2)}, u32[]{:S(2)}) collective-permute-start(f32[8192]{0:T(1024)S(1)} %add.394), channel_id=1, source_target_pairs={{0,16},{8,24},{16,0},{24,8},{1,17},{9,25},{17,1},{25,9},{2,18},{10... | collective-permute-start | bytes 98312 | tf_op jit(solution)/shard_map/ppermute | solution.py:25
  42.4 5.1 %collective-permute-start.9 = (f32[8192]{0:T(1024)S(1)}, f32[8192]{0:T(1024)S(1)}, u32[]{:S(2)}, u32[]{:S(2)}) collective-permute-start(f32[8192]{0:T(1024)S(1)} %add.394), channel_id=1, source_target_pairs={{0,24},{8,0},{16,8},{24,16},{1,25},{9,1},{17,9},{25,17},{2,26},{10... | collective-permute-start | bytes 98312 | tf_op jit(solution)/shard_map/ppermute | solution.py:25
  47.5 7.0 %collective-permute-start.10 = (f32[8192]{0:T(1024)S(1)}, f32[8192]{0:T(1024)S(1)}, u32[]{:S(2)}, u32[]{:S(2)}) collective-permute-start(f32[8192]{0:T(1024)S(1)} %add_add_fusion.2), channel_id=1, source_target_pairs={{0,32},{32,64},{64,96},{96,0},{1,33},{33,65},{65,97},{97,1},{2,34}... | collective-permute-start | bytes 98312 | tf_op jit(solution)/shard_map/ppermute | solution.py:25
  49.2 5.4 %collective-permute-start.11 = (f32[8192]{0:T(1024)S(1)}, f32[8192]{0:T(1024)S(1)}, u32[]{:S(2)}, u32[]{:S(2)}) collective-permute-start(f32[8192]{0:T(1024)S(1)} %add_add_fusion.2), channel_id=1, source_target_pairs={{0,64},{32,96},{64,0},{96,32},{1,65},{33,97},{65,1},{97,33},{2,66}... | collective-permute-start | bytes 98312 | tf_op jit(solution)/shard_map/ppermute | solution.py:25
  67.1 4.9 %collective-permute-start.13 = (f32[2,512]{1,0:T(2,128)S(1)}, f32[2,512]{1,0:T(2,128)S(1)}, u32[]{:S(2)}, u32[]{:S(2)}) collective-permute-start(f32[2,512]{1,0:T(2,128)S(1)} %pad_maximum_fusion.2), channel_id=1, source_target_pairs={{0,1},{1,2},{2,3},{3,0},{4,5},{5,6},{6,7},{7,4},{8,9},{9,10},{10,1... | collective-permute-start | bytes 12296 | tf_op jit(solution)/shard_map/ppermute | solution.py:25
  68.0 5.1 %collective-permute-start.14 = (f32[2,512]{1,0:T(2,128)S(1)}, f32[2,512]{1,0:T(2,128)S(1)}, u32[]{:S(2)}, u32[]{:S(2)}) collective-permute-start(f32[2,512]{1,0:T(2,128)S(1)} %pad_maximum_fusion.2), channel_id=1, source_target_pairs={{0,2},{1,3},{2,0},{3,1},{4,6},{5,7},{6,4},{7,5},{8,10},{9,11},{10,... | collective-permute-start | bytes 12296 | tf_op jit(solution)/shard_map/ppermute | solution.py:25
  87.9 5.4 %collective-permute-start.18 = (f32[8192]{0:T(1024)S(1)}, f32[8192]{0:T(1024)S(1)}, u32[]{:S(2)}, u32[]{:S(2)}) collective-permute-start(f32[8192]{0:T(1024)S(1)} %add.404), channel_id=1, source_target_pairs={{0,16},{8,24},{16,0},{24,8},{1,17},{9,25},{17,1},{25,9},{2,18},{10... | collective-permute-start | bytes 98312 | tf_op jit(solution)/shard_map/ppermute | solution.py:25
  88.8 5.1 %collective-permute-start.19 = (f32[8192]{0:T(1024)S(1)}, f32[8192]{0:T(1024)S(1)}, u32[]{:S(2)}, u32[]{:S(2)}) collective-permute-start(f32[8192]{0:T(1024)S(1)} %add.404), channel_id=1, source_target_pairs={{0,24},{8,0},{16,8},{24,16},{1,25},{9,1},{17,9},{25,17},{2,26},{10... | collective-permute-start | bytes 98312 | tf_op jit(solution)/shard_map/ppermute | solution.py:25
  93.9 5.2 %collective-permute-start.20 = (f32[8192]{0:T(1024)S(1)}, f32[8192]{0:T(1024)S(1)}, u32[]{:S(2)}, u32[]{:S(2)}) collective-permute-start(f32[8192]{0:T(1024)S(1)} %add_add_fusion.1), channel_id=1, source_target_pairs={{0,32},{32,64},{64,96},{96,0},{1,33},{33,65},{65,97},{97,1},{2,34}... | collective-permute-start | bytes 98312 | tf_op jit(solution)/shard_map/ppermute | solution.py:25
  94.1 6.1 %collective-permute-start.21 = (f32[8192]{0:T(1024)S(1)}, f32[8192]{0:T(1024)S(1)}, u32[]{:S(2)}, u32[]{:S(2)}) collective-permute-start(f32[8192]{0:T(1024)S(1)} %add_add_fusion.1), channel_id=1, source_target_pairs={{0,64},{32,96},{64,0},{96,32},{1,65},{33,97},{65,1},{97,33},{2,66}... | collective-permute-start | bytes 98312 | tf_op jit(solution)/shard_map/ppermute | solution.py:25
  113.0 4.9 %collective-permute-start.23 = (f32[512]{0:T(512)S(1)}, f32[512]{0:T(512)S(1)}, u32[]{:S(2)}, u32[]{:S(2)}) collective-permute-start(f32[512]{0:T(512)S(1)} %reduce.3), channel_id=1, source_target_pairs={{0,1},{1,2},{2,3},{3,0},{4,5},{5,6},{6,7},{7,4},{8,9},{9,10},{10,1... | collective-permute-start | bytes 6152 | tf_op jit(solution)/shard_map/ppermute | solution.py:25
  113.1 5.2 %collective-permute-start.24 = (f32[512]{0:T(512)S(1)}, f32[512]{0:T(512)S(1)}, u32[]{:S(2)}, u32[]{:S(2)}) collective-permute-start(f32[512]{0:T(512)S(1)} %reduce.3), channel_id=1, source_target_pairs={{0,2},{1,3},{2,0},{3,1},{4,6},{5,7},{6,4},{7,5},{8,10},{9,11},{10,... | collective-permute-start | bytes 6152 | tf_op jit(solution)/shard_map/ppermute | solution.py:25
  131.7 4.2 %collective-permute-start.27 = (f32[8192]{0:T(1024)S(1)}, f32[8192]{0:T(1024)S(1)}, u32[]{:S(2)}, u32[]{:S(2)}) collective-permute-start(f32[8192]{0:T(1024)S(1)} %add.414), channel_id=1, source_target_pairs={{0,8},{8,16},{16,24},{24,0},{1,9},{9,17},{17,25},{25,1},{2,10},{10... | collective-permute-start | bytes 98312 | tf_op jit(solution)/shard_map/ppermute | solution.py:25
  133.7 5.4 %collective-permute-start.28 = (f32[8192]{0:T(1024)S(1)}, f32[8192]{0:T(1024)S(1)}, u32[]{:S(2)}, u32[]{:S(2)}) collective-permute-start(f32[8192]{0:T(1024)S(1)} %add.414), channel_id=1, source_target_pairs={{0,16},{8,24},{16,0},{24,8},{1,17},{9,25},{17,1},{25,9},{2,18},{10... | collective-permute-start | bytes 98312 | tf_op jit(solution)/shard_map/ppermute | solution.py:25
  134.6 5.1 %collective-permute-start.29 = (f32[8192]{0:T(1024)S(1)}, f32[8192]{0:T(1024)S(1)}, u32[]{:S(2)}, u32[]{:S(2)}) collective-permute-start(f32[8192]{0:T(1024)S(1)} %add.414), channel_id=1, source_target_pairs={{0,24},{8,0},{16,8},{24,16},{1,25},{9,1},{17,9},{25,17},{2,26},{10... | collective-permute-start | bytes 98312 | tf_op jit(solution)/shard_map/ppermute | solution.py:25
  139.7 5.2 %collective-permute-start.30 = (f32[8192]{0:T(1024)S(1)}, f32[8192]{0:T(1024)S(1)}, u32[]{:S(2)}, u32[]{:S(2)}) collective-permute-start(f32[8192]{0:T(1024)S(1)} %add_add_fusion), channel_id=1, source_target_pairs={{0,32},{32,64},{64,96},{96,0},{1,33},{33,65},{65,97},{97,1},{2,34}... | collective-permute-start | bytes 98312 | tf_op jit(solution)/shard_map/ppermute | solution.py:25
  139.8 5.4 %collective-permute-start.31 = (f32[8192]{0:T(1024)S(1)}, f32[8192]{0:T(1024)S(1)}, u32[]{:S(2)}, u32[]{:S(2)}) collective-permute-start(f32[8192]{0:T(1024)S(1)} %add_add_fusion), channel_id=1, source_target_pairs={{0,64},{32,96},{64,0},{96,32},{1,65},{33,97},{65,1},{97,33},{2,66}... | collective-permute-start | bytes 98312 | tf_op jit(solution)/shard_map/ppermute | solution.py:25
  157.6 4.9 %collective-permute-start.33 = (f32[512]{0:T(512)S(1)}, f32[512]{0:T(512)S(1)}, u32[]{:S(2)}, u32[]{:S(2)}) collective-permute-start(f32[512]{0:T(512)S(1)} %reduce.4), channel_id=1, source_target_pairs={{0,1},{1,2},{2,3},{3,0},{4,5},{5,6},{6,7},{7,4},{8,9},{9,10},{10,1... | collective-permute-start | bytes 6152 | tf_op jit(solution)/shard_map/ppermute | solution.py:25
  159.1 5.1 %collective-permute-start.34 = (f32[512]{0:T(512)S(1)}, f32[512]{0:T(512)S(1)}, u32[]{:S(2)}, u32[]{:S(2)}) collective-permute-start(f32[512]{0:T(512)S(1)} %reduce.4), channel_id=1, source_target_pairs={{0,2},{1,3},{2,0},{3,1},{4,6},{5,7},{6,4},{7,5},{8,10},{9,11},{10,... | collective-permute-start | bytes 6152 | tf_op jit(solution)/shard_map/ppermute | solution.py:25
  178.9 10.5 %collective-permute-start.50 = (bf16[512,256]{1,0:T(8,128)(2,1)S(1)}, bf16[512,256]{1,0:T(8,128)(2,1)S(1)}, u32[]{:S(2)}, u32[]{:S(2)}) collective-permute-start(bf16[512,256]{1,0:T(8,128)(2,1)S(1)} %get-tuple-element.36), channel_id=1, source_target_pairs={{0,1},{1,2},{2,3},{3,0},{4,5},{5,6},{6,7},{7,4},{8,9},{9,10},{10,1... | collective-permute-start | bytes 786440 | tf_op jit(solution)/shard_map/ppermute | solution.py:25
  179.0 10.4 %collective-permute-start.51 = (bf16[512,256]{1,0:T(8,128)(2,1)S(1)}, bf16[512,256]{1,0:T(8,128)(2,1)S(1)}, u32[]{:S(2)}, u32[]{:S(2)}) collective-permute-start(bf16[512,256]{1,0:T(8,128)(2,1)S(1)} %get-tuple-element.36), channel_id=1, source_target_pairs={{0,2},{1,3},{2,0},{3,1},{4,6},{5,7},{6,4},{7,5},{8,10},{9,11},{10,... | collective-permute-start | bytes 786440 | tf_op jit(solution)/shard_map/ppermute | solution.py:25
  181.7 8.6 %collective-permute-start.52 = (bf16[512,256]{1,0:T(8,128)(2,1)S(1)}, bf16[512,256]{1,0:T(8,128)(2,1)S(1)}, u32[]{:S(2)}, u32[]{:S(2)}) collective-permute-start(bf16[512,256]{1,0:T(8,128)(2,1)S(1)} %get-tuple-element.36), channel_id=1, source_target_pairs={{0,3},{1,0},{2,1},{3,2},{4,7},{5,4},{6,5},{7,6},{8,11},{9,8},{10,9... | collective-permute-start | bytes 786440 | tf_op jit(solution)/shard_map/ppermute | solution.py:25
  191.5 16.4 %collective-permute-start.36 = (bf16[4,4,8,4096]{3,2,1,0:T(8,128)(2,1)S(1)}, bf16[4,4,8,4096]{3,2,1,0:T(8,128)(2,1)S(1)}, u32[]{:S(2)}, u32[]{:S(2)}) collective-permute-start(bf16[4,4,8,4096]{3,2,1,0:T(8,128)(2,1)S(1)} %fusion.4), channel_id=1, source_target_pairs={{0,4},{4,0},{1,5},{5,1},{2,6},{6,2},{3,7},{7,3},{8,12},{12,8},{9,1... | collective-permute-start | bytes 3145736 | tf_op jit(solution)/shard_map/ppermute | solution.py:25
  192.7 4.2 %collective-permute-start.54 = (bf16[4,8,512]{2,1,0:T(8,128)(2,1)S(1)}, bf16[4,8,512]{2,1,0:T(8,128)(2,1)S(1)}, u32[]{:S(2)}, u32[]{:S(2)}) collective-permute-start(bf16[4,8,512]{2,1,0:T(8,128)(2,1)S(1)} %get-tuple-element.28), channel_id=1, source_target_pairs={{0,8},{8,16},{16,24},{24,0},{1,9},{9,17},{17,25},{25,1},{2,10},{10... | collective-permute-start | bytes 98312 | tf_op jit(solution)/shard_map/ppermute | solution.py:25
  193.4 5.4 %collective-permute-start.55 = (bf16[4,8,512]{2,1,0:T(8,128)(2,1)S(1)}, bf16[4,8,512]{2,1,0:T(8,128)(2,1)S(1)}, u32[]{:S(2)}, u32[]{:S(2)}) collective-permute-start(bf16[4,8,512]{2,1,0:T(8,128)(2,1)S(1)} %get-tuple-element.30), channel_id=1, source_target_pairs={{0,16},{8,24},{16,0},{24,8},{1,17},{9,25},{17,1},{25,9},{2,18},{10... | collective-permute-start | bytes 98312 | tf_op jit(solution)/shard_map/ppermute | solution.py:25
  194.3 5.1 %collective-permute-start.56 = (bf16[4,8,512]{2,1,0:T(8,128)(2,1)S(1)}, bf16[4,8,512]{2,1,0:T(8,128)(2,1)S(1)}, u32[]{:S(2)}, u32[]{:S(2)}) collective-permute-start(bf16[4,8,512]{2,1,0:T(8,128)(2,1)S(1)} %get-tuple-element.29), channel_id=1, source_target_pairs={{0,24},{8,0},{16,8},{24,16},{1,25},{9,1},{17,9},{25,17},{2,26},{10... | collective-permute-start | bytes 98312 | tf_op jit(solution)/shard_map/ppermute | solution.py:25
  199.5 4.9 %collective-permute-start.57 = (bf16[8,512]{1,0:T(8,128)(2,1)S(1)}, bf16[8,512]{1,0:T(8,128)(2,1)S(1)}, u32[]{:S(2)}, u32[]{:S(2)}) collective-permute-start(bf16[8,512]{1,0:T(8,128)(2,1)S(1)} %get-tuple-element.31), channel_id=1, source_target_pairs={{0,32},{32,64},{64,96},{96,0},{1,33},{33,65},{65,97},{97,1},{2,34}... | collective-permute-start | bytes 24584 | tf_op jit(solution)/shard_map/ppermute | solution.py:25
  200.8 5.2 %collective-permute-start.58 = (bf16[8,512]{1,0:T(8,128)(2,1)S(1)}, bf16[8,512]{1,0:T(8,128)(2,1)S(1)}, u32[]{:S(2)}, u32[]{:S(2)}) collective-permute-start(bf16[8,512]{1,0:T(8,128)(2,1)S(1)} %get-tuple-element.33), channel_id=1, source_target_pairs={{0,64},{32,96},{64,0},{96,32},{1,65},{33,97},{65,1},{97,33},{2,66}... | collective-permute-start | bytes 24584 | tf_op jit(solution)/shard_map/ppermute | solution.py:25
  204.1 7.1 %collective-permute-start.43 = (bf16[4,4,8,4096]{3,2,0,1:T(8,128)(2,1)S(1)}, bf16[4,4,8,4096]{3,2,0,1:T(8,128)(2,1)S(1)}, u32[]{:S(2)}, u32[]{:S(2)}) collective-permute-start(bf16[4,4,8,4096]{3,2,0,1:T(8,128)(2,1)S(1)} %fusion.5), channel_id=1, source_target_pairs={{0,4},{4,0},{1,5},{5,1},{2,6},{6,2},{3,7},{7,3},{8,12},{12,8},{9,1... | collective-permute-start | bytes 3145736 | tf_op jit(solution)/shard_map/ppermute | solution.py:25
  208.2 12.4 %collective-permute-start.37 = (bf16[4,8,4096]{2,1,0:T(8,128)(2,1)S(1)}, bf16[4,8,4096]{2,1,0:T(8,128)(2,1)S(1)}, u32[]{:S(2)}, u32[]{:S(2)}) collective-permute-start(bf16[4,8,4096]{2,1,0:T(8,128)(2,1)S(1)} %get-tuple-element.13), channel_id=1, source_target_pairs={{0,8},{8,16},{16,24},{24,0},{1,9},{9,17},{17,25},{25,1},{2,10},{10... | collective-permute-start | bytes 786440 | tf_op jit(solution)/shard_map/ppermute | solution.py:25
  210.2 11.9 %collective-permute-start.38 = (bf16[4,8,4096]{2,1,0:T(8,128)(2,1)S(1)}, bf16[4,8,4096]{2,1,0:T(8,128)(2,1)S(1)}, u32[]{:S(2)}, u32[]{:S(2)}) collective-permute-start(bf16[4,8,4096]{2,1,0:T(8,128)(2,1)S(1)} %get-tuple-element.15), channel_id=1, source_target_pairs={{0,16},{8,24},{16,0},{24,8},{1,17},{9,25},{17,1},{25,9},{2,18},{10... | collective-permute-start | bytes 786440 | tf_op jit(solution)/shard_map/ppermute | solution.py:25
  211.1 16.0 %collective-permute-start.39 = (bf16[4,8,4096]{2,1,0:T(8,128)(2,1)S(1)}, bf16[4,8,4096]{2,1,0:T(8,128)(2,1)S(1)}, u32[]{:S(2)}, u32[]{:S(2)}) collective-permute-start(bf16[4,8,4096]{2,1,0:T(8,128)(2,1)S(1)} %get-tuple-element.14), channel_id=1, source_target_pairs={{0,24},{8,0},{16,8},{24,16},{1,25},{9,1},{17,9},{25,17},{2,26},{10... | collective-permute-start | bytes 786440 | tf_op jit(solution)/shard_map/ppermute | solution.py:25
  211.6 18.6 %collective-permute-start.44 = (bf16[4,8,4096]{2,1,0:T(8,128)(2,1)S(1)}, bf16[4,8,4096]{2,1,0:T(8,128)(2,1)S(1)}, u32[]{:S(2)}, u32[]{:S(2)}) collective-permute-start(bf16[4,8,4096]{2,1,0:T(8,128)(2,1)S(1)} %get-tuple-element.16), channel_id=1, source_target_pairs={{0,8},{8,16},{16,24},{24,0},{1,9},{9,17},{17,25},{25,1},{2,10},{10... | collective-permute-start | bytes 786440 | tf_op jit(solution)/shard_map/ppermute | solution.py:25
  214.8 16.7 %collective-permute-start.45 = (bf16[4,8,4096]{2,1,0:T(8,128)(2,1)S(1)}, bf16[4,8,4096]{2,1,0:T(8,128)(2,1)S(1)}, u32[]{:S(2)}, u32[]{:S(2)}) collective-permute-start(bf16[4,8,4096]{2,1,0:T(8,128)(2,1)S(1)} %get-tuple-element.18), channel_id=1, source_target_pairs={{0,16},{8,24},{16,0},{24,8},{1,17},{9,25},{17,1},{25,9},{2,18},{10... | collective-permute-start | bytes 786440 | tf_op jit(solution)/shard_map/ppermute | solution.py:25
  220.6 13.2 %collective-permute-start.46 = (bf16[4,8,4096]{2,1,0:T(8,128)(2,1)S(1)}, bf16[4,8,4096]{2,1,0:T(8,128)(2,1)S(1)}, u32[]{:S(2)}, u32[]{:S(2)}) collective-permute-start(bf16[4,8,4096]{2,1,0:T(8,128)(2,1)S(1)} %get-tuple-element.17), channel_id=1, source_target_pairs={{0,24},{8,0},{16,8},{24,16},{1,25},{9,1},{17,9},{25,17},{2,26},{10... | collective-permute-start | bytes 786440 | tf_op jit(solution)/shard_map/ppermute | solution.py:25
  227.3 9.5 %collective-permute-start.40 = (bf16[8,4096]{1,0:T(8,128)(2,1)S(1)}, bf16[8,4096]{1,0:T(8,128)(2,1)S(1)}, u32[]{:S(2)}, u32[]{:S(2)}) collective-permute-start(bf16[8,4096]{1,0:T(8,128)(2,1)S(1)} %get-tuple-element.19), channel_id=1, source_target_pairs={{0,32},{32,64},{64,96},{96,0},{1,33},{33,65},{65,97},{97,1},{2,34}... | collective-permute-start | bytes 196616 | tf_op jit(solution)/shard_map/ppermute | solution.py:25
  227.4 11.2 %collective-permute-start.41 = (bf16[8,4096]{1,0:T(8,128)(2,1)S(1)}, bf16[8,4096]{1,0:T(8,128)(2,1)S(1)}, u32[]{:S(2)}, u32[]{:S(2)}) collective-permute-start(bf16[8,4096]{1,0:T(8,128)(2,1)S(1)} %get-tuple-element.21), channel_id=1, source_target_pairs={{0,64},{32,96},{64,0},{96,32},{1,65},{33,97},{65,1},{97,33},{2,66}... | collective-permute-start | bytes 196616 | tf_op jit(solution)/shard_map/ppermute | solution.py:25
  230.2 8.5 %collective-permute-start.42 = (bf16[8,4096]{1,0:T(8,128)(2,1)S(1)}, bf16[8,4096]{1,0:T(8,128)(2,1)S(1)}, u32[]{:S(2)}, u32[]{:S(2)}) collective-permute-start(bf16[8,4096]{1,0:T(8,128)(2,1)S(1)} %get-tuple-element.20), channel_id=1, source_target_pairs={{0,96},{32,0},{64,32},{96,64},{1,97},{33,1},{65,33},{97,65},{2,98}... | collective-permute-start | bytes 196616 | tf_op jit(solution)/shard_map/ppermute | solution.py:25
  234.0 5.5 %collective-permute-start.47 = (bf16[8,4096]{1,0:T(8,128)(2,1)S(1)}, bf16[8,4096]{1,0:T(8,128)(2,1)S(1)}, u32[]{:S(2)}, u32[]{:S(2)}) collective-permute-start(bf16[8,4096]{1,0:T(8,128)(2,1)S(1)} %get-tuple-element.22), channel_id=1, source_target_pairs={{0,32},{32,64},{64,96},{96,0},{1,33},{33,65},{65,97},{97,1},{2,34}... | collective-permute-start | bytes 196616 | tf_op jit(solution)/shard_map/ppermute | solution.py:25
  235.8 5.8 %collective-permute-start.48 = (bf16[8,4096]{1,0:T(8,128)(2,1)S(1)}, bf16[8,4096]{1,0:T(8,128)(2,1)S(1)}, u32[]{:S(2)}, u32[]{:S(2)}) collective-permute-start(bf16[8,4096]{1,0:T(8,128)(2,1)S(1)} %get-tuple-element.24), channel_id=1, source_target_pairs={{0,64},{32,96},{64,0},{96,32},{1,65},{33,97},{65,1},{97,33},{2,66}... | collective-permute-start | bytes 196616 | tf_op jit(solution)/shard_map/ppermute | solution.py:25
  236.8 4.8 %collective-permute-start.49 = (bf16[8,4096]{1,0:T(8,128)(2,1)S(1)}, bf16[8,4096]{1,0:T(8,128)(2,1)S(1)}, u32[]{:S(2)}, u32[]{:S(2)}) collective-permute-start(bf16[8,4096]{1,0:T(8,128)(2,1)S(1)} %get-tuple-element.23), channel_id=1, source_target_pairs={{0,96},{32,0},{64,32},{96,64},{1,97},{33,1},{65,33},{97,65},{2,98}... | collective-permute-start | bytes 196616 | tf_op jit(solution)/shard_map/ppermute | solution.py:25
  (17 other events, 92.3 us)
where the time goes:
time: 244 us; the launch traced here: 242 us
  starting transfers between devices  75.7 us (31%)
  waiting for transfers between devices  67.9 us (28%)
  Pallas kernels  57.5 us (24%)
  other arithmetic  29.3 us (12%)
  matrix products  6.97 us (3%)
  local copies, waits for them, and re-layouts  4.05 us (2%)
    ppermute x60, starting transfers between devices, _shift(): return lax.ppermute(v, ax, [(i, (i + k) % n) for i in range(n)])  75.7 us
    ppermute x60, waiting for transfers between devices, _shift(): return lax.ppermute(v, ax, [(i, (i + k) % n) for i in range(n)])  67.9 us
    pallas_call x3, Pallas kernels, _rowpass(): pl.pallas_call(_row_kernel, grid=(T // bt,), in_specs=[pl.BlockSpec((bt,...  28.2 us
    pallas_call x2, Pallas kernels, _colpass(): pl.pallas_call(_col_kernel, grid=(Pn // bp,), in_specs=[pl.BlockSpec((T,...  18.5 us
    convert_element_type x1, other arithmetic, on_device(): dscore = ((probs - plan) * factor).astype(BF16)  11.1 us
    pallas_call x1, Pallas kernels, _scores(): pl.pallas_call(_score_kernel, grid=(Pn // bp,), in_specs=[pl.BlockSpec((T...  10.7 us
  transfers between devices with their start and end apart: 60, of which 44 were waited for; matrix products, arithmetic and copies ran while one was open for 5% of the time, Pallas kernels for 0%

commit v1 on v0

--- a/solution.py
+++ b/solution.py
@@ -167,20 +167,14 @@
     tokens_all = 32 * T
     factor = PROTOS / (soft_temp * math.sqrt(tokens_all))
     dscore = ((probs - plan) * factor).astype(BF16)
-    half = dscore.shape[1] // 2
-    pg = []
-    for h in range(2):
-        pg_part = lax.dot_general(
-            unit_b, dscore[:, h * half:(h + 1) * half], (((0,), (0,)), ((), ())), preferred_element_type=F32
-        )
-        pg.append(_rs_dp(pg_part, BF16))
-    proto_grad = jnp.concatenate(pg, axis=1)
+    pg_part = lax.dot_general(unit_b, dscore, (((0,), (0,)), ((), ())), preferred_element_type=F32)
     dunit_part = lax.dot_general(dscore, normed, (((1,), (1,)), ((), ())), preferred_element_type=F32)
     dunit = _allsum(dunit_part, "z", BF16)
     dproj = ((dunit - unit * jnp.sum(unit * dunit, axis=1, keepdims=True)) / length).astype(BF16)
     head_part = lax.dot_general(dproj, features, (((0,), (0,)), ((), ())), preferred_element_type=F32)
-    head_grad = _rs_dp(head_part, BF16)
-    return (codes, proto_grad, head_grad)
+    Pn = pg_part.shape[1]
+    both = _rs_dp(jnp.concatenate([pg_part, head_part], axis=1), BF16)
+    return (codes, both[:, :Pn], both[:, Pn:])
 
 
 def solution(mesh):

time: 244 us -> 256 us (1.049)
  starting transfers between devices: 75.7 us -> 56.9 us
  waiting for transfers between devices: 67.9 us -> 79.1 us
  other arithmetic: 29.3 us -> 39.1 us
  local copies, waits for them, and re-layouts: 4.05 us -> 10.8 us
  matrix products: 6.97 us -> 10.2 us
    ppermute x60 -> x46, starting transfers between devices: 75.7 us -> 56.9 us  [_shift(): return lax.ppermute(v, ax, [(i, (i + k) % n) for i in range(n)])]
    ppermute x60 -> x46, waiting for transfers between devices: 67.9 us -> 79.1 us  [_shift(): return lax.ppermute(v, ax, [(i, (i + k) % n) for i in range(n)])]
    concatenate x1, other arithmetic: 0.72 us -> 7.64 us  [on_device(): both = _rs_dp(jnp.concatenate([pg_part, head_part], axis=1), BF16)]
    convert_element_type x9 -> x3, local copies, waits for them, and re-layouts: 0.56 us -> 4.06 us  [_rs(): blk = blk.astype(dt)]
    dot_general x2 -> x1, matrix products: 2.59 us -> 5.8 us  [on_device(): lax.dot_general(unit_b, dscore, (((0,), (0,)), ((), ())), preferred_eleme...]
    add x10 -> x4, other arithmetic: 1.5 us -> 4.4 us  [_rs(): acc = acc + _shift(blk, ax, k).astype(a.dtype)]
  transfers between devices with their start and end apart: 60 -> 46, of which waited for: 44 -> 39; matrix products, arithmetic and copies ran while one was open for 5% -> 5% of each run, Pallas kernels for 0% -> 0%
where the time goes in v1:
time: 256 us; the launch traced here: 255 us
  waiting for transfers between devices  79.1 us (31%)
  Pallas kernels  57.7 us (23%)
  starting transfers between devices  56.9 us (22%)
  other arithmetic  39.1 us (15%)
  local copies, waits for them, and re-layouts  10.8 us (4%)
  matrix products  10.2 us (4%)
    ppermute x46, waiting for transfers between devices, _shift(): return lax.ppermute(v, ax, [(i, (i + k) % n) for i in range(n)])  79.1 us
    ppermute x46, starting transfers between devices, _shift(): return lax.ppermute(v, ax, [(i, (i + k) % n) for i in range(n)])  56.9 us
    pallas_call x3, Pallas kernels, _rowpass(): pl.pallas_call(_row_kernel, grid=(T // bt,), in_specs=[pl.BlockSpec((bt,...  28.6 us
    pallas_call x2, Pallas kernels, _colpass(): pl.pallas_call(_col_kernel, grid=(Pn // bp,), in_specs=[pl.BlockSpec((T,...  18.5 us
    convert_element_type x1, other arithmetic, on_device(): dscore = ((probs - plan) * factor).astype(BF16)  11.1 us
    pallas_call x1, Pallas kernels, _scores(): pl.pallas_call(_score_kernel, grid=(Pn // bp,), in_specs=[pl.BlockSpec((T...  10.7 us
    concatenate x1, other arithmetic, on_device(): both = _rs_dp(jnp.concatenate([pg_part, head_part], axis=1), BF16)  7.64 us
    dot_general x1, matrix products, on_device(): lax.dot_general(unit_b, dscore, (((0,), (0,)), ((), ())), preferred_eleme...  5.8 us
  transfers between devices with their start and end apart: 46, of which 39 were waited for; matrix products, arithmetic and copies ran while one was open for 5% of the time, Pallas kernels for 0%

profile of v1, /device:TPU:6, one launch (start us, length us, event | category | flops | bytes accessed | tf_op | source)
XLA Modules:
  0.0 254.7 jit_solution(13337601002908009744)
XLA Ops:
  3.1 2.0 collective-permute-start
  5.1 3.6 %collective-permute-start.1 = (f32[128,256]{1,0:T(8,128)S(1)}, f32[128,256]{1,0:T(8,128)S(1)}, u32[]{:S(2)}, u32[]{:S(2)}) collective-permute-start(f32[128,256]{1,0:T(8,128)S(1)} %get-tuple-element.21), channel_id=1, source_target_pairs={{0,2},{1,3},{2,0},{3,1},{4,6},{5,7},{6,4},{7,5},{8,10},{9,11},{10,... | collective-permute-start | bytes 393224 | tf_op jit(solution)/shard_map/ppermute | solution.py:25
  9.7 3.1 %fusion = f32[8192]{0:T(1024)S(1)} fusion(bf16[256,8192]{1,0:T(8,128)(2,1)} %param.5), kind=kLoop, calls=%fused_computation.7 | loop fusion | flops 6283264 | bytes 4227072 | tf_op jit(solution)/shard_map/reduce_sum | solution.py:149
  12.8 2.9 %fusion.1.n_ref = bf16[256,8192]{1,0:T(8,128)(2,1)} fusion(bf16[256,8192]{1,0:T(8,128)(2,1)S(1)} %copy-done.1, f32[8192]{0:T(1024)S(1)} %add_sqrt_fusion), kind=kLoop, calls=%fused_computation.8 | loop fusion | flops 6291456 | bytes 8421376 | tf_op jit(solution)/shard_map/convert_element_type | solution.py:149
  16.9 1.6 collective-permute-start.4
  19.7 4.7 %collective-permute-done.3 = f32[128,256]{1,0:T(8,128)S(1)} collective-permute-done((f32[128,256]{1,0:T(8,128)S(1)}, f32[128,256]{1,0:T(8,128)S(1)}, u32[]{:S(2)}, u32[]{:S(2)}) %collective-permute-start.3) | collective-permute-done | bytes 131104 | tf_op jit(solution)/shard_map/ppermute | solution.py:25
  26.5 10.7 %shard_map.58 = (f32[512,8192]{1,0:T(8,128)}, f32[1,8192]{1,0:T(1,128)}, f32[512,1]{1,0:T(8,128)}) custom-call(bf16[512,256]{1,0:T(8,128)(2,1)} %get-tuple-element.9.u_ref, bf16[256,8192]{1,0:T(8,128)(2,1)} %fusion.1.n_ref), custom_call_target="tpu_custom_call" | custom-call | tf_op jit(solution)/shard_map/pallas_call | solution.py:89
  39.9 2.4 collective-permute-start.8
  43.4 1.9 collective-permute-done.8
  45.3 2.1 collective-permute-done.9
  47.4 1.6 collective-permute-start.10
  49.1 2.9 %collective-permute-start.11 = (f32[8192]{0:T(1024)S(1)}, f32[8192]{0:T(1024)S(1)}, u32[]{:S(2)}, u32[]{:S(2)}) collective-permute-start(f32[8192]{0:T(1024)S(1)} %add_add_fusion.2), channel_id=1, source_target_pairs={{0,64},{32,96},{64,0},{96,32},{1,65},{33,97},{65,1},{97,33},{2,66}... | collective-permute-start | bytes 98312 | tf_op jit(solution)/shard_map/ppermute | solution.py:25
  56.5 9.4 %shard_map.59 = f32[512,1]{1,0:T(8,128)} custom-call(f32[512,8192]{1,0:T(8,128)} %get-tuple-element.6.s_ref, f32[1,8192]{1,0:T(1,128)} %bitcast.82), custom_call_target="tpu_custom_call" | custom-call | tf_op jit(solution)/shard_map/pallas_call | solution.py:130
  67.9 3.3 %collective-permute-start.14 = (f32[2,512]{1,0:T(2,128)S(1)}, f32[2,512]{1,0:T(2,128)S(1)}, u32[]{:S(2)}, u32[]{:S(2)}) collective-permute-start(f32[2,512]{1,0:T(2,128)S(1)} %pad_maximum_fusion.2), channel_id=1, source_target_pairs={{0,2},{1,3},{2,0},{3,1},{4,6},{5,7},{6,4},{7,5},{8,10},{9,11},{10,... | collective-permute-start | bytes 12296 | tf_op jit(solution)/shard_map/ppermute | solution.py:25
  73.0 1.8 collective-permute-done.15
  75.7 9.3 %shard_map.60 = f32[1,8192]{1,0:T(1,128)} custom-call(f32[512,8192]{1,0:T(8,128)} %get-tuple-element.6.s_ref, f32[512,1]{1,0:T(8,128)} %copy.10.r_ref), custom_call_target="tpu_custom_call" | custom-call | tf_op jit(solution)/shard_map/pallas_call | solution.py:114
  89.2 1.9 collective-permute-done.17
  91.1 2.1 collective-permute-done.18
  94.1 3.8 %collective-permute-start.21 = (f32[8192]{0:T(1024)S(1)}, f32[8192]{0:T(1024)S(1)}, u32[]{:S(2)}, u32[]{:S(2)}) collective-permute-start(f32[8192]{0:T(1024)S(1)} %add_add_fusion.1), channel_id=1, source_target_pairs={{0,64},{32,96},{64,0},{96,32},{1,65},{33,97},{65,1},{97,33},{2,66}... | collective-permute-start | bytes 98312 | tf_op jit(solution)/shard_map/ppermute | solution.py:25
  100.1 1.7 collective-permute-done.22
  102.4 9.4 %shard_map.61 = f32[512,1]{1,0:T(8,128)} custom-call(f32[512,8192]{1,0:T(8,128)} %get-tuple-element.6.s_ref, f32[1,8192]{1,0:T(1,128)} %bitcast.83), custom_call_target="tpu_custom_call" | custom-call | tf_op jit(solution)/shard_map/pallas_call | solution.py:130
  113.0 2.7 %collective-permute-start.24 = (f32[512]{0:T(512)S(1)}, f32[512]{0:T(512)S(1)}, u32[]{:S(2)}, u32[]{:S(2)}) collective-permute-start(f32[512]{0:T(512)S(1)} %reduce.3), channel_id=1, source_target_pairs={{0,2},{1,3},{2,0},{3,1},{4,6},{5,7},{6,4},{7,5},{8,10},{9,11},{10,... | collective-permute-start | bytes 6152 | tf_op jit(solution)/shard_map/ppermute | solution.py:25
  115.7 1.5 collective-permute-start.25
  120.1 9.3 %shard_map.62 = f32[1,8192]{1,0:T(1,128)} custom-call(f32[512,8192]{1,0:T(8,128)} %get-tuple-element.6.s_ref, f32[512,1]{1,0:T(8,128)} %copy.11.r_ref), custom_call_target="tpu_custom_call" | custom-call | tf_op jit(solution)/shard_map/pallas_call | solution.py:114
  131.6 2.0 collective-permute-start.27
  135.7 3.2 %collective-permute-done.28 = f32[8192]{0:T(1024)S(1)} collective-permute-done((f32[8192]{0:T(1024)S(1)}, f32[8192]{0:T(1024)S(1)}, u32[]{:S(2)}, u32[]{:S(2)}) %collective-permute-start.28) | collective-permute-done | bytes 32800 | tf_op jit(solution)/shard_map/ppermute | solution.py:25
  139.7 2.7 %collective-permute-start.31 = (f32[8192]{0:T(1024)S(1)}, f32[8192]{0:T(1024)S(1)}, u32[]{:S(2)}, u32[]{:S(2)}) collective-permute-start(f32[8192]{0:T(1024)S(1)} %add_add_fusion), channel_id=1, source_target_pairs={{0,64},{32,96},{64,0},{96,32},{1,65},{33,97},{65,1},{97,33},{2,66}... | collective-permute-start | bytes 98312 | tf_op jit(solution)/shard_map/ppermute | solution.py:25
  147.0 9.8 %shard_map.63 = f32[512,1]{1,0:T(8,128)} custom-call(f32[512,8192]{1,0:T(8,128)} %get-tuple-element.6.s_ref, f32[1,8192]{1,0:T(1,128)} %bitcast.77), custom_call_target="tpu_custom_call" | custom-call | tf_op jit(solution)/shard_map/pallas_call | solution.py:130
  157.9 1.5 collective-permute-start.33
  159.3 2.7 %collective-permute-start.34 = (f32[512]{0:T(512)S(1)}, f32[512]{0:T(512)S(1)}, u32[]{:S(2)}, u32[]{:S(2)}) collective-permute-start(f32[512]{0:T(512)S(1)} %reduce.4), channel_id=1, source_target_pairs={{0,2},{1,3},{2,0},{3,1},{4,6},{5,7},{6,4},{7,5},{8,10},{9,11},{10,... | collective-permute-start | bytes 6152 | tf_op jit(solution)/shard_map/ppermute | solution.py:25
  162.7 1.7 collective-permute-done.34
  165.7 11.1 %multiply_convert_fusion = (bf16[512,8192]{1,0:T(8,128)(2,1)S(1)}, bf16[512,8192]{1,0:T(8,128)(2,1)}) fusion(f32[512,8192]{1,0:T(8,128)} %get-tuple-element.6.s_ref, f32[512]{0:T(512)S(1)} %bitcast.94, f32[512]{0:T(512)S(1)} %add_divide_fusion.3, f32[8192]{0:T(1024)S(1)} %copy-done.5), kind=kLoop, calls=%fused_computation.1 | loop fusion | flops 37748736 | bytes 33591296 | tf_op jit(solution)/shard_map/convert_element_type | solution.py:169
  176.8 2.4 fusion.23
  179.3 2.7 %collective-permute-start.37 = (bf16[512,256]{1,0:T(8,128)(2,1)S(1)}, bf16[512,256]{1,0:T(8,128)(2,1)S(1)}, u32[]{:S(2)}, u32[]{:S(2)}) collective-permute-start(bf16[512,256]{1,0:T(8,128)(2,1)S(1)} %get-tuple-element.24), channel_id=1, source_target_pairs={{0,2},{1,3},{2,0},{3,1},{4,6},{5,7},{6,4},{7,5},{8,10},{9,11},{10,... | collective-permute-start | bytes 786440 | tf_op jit(solution)/shard_map/ppermute | solution.py:25
  182.0 1.4 collective-permute-start.38
  183.4 5.8 %fusion.25 = f32[256,8192]{1,0:T(8,128)} fusion(bf16[512,256]{1,0:T(8,128)(2,1)S(1)} %copy-done.4, bf16[512,8192]{1,0:T(8,128)(2,1)S(1)} %get-tuple-element.11), kind=kOutput, calls=%fused_computation.72 | convolution fusion | flops 2147483648 | bytes 17039360 | tf_op jit(solution)/shard_map/dot_general | solution.py:170
  191.4 7.6 %pad_maximum_fusion = f32[256,8704]{1,0:T(8,128)} fusion(f32[256,512]{1,0:T(8,128)S(1)} %fusion.10, f32[256,8192]{1,0:T(8,128)} %fusion.25), kind=kLoop, calls=%fused_computation.6 | loop fusion | flops 2228224 | bytes 17825792 | tf_op jit(solution)/shard_map/concatenate | solution.py:176
  199.0 3.8 %fusion.2 = bf16[4,4,8,8704]{3,2,0,1:T(8,128)(2,1)} fusion(f32[4,4,2,8,8704]{4,3,2,1,0:T(8,128)} %bitcast.72, s32[]{:T(128)S(6)} %select_n.123), kind=kLoop, calls=%fused_computation.11 | loop fusion | bytes 4456452 | tf_op jit(solution)/shard_map/convert_element_type | solution.py:49
  202.9 4.6 %collective-permute-done.39 = bf16[4,4,8,8704]{3,2,0,1:T(8,128)(2,1)S(1)} collective-permute-done((bf16[4,4,8,8704]{3,2,0,1:T(8,128)(2,1)}, bf16[4,4,8,8704]{3,2,0,1:T(8,128)(2,1)S(1)}, u32[]{:S(2)}, u32[]{:S(2)}) %collective-permute-start.39) | collective-permute-done | bytes 2228256 | tf_op jit(solution)/shard_map/ppermute | solution.py:25
  207.4 2.7 %bitcast_add_fusion = f32[4,4,8,8704]{3,2,0,1:T(8,128)S(1)} fusion(bf16[4,4,8,8704]{3,2,0,1:T(8,128)(2,1)S(1)} %collective-permute-done.39, f32[4,4,2,8,8704]{4,3,2,1,0:T(8,128)} %bitcast.73, s32[]{:T(128)S(6)} %select_n.121), kind=kLoop, calls=%fused_computation.10 | loop fusion | flops 2228224 | bytes 11141124 | tf_op jit(solution)/shard_map/add | solution.py:50
  210.1 2.1 copy-done.3
  215.2 12.7 %collective-permute-done.40 = bf16[4,8,8704]{2,1,0:T(8,128)(2,1)S(1)} collective-permute-done((bf16[4,8,8704]{2,1,0:T(8,128)(2,1)S(1)}, bf16[4,8,8704]{2,1,0:T(8,128)(2,1)S(1)}, u32[]{:S(2)}, u32[]{:S(2)}) %collective-permute-start.40) | collective-permute-done | bytes 557088 | tf_op jit(solution)/shard_map/ppermute | solution.py:25
  227.9 2.1 collective-permute-done.41
  230.0 10.9 %collective-permute-done.42 = bf16[4,8,8704]{2,1,0:T(8,128)(2,1)} collective-permute-done((bf16[4,8,8704]{2,1,0:T(8,128)(2,1)S(1)}, bf16[4,8,8704]{2,1,0:T(8,128)(2,1)}, u32[]{:S(2)}, u32[]{:S(2)}) %collective-permute-start.42) | collective-permute-done | bytes 557088 | tf_op jit(solution)/shard_map/ppermute | solution.py:25
  240.9 1.6 fusion.4
  244.0 2.7 %collective-permute-start.44 = (bf16[8,8704]{1,0:T(8,128)(2,1)S(1)}, bf16[8,8704]{1,0:T(8,128)(2,1)S(1)}, u32[]{:S(2)}, u32[]{:S(2)}) collective-permute-start(bf16[8,8704]{1,0:T(8,128)(2,1)S(1)} %get-tuple-element.18), channel_id=1, source_target_pairs={{0,64},{32,96},{64,0},{96,32},{1,65},{33,97},{65,1},{97,33},{2,66}... | collective-permute-start | bytes 417800 | tf_op jit(solution)/shard_map/ppermute | solution.py:25
  247.0 2.7 %collective-permute-done.43 = bf16[8,8704]{1,0:T(8,128)(2,1)S(1)} collective-permute-done((bf16[8,8704]{1,0:T(8,128)(2,1)S(1)}, bf16[8,8704]{1,0:T(8,128)(2,1)S(1)}, u32[]{:S(2)}, u32[]{:S(2)}) %collective-permute-start.43) | collective-permute-done | bytes 139296 | tf_op jit(solution)/shard_map/ppermute | solution.py:25
  249.7 3.6 %collective-permute-done.44 = bf16[8,8704]{1,0:T(8,128)(2,1)S(1)} collective-permute-done((bf16[8,8704]{1,0:T(8,128)(2,1)S(1)}, bf16[8,8704]{1,0:T(8,128)(2,1)S(1)}, u32[]{:S(2)}, u32[]{:S(2)}) %collective-permute-start.44) | collective-permute-done | bytes 139296 | tf_op jit(solution)/shard_map/ppermute | solution.py:25
  (109 shorter events, 54.1 us)
Async XLA Ops:
  3.1 12.6 %collective-permute-start = (f32[128,256]{1,0:T(8,128)S(1)}, f32[128,256]{1,0:T(8,128)S(1)}, u32[]{:S(2)}, u32[]{:S(2)}) collective-permute-start(f32[128,256]{1,0:T(8,128)S(1)} %get-tuple-element.19), channel_id=1, source_target_pairs={{0,1},{1,2},{2,3},{3,0},{4,5},{5,6},{6,7},{7,4},{8,9},{9,10},{10,1... | collective-permute-start | bytes 393224 | tf_op jit(solution)/shard_map/ppermute | solution.py:25
  5.1 10.6 %collective-permute-start.1 = (f32[128,256]{1,0:T(8,128)S(1)}, f32[128,256]{1,0:T(8,128)S(1)}, u32[]{:S(2)}, u32[]{:S(2)}) collective-permute-start(f32[128,256]{1,0:T(8,128)S(1)} %get-tuple-element.21), channel_id=1, source_target_pairs={{0,2},{1,3},{2,0},{3,1},{4,6},{5,7},{6,4},{7,5},{8,10},{9,11},{10,... | collective-permute-start | bytes 393224 | tf_op jit(solution)/shard_map/ppermute | solution.py:25
  8.7 7.1 %collective-permute-start.2 = (f32[128,256]{1,0:T(8,128)S(1)}, f32[128,256]{1,0:T(8,128)S(1)}, u32[]{:S(2)}, u32[]{:S(2)}) collective-permute-start(f32[128,256]{1,0:T(8,128)S(1)} %get-tuple-element.20), channel_id=1, source_target_pairs={{0,3},{1,0},{2,1},{3,2},{4,7},{5,4},{6,5},{7,6},{8,11},{9,8},{10,9... | collective-permute-start | bytes 393224 | tf_op jit(solution)/shard_map/ppermute | solution.py:25
  15.8 8.6 %collective-permute-start.3 = (f32[128,256]{1,0:T(8,128)S(1)}, f32[128,256]{1,0:T(8,128)S(1)}, u32[]{:S(2)}, u32[]{:S(2)}) collective-permute-start(f32[128,256]{1,0:T(8,128)S(1)} %fusion.17), channel_id=1, source_target_pairs={{0,1},{1,2},{2,3},{3,0},{4,5},{5,6},{6,7},{7,4},{8,9},{9,10},{10,1... | collective-permute-start | bytes 393224 | tf_op jit(solution)/shard_map/ppermute | solution.py:25
  16.9 7.6 %collective-permute-start.4 = (f32[128,256]{1,0:T(8,128)S(1)}, f32[128,256]{1,0:T(8,128)S(1)}, u32[]{:S(2)}, u32[]{:S(2)}) collective-permute-start(f32[128,256]{1,0:T(8,128)S(1)} %fusion.17), channel_id=1, source_target_pairs={{0,2},{1,3},{2,0},{3,1},{4,6},{5,7},{6,4},{7,5},{8,10},{9,11},{10,... | collective-permute-start | bytes 393224 | tf_op jit(solution)/shard_map/ppermute | solution.py:25
  18.4 6.4 %collective-permute-start.5 = (f32[128,256]{1,0:T(8,128)S(1)}, f32[128,256]{1,0:T(8,128)S(1)}, u32[]{:S(2)}, u32[]{:S(2)}) collective-permute-start(f32[128,256]{1,0:T(8,128)S(1)} %fusion.17), channel_id=1, source_target_pairs={{0,3},{1,0},{2,1},{3,2},{4,7},{5,4},{6,5},{7,6},{8,11},{9,8},{10,9... | collective-permute-start | bytes 393224 | tf_op jit(solution)/shard_map/ppermute | solution.py:25
  37.2 1.5 collective-permute-start.6
  39.4 4.0 %collective-permute-start.7 = (f32[8192]{0:T(1024)S(1)}, f32[8192]{0:T(1024)S(1)}, u32[]{:S(2)}, u32[]{:S(2)}) collective-permute-start(f32[8192]{0:T(1024)S(1)} %add.301), channel_id=1, source_target_pairs={{0,8},{8,16},{16,24},{24,0},{1,9},{9,17},{17,25},{25,1},{2,10},{10... | collective-permute-start | bytes 98312 | tf_op jit(solution)/shard_map/ppermute | solution.py:25
  39.9 5.4 %collective-permute-start.8 = (f32[8192]{0:T(1024)S(1)}, f32[8192]{0:T(1024)S(1)}, u32[]{:S(2)}, u32[]{:S(2)}) collective-permute-start(f32[8192]{0:T(1024)S(1)} %add.301), channel_id=1, source_target_pairs={{0,16},{8,24},{16,0},{24,8},{1,17},{9,25},{17,1},{25,9},{2,18},{10... | collective-permute-start | bytes 98312 | tf_op jit(solution)/shard_map/ppermute | solution.py:25
  42.3 5.1 %collective-permute-start.9 = (f32[8192]{0:T(1024)S(1)}, f32[8192]{0:T(1024)S(1)}, u32[]{:S(2)}, u32[]{:S(2)}) collective-permute-start(f32[8192]{0:T(1024)S(1)} %add.301), channel_id=1, source_target_pairs={{0,24},{8,0},{16,8},{24,16},{1,25},{9,1},{17,9},{25,17},{2,26},{10... | collective-permute-start | bytes 98312 | tf_op jit(solution)/shard_map/ppermute | solution.py:25
  47.4 7.0 %collective-permute-start.10 = (f32[8192]{0:T(1024)S(1)}, f32[8192]{0:T(1024)S(1)}, u32[]{:S(2)}, u32[]{:S(2)}) collective-permute-start(f32[8192]{0:T(1024)S(1)} %add_add_fusion.2), channel_id=1, source_target_pairs={{0,32},{32,64},{64,96},{96,0},{1,33},{33,65},{65,97},{97,1},{2,34}... | collective-permute-start | bytes 98312 | tf_op jit(solution)/shard_map/ppermute | solution.py:25
  49.1 5.4 %collective-permute-start.11 = (f32[8192]{0:T(1024)S(1)}, f32[8192]{0:T(1024)S(1)}, u32[]{:S(2)}, u32[]{:S(2)}) collective-permute-start(f32[8192]{0:T(1024)S(1)} %add_add_fusion.2), channel_id=1, source_target_pairs={{0,64},{32,96},{64,0},{96,32},{1,65},{33,97},{65,1},{97,33},{2,66}... | collective-permute-start | bytes 98312 | tf_op jit(solution)/shard_map/ppermute | solution.py:25
  52.0 3.9 %collective-permute-start.12 = (f32[8192]{0:T(1024)S(1)}, f32[8192]{0:T(1024)S(1)}, u32[]{:S(2)}, u32[]{:S(2)}) collective-permute-start(f32[8192]{0:T(1024)S(1)} %add_add_fusion.2), channel_id=1, source_target_pairs={{0,96},{32,0},{64,32},{96,64},{1,97},{33,1},{65,33},{97,65},{2,98}... | collective-permute-start | bytes 98312 | tf_op jit(solution)/shard_map/ppermute | solution.py:25
  67.0 4.9 %collective-permute-start.13 = (f32[2,512]{1,0:T(2,128)S(1)}, f32[2,512]{1,0:T(2,128)S(1)}, u32[]{:S(2)}, u32[]{:S(2)}) collective-permute-start(f32[2,512]{1,0:T(2,128)S(1)} %pad_maximum_fusion.2), channel_id=1, source_target_pairs={{0,1},{1,2},{2,3},{3,0},{4,5},{5,6},{6,7},{7,4},{8,9},{9,10},{10,1... | collective-permute-start | bytes 12296 | tf_op jit(solution)/shard_map/ppermute | solution.py:25
  67.9 5.1 %collective-permute-start.14 = (f32[2,512]{1,0:T(2,128)S(1)}, f32[2,512]{1,0:T(2,128)S(1)}, u32[]{:S(2)}, u32[]{:S(2)}) collective-permute-start(f32[2,512]{1,0:T(2,128)S(1)} %pad_maximum_fusion.2), channel_id=1, source_target_pairs={{0,2},{1,3},{2,0},{3,1},{4,6},{5,7},{6,4},{7,5},{8,10},{9,11},{10,... | collective-permute-start | bytes 12296 | tf_op jit(solution)/shard_map/ppermute | solution.py:25
  71.2 3.6 %collective-permute-start.15 = (f32[2,512]{1,0:T(2,128)S(1)}, f32[2,512]{1,0:T(2,128)S(1)}, u32[]{:S(2)}, u32[]{:S(2)}) collective-permute-start(f32[2,512]{1,0:T(2,128)S(1)} %pad_maximum_fusion.2), channel_id=1, source_target_pairs={{0,3},{1,0},{2,1},{3,2},{4,7},{5,4},{6,5},{7,6},{8,11},{9,8},{10,9... | collective-permute-start | bytes 12296 | tf_op jit(solution)/shard_map/ppermute | solution.py:25
  85.0 1.4 collective-permute-start.16
  87.2 3.9 %collective-permute-start.17 = (f32[8192]{0:T(1024)S(1)}, f32[8192]{0:T(1024)S(1)}, u32[]{:S(2)}, u32[]{:S(2)}) collective-permute-start(f32[8192]{0:T(1024)S(1)} %add.311), channel_id=1, source_target_pairs={{0,8},{8,16},{16,24},{24,0},{1,9},{9,17},{17,25},{25,1},{2,10},{10... | collective-permute-start | bytes 98312 | tf_op jit(solution)/shard_map/ppermute | solution.py:25
  87.8 5.4 %collective-permute-start.18 = (f32[8192]{0:T(1024)S(1)}, f32[8192]{0:T(1024)S(1)}, u32[]{:S(2)}, u32[]{:S(2)}) collective-permute-start(f32[8192]{0:T(1024)S(1)} %add.311), channel_id=1, source_target_pairs={{0,16},{8,24},{16,0},{24,8},{1,17},{9,25},{17,1},{25,9},{2,18},{10... | collective-permute-start | bytes 98312 | tf_op jit(solution)/shard_map/ppermute | solution.py:25
  88.7 5.1 %collective-permute-start.19 = (f32[8192]{0:T(1024)S(1)}, f32[8192]{0:T(1024)S(1)}, u32[]{:S(2)}, u32[]{:S(2)}) collective-permute-start(f32[8192]{0:T(1024)S(1)} %add.311), channel_id=1, source_target_pairs={{0,24},{8,0},{16,8},{24,16},{1,25},{9,1},{17,9},{25,17},{2,26},{10... | collective-permute-start | bytes 98312 | tf_op jit(solution)/shard_map/ppermute | solution.py:25
  93.8 5.2 %collective-permute-start.20 = (f32[8192]{0:T(1024)S(1)}, f32[8192]{0:T(1024)S(1)}, u32[]{:S(2)}, u32[]{:S(2)}) collective-permute-start(f32[8192]{0:T(1024)S(1)} %add_add_fusion.1), channel_id=1, source_target_pairs={{0,32},{32,64},{64,96},{96,0},{1,33},{33,65},{65,97},{97,1},{2,34}... | collective-permute-start | bytes 98312 | tf_op jit(solution)/shard_map/ppermute | solution.py:25
  94.1 6.1 %collective-permute-start.21 = (f32[8192]{0:T(1024)S(1)}, f32[8192]{0:T(1024)S(1)}, u32[]{:S(2)}, u32[]{:S(2)}) collective-permute-start(f32[8192]{0:T(1024)S(1)} %add_add_fusion.1), channel_id=1, source_target_pairs={{0,64},{32,96},{64,0},{96,32},{1,65},{33,97},{65,1},{97,33},{2,66}... | collective-permute-start | bytes 98312 | tf_op jit(solution)/shard_map/ppermute | solution.py:25
  97.9 3.9 %collective-permute-start.22 = (f32[8192]{0:T(1024)S(1)}, f32[8192]{0:T(1024)S(1)}, u32[]{:S(2)}, u32[]{:S(2)}) collective-permute-start(f32[8192]{0:T(1024)S(1)} %add_add_fusion.1), channel_id=1, source_target_pairs={{0,96},{32,0},{64,32},{96,64},{1,97},{33,1},{65,33},{97,65},{2,98}... | collective-permute-start | bytes 98312 | tf_op jit(solution)/shard_map/ppermute | solution.py:25
  112.9 4.9 %collective-permute-start.23 = (f32[512]{0:T(512)S(1)}, f32[512]{0:T(512)S(1)}, u32[]{:S(2)}, u32[]{:S(2)}) collective-permute-start(f32[512]{0:T(512)S(1)} %reduce.3), channel_id=1, source_target_pairs={{0,1},{1,2},{2,3},{3,0},{4,5},{5,6},{6,7},{7,4},{8,9},{9,10},{10,1... | collective-permute-start | bytes 6152 | tf_op jit(solution)/shard_map/ppermute | solution.py:25
  113.0 5.2 %collective-permute-start.24 = (f32[512]{0:T(512)S(1)}, f32[512]{0:T(512)S(1)}, u32[]{:S(2)}, u32[]{:S(2)}) collective-permute-start(f32[512]{0:T(512)S(1)} %reduce.3), channel_id=1, source_target_pairs={{0,2},{1,3},{2,0},{3,1},{4,6},{5,7},{6,4},{7,5},{8,10},{9,11},{10,... | collective-permute-start | bytes 6152 | tf_op jit(solution)/shard_map/ppermute | solution.py:25
  115.7 3.6 %collective-permute-start.25 = (f32[512]{0:T(512)S(1)}, f32[512]{0:T(512)S(1)}, u32[]{:S(2)}, u32[]{:S(2)}) collective-permute-start(f32[512]{0:T(512)S(1)} %reduce.3), channel_id=1, source_target_pairs={{0,3},{1,0},{2,1},{3,2},{4,7},{5,4},{6,5},{7,6},{8,11},{9,8},{10,9... | collective-permute-start | bytes 6152 | tf_op jit(solution)/shard_map/ppermute | solution.py:25
  129.4 1.4 collective-permute-start.26
  131.6 4.2 %collective-permute-start.27 = (f32[8192]{0:T(1024)S(1)}, f32[8192]{0:T(1024)S(1)}, u32[]{:S(2)}, u32[]{:S(2)}) collective-permute-start(f32[8192]{0:T(1024)S(1)} %add.321), channel_id=1, source_target_pairs={{0,8},{8,16},{16,24},{24,0},{1,9},{9,17},{17,25},{25,1},{2,10},{10... | collective-permute-start | bytes 98312 | tf_op jit(solution)/shard_map/ppermute | solution.py:25
  133.6 5.4 %collective-permute-start.28 = (f32[8192]{0:T(1024)S(1)}, f32[8192]{0:T(1024)S(1)}, u32[]{:S(2)}, u32[]{:S(2)}) collective-permute-start(f32[8192]{0:T(1024)S(1)} %add.321), channel_id=1, source_target_pairs={{0,16},{8,24},{16,0},{24,8},{1,17},{9,25},{17,1},{25,9},{2,18},{10... | collective-permute-start | bytes 98312 | tf_op jit(solution)/shard_map/ppermute | solution.py:25
  134.5 5.1 %collective-permute-start.29 = (f32[8192]{0:T(1024)S(1)}, f32[8192]{0:T(1024)S(1)}, u32[]{:S(2)}, u32[]{:S(2)}) collective-permute-start(f32[8192]{0:T(1024)S(1)} %add.321), channel_id=1, source_target_pairs={{0,24},{8,0},{16,8},{24,16},{1,25},{9,1},{17,9},{25,17},{2,26},{10... | collective-permute-start | bytes 98312 | tf_op jit(solution)/shard_map/ppermute | solution.py:25
  139.6 5.2 %collective-permute-start.30 = (f32[8192]{0:T(1024)S(1)}, f32[8192]{0:T(1024)S(1)}, u32[]{:S(2)}, u32[]{:S(2)}) collective-permute-start(f32[8192]{0:T(1024)S(1)} %add_add_fusion), channel_id=1, source_target_pairs={{0,32},{32,64},{64,96},{96,0},{1,33},{33,65},{65,97},{97,1},{2,34}... | collective-permute-start | bytes 98312 | tf_op jit(solution)/shard_map/ppermute | solution.py:25
  139.7 5.4 %collective-permute-start.31 = (f32[8192]{0:T(1024)S(1)}, f32[8192]{0:T(1024)S(1)}, u32[]{:S(2)}, u32[]{:S(2)}) collective-permute-start(f32[8192]{0:T(1024)S(1)} %add_add_fusion), channel_id=1, source_target_pairs={{0,64},{32,96},{64,0},{96,32},{1,65},{33,97},{65,1},{97,33},{2,66}... | collective-permute-start | bytes 98312 | tf_op jit(solution)/shard_map/ppermute | solution.py:25
  142.5 3.9 %collective-permute-start.32 = (f32[8192]{0:T(1024)S(1)}, f32[8192]{0:T(1024)S(1)}, u32[]{:S(2)}, u32[]{:S(2)}) collective-permute-start(f32[8192]{0:T(1024)S(1)} %add_add_fusion), channel_id=1, source_target_pairs={{0,96},{32,0},{64,32},{96,64},{1,97},{33,1},{65,33},{97,65},{2,98}... | collective-permute-start | bytes 98312 | tf_op jit(solution)/shard_map/ppermute | solution.py:25
  147.0 18.7 %copy-start.5 = (f32[8192]{0:T(1024)S(1)}, f32[8192]{0:T(1024)}, u32[]{:S(2)}) copy-start(f32[8192]{0:T(1024)} %add_divide_fusion) | copy-start | bytes 98308
  157.9 4.9 %collective-permute-start.33 = (f32[512]{0:T(512)S(1)}, f32[512]{0:T(512)S(1)}, u32[]{:S(2)}, u32[]{:S(2)}) collective-permute-start(f32[512]{0:T(512)S(1)} %reduce.4), channel_id=1, source_target_pairs={{0,1},{1,2},{2,3},{3,0},{4,5},{5,6},{6,7},{7,4},{8,9},{9,10},{10,1... | collective-permute-start | bytes 6152 | tf_op jit(solution)/shard_map/ppermute | solution.py:25
  159.3 5.1 %collective-permute-start.34 = (f32[512]{0:T(512)S(1)}, f32[512]{0:T(512)S(1)}, u32[]{:S(2)}, u32[]{:S(2)}) collective-permute-start(f32[512]{0:T(512)S(1)} %reduce.4), channel_id=1, source_target_pairs={{0,2},{1,3},{2,0},{3,1},{4,6},{5,7},{6,4},{7,5},{8,10},{9,11},{10,... | collective-permute-start | bytes 6152 | tf_op jit(solution)/shard_map/ppermute | solution.py:25
  162.1 3.6 %collective-permute-start.35 = (f32[512]{0:T(512)S(1)}, f32[512]{0:T(512)S(1)}, u32[]{:S(2)}, u32[]{:S(2)}) collective-permute-start(f32[512]{0:T(512)S(1)} %reduce.4), channel_id=1, source_target_pairs={{0,3},{1,0},{2,1},{3,2},{4,7},{5,4},{6,5},{7,6},{8,11},{9,8},{10,9... | collective-permute-start | bytes 6152 | tf_op jit(solution)/shard_map/ppermute | solution.py:25
  165.7 11.1 %copy-start.2 = (bf16[256,8192]{1,0:T(8,128)(2,1)S(1)}, bf16[256,8192]{1,0:T(8,128)(2,1)}, u32[]{:S(2)}) copy-start(bf16[256,8192]{1,0:T(8,128)(2,1)} %fusion.1.n_ref) | copy-start | bytes 12582916
  179.2 10.5 %collective-permute-start.36 = (bf16[512,256]{1,0:T(8,128)(2,1)S(1)}, bf16[512,256]{1,0:T(8,128)(2,1)S(1)}, u32[]{:S(2)}, u32[]{:S(2)}) collective-permute-start(bf16[512,256]{1,0:T(8,128)(2,1)S(1)} %get-tuple-element.24), channel_id=1, source_target_pairs={{0,1},{1,2},{2,3},{3,0},{4,5},{5,6},{6,7},{7,4},{8,9},{9,10},{10,1... | collective-permute-start | bytes 786440 | tf_op jit(solution)/shard_map/ppermute | solution.py:25
  179.3 10.4 %collective-permute-start.37 = (bf16[512,256]{1,0:T(8,128)(2,1)S(1)}, bf16[512,256]{1,0:T(8,128)(2,1)S(1)}, u32[]{:S(2)}, u32[]{:S(2)}) collective-permute-start(bf16[512,256]{1,0:T(8,128)(2,1)S(1)} %get-tuple-element.24), channel_id=1, source_target_pairs={{0,2},{1,3},{2,0},{3,1},{4,6},{5,7},{6,4},{7,5},{8,10},{9,11},{10,... | collective-permute-start | bytes 786440 | tf_op jit(solution)/shard_map/ppermute | solution.py:25
  182.0 8.6 %collective-permute-start.38 = (bf16[512,256]{1,0:T(8,128)(2,1)S(1)}, bf16[512,256]{1,0:T(8,128)(2,1)S(1)}, u32[]{:S(2)}, u32[]{:S(2)}) collective-permute-start(bf16[512,256]{1,0:T(8,128)(2,1)S(1)} %get-tuple-element.24), channel_id=1, source_target_pairs={{0,3},{1,0},{2,1},{3,2},{4,7},{5,4},{6,5},{7,6},{8,11},{9,8},{10,9... | collective-permute-start | bytes 786440 | tf_op jit(solution)/shard_map/ppermute | solution.py:25
  202.9 4.6 %collective-permute-start.39 = (bf16[4,4,8,8704]{3,2,0,1:T(8,128)(2,1)}, bf16[4,4,8,8704]{3,2,0,1:T(8,128)(2,1)S(1)}, u32[]{:S(2)}, u32[]{:S(2)}) collective-permute-start(bf16[4,4,8,8704]{3,2,0,1:T(8,128)(2,1)} %fusion.2), channel_id=1, source_target_pairs={{0,4},{4,0},{1,5},{5,1},{2,6},{6,2},{3,7},{7,3},{8,12},{12,8},{9,1... | collective-permute-start | bytes 6684680 | tf_op jit(solution)/shard_map/ppermute | solution.py:25
  212.3 15.6 %collective-permute-start.40 = (bf16[4,8,8704]{2,1,0:T(8,128)(2,1)S(1)}, bf16[4,8,8704]{2,1,0:T(8,128)(2,1)S(1)}, u32[]{:S(2)}, u32[]{:S(2)}) collective-permute-start(bf16[4,8,8704]{2,1,0:T(8,128)(2,1)S(1)} %get-tuple-element.13), channel_id=1, source_target_pairs={{0,8},{8,16},{16,24},{24,0},{1,9},{9,17},{17,25},{25,1},{2,10},{10... | collective-permute-start | bytes 1671176 | tf_op jit(solution)/shard_map/ppermute | solution.py:25
  213.0 17.0 %collective-permute-start.41 = (bf16[4,8,8704]{2,1,0:T(8,128)(2,1)S(1)}, bf16[4,8,8704]{2,1,0:T(8,128)(2,1)S(1)}, u32[]{:S(2)}, u32[]{:S(2)}) collective-permute-start(bf16[4,8,8704]{2,1,0:T(8,128)(2,1)S(1)} %get-tuple-element.15), channel_id=1, source_target_pairs={{0,16},{8,24},{16,0},{24,8},{1,17},{9,25},{17,1},{25,9},{2,18},{10... | collective-permute-start | bytes 1671176 | tf_op jit(solution)/shard_map/ppermute | solution.py:25
  213.9 27.0 %collective-permute-start.42 = (bf16[4,8,8704]{2,1,0:T(8,128)(2,1)S(1)}, bf16[4,8,8704]{2,1,0:T(8,128)(2,1)}, u32[]{:S(2)}, u32[]{:S(2)}) collective-permute-start(bf16[4,8,8704]{2,1,0:T(8,128)(2,1)S(1)} %get-tuple-element.14), channel_id=1, source_target_pairs={{0,24},{8,0},{16,8},{24,16},{1,25},{9,1},{17,9},{25,17},{2,26},{10... | collective-permute-start | bytes 1671176 | tf_op jit(solution)/shard_map/ppermute | solution.py:25
  242.6 7.0 %collective-permute-start.43 = (bf16[8,8704]{1,0:T(8,128)(2,1)S(1)}, bf16[8,8704]{1,0:T(8,128)(2,1)S(1)}, u32[]{:S(2)}, u32[]{:S(2)}) collective-permute-start(bf16[8,8704]{1,0:T(8,128)(2,1)S(1)} %get-tuple-element.16), channel_id=1, source_target_pairs={{0,32},{32,64},{64,96},{96,0},{1,33},{33,65},{65,97},{97,1},{2,34}... | collective-permute-start | bytes 417800 | tf_op jit(solution)/shard_map/ppermute | solution.py:25
  244.0 9.3 %collective-permute-start.44 = (bf16[8,8704]{1,0:T(8,128)(2,1)S(1)}, bf16[8,8704]{1,0:T(8,128)(2,1)S(1)}, u32[]{:S(2)}, u32[]{:S(2)}) collective-permute-start(bf16[8,8704]{1,0:T(8,128)(2,1)S(1)} %get-tuple-element.18), channel_id=1, source_target_pairs={{0,64},{32,96},{64,0},{96,32},{1,65},{33,97},{65,1},{97,33},{2,66}... | collective-permute-start | bytes 417800 | tf_op jit(solution)/shard_map/ppermute | solution.py:25
  246.7 6.6 %collective-permute-start.45 = (bf16[8,8704]{1,0:T(8,128)(2,1)S(1)}, bf16[8,8704]{1,0:T(8,128)(2,1)S(1)}, u32[]{:S(2)}, u32[]{:S(2)}) collective-permute-start(bf16[8,8704]{1,0:T(8,128)(2,1)S(1)} %get-tuple-element.17), channel_id=1, source_target_pairs={{0,96},{32,0},{64,32},{96,64},{1,97},{33,1},{65,33},{97,65},{2,98}... | collective-permute-start | bytes 417800 | tf_op jit(solution)/shard_map/ppermute | solution.py:25
  (4 other events, 20.8 us)

commit v2 on v1

--- a/solution.py
+++ b/solution.py
@@ -5,13 +5,13 @@
 from jax import lax
 from jax.experimental import pallas as pl
 from jax.sharding import Mesh
+
 from jax.sharding import PartitionSpec as P
 
 PROTOS = 32768
 ITERS = 3
 
 
-sink_eps = 0.05
 soft_temp = 0.1
 
 DP = ("y", "x", "core")
@@ -168,13 +168,17 @@
     factor = PROTOS / (soft_temp * math.sqrt(tokens_all))
     dscore = ((probs - plan) * factor).astype(BF16)
     pg_part = lax.dot_general(unit_b, dscore, (((0,), (0,)), ((), ())), preferred_element_type=F32)
+    R, N = pg_part.shape
+    a = pg_part.reshape(SIZES["y"], SIZES["x"], SIZES["core"], R // 32, N)
+    a = _rs(a, "core", 2, BF16)
     dunit_part = lax.dot_general(dscore, normed, (((1,), (1,)), ((), ())), preferred_element_type=F32)
+    a = _rs(a, "x", 1, BF16)
     dunit = _allsum(dunit_part, "z", BF16)
     dproj = ((dunit - unit * jnp.sum(unit * dunit, axis=1, keepdims=True)) / length).astype(BF16)
     head_part = lax.dot_general(dproj, features, (((0,), (0,)), ((), ())), preferred_element_type=F32)
-    Pn = pg_part.shape[1]
-    both = _rs_dp(jnp.concatenate([pg_part, head_part], axis=1), BF16)
-    return (codes, both[:, :Pn], both[:, Pn:])
+    head_grad = _rs_dp(head_part, BF16)
+    proto_grad = _rs(a, "y", 0, BF16)
+    return (codes, proto_grad, head_grad)
 
 
 def solution(mesh):
@@ -182,4 +186,5 @@
     m4 = Mesh(devs, ("y", "x", "core", "z"))
     in_specs = (P(DP, "z"), P("z", None), P(None, "z"))
     out_specs = (P(DP, "z"), P(DP, "z"), P(DP, "z"))
+
     return jax.shard_map(on_device, mesh=m4, in_specs=in_specs, out_specs=out_specs, check_vma=False)

time: 256 us -> 256 us (level)
  starting transfers between devices: 56.9 us -> 64.9 us
  other arithmetic: 39.1 us -> 34.2 us
  local copies, waits for them, and re-layouts: 10.8 us -> 6.61 us
    ppermute x46 -> x53, starting transfers between devices: 56.9 us -> 64.9 us  [_shift(): return lax.ppermute(v, ax, [(i, (i + k) % n) for i in range(n)])]
    concatenate x1 -> x0, other arithmetic: 7.64 us -> none  [on_device(): both = _rs_dp(jnp.concatenate([pg_part, head_part], axis=1), BF16)]
    dot_general x1, matrix products: 5.8 us -> 2.45 us  [on_device(): lax.dot_general(unit_b, dscore, (((0,), (0,)), ((), ())), preferred_eleme...]
    convert_element_type x3 -> x6, local copies, waits for them, and re-layouts: 4.06 us -> 1.16 us  [_rs(): blk = blk.astype(dt)]
    ppermute x46 -> x53, waiting for transfers between devices: 79.1 us -> 81.5 us  [_shift(): return lax.ppermute(v, ax, [(i, (i + k) % n) for i in range(n)])]
    add x4 -> x7, other arithmetic: 4.4 us -> 6.29 us  [_rs(): acc = acc + _shift(blk, ax, k).astype(a.dtype)]
  transfers between devices with their start and end apart: 46 -> 53, of which waited for: 39 -> 39; matrix products, arithmetic and copies ran while one was open for 5% -> 8% of each run, Pallas kernels for 0% -> 0%
where the time goes in v2:
time: 256 us; the launch traced here: 254 us
  waiting for transfers between devices  81.5 us (32%)
  starting transfers between devices  64.9 us (25%)
  Pallas kernels  57.4 us (22%)
  other arithmetic  34.2 us (13%)
  matrix products  8.88 us (3%)
  local copies, waits for them, and re-layouts  6.61 us (3%)
    ppermute x53, waiting for transfers between devices, _shift(): return lax.ppermute(v, ax, [(i, (i + k) % n) for i in range(n)])  81.5 us
    ppermute x53, starting transfers between devices, _shift(): return lax.ppermute(v, ax, [(i, (i + k) % n) for i in range(n)])  64.9 us
    pallas_call x3, Pallas kernels, _rowpass(): pl.pallas_call(_row_kernel, grid=(T // bt,), in_specs=[pl.BlockSpec((bt,...  28.2 us
    pallas_call x2, Pallas kernels, _colpass(): pl.pallas_call(_col_kernel, grid=(Pn // bp,), in_specs=[pl.BlockSpec((T,...  18.5 us
    convert_element_type x1, other arithmetic, on_device(): dscore = ((probs - plan) * factor).astype(BF16)  10.8 us
    pallas_call x1, Pallas kernels, _scores(): pl.pallas_call(_score_kernel, grid=(Pn // bp,), in_specs=[pl.BlockSpec((T...  10.7 us
    add x7, other arithmetic, _rs(): acc = acc + _shift(blk, ax, k).astype(a.dtype)  6.29 us
  transfers between devices with their start and end apart: 53, of which 39 were waited for; matrix products, arithmetic and copies ran while one was open for 8% of the time, Pallas kernels for 0%

profile of v2, /device:TPU:6, one launch (start us, length us, event | category | flops | bytes accessed | tf_op | source)
XLA Modules:
  0.0 254.4 jit_solution(17841115640190270445)
XLA Ops:
  3.1 2.0 collective-permute-start
  5.1 3.6 %collective-permute-start.1 = (f32[128,256]{1,0:T(8,128)S(1)}, f32[128,256]{1,0:T(8,128)S(1)}, u32[]{:S(2)}, u32[]{:S(2)}) collective-permute-start(f32[128,256]{1,0:T(8,128)S(1)} %get-tuple-element.21), channel_id=1, source_target_pairs={{0,2},{1,3},{2,0},{3,1},{4,6},{5,7},{6,4},{7,5},{8,10},{9,11},{10,... | collective-permute-start | bytes 393224 | tf_op jit(solution)/shard_map/ppermute | solution.py:25
  9.7 3.1 %fusion = f32[8192]{0:T(1024)S(1)} fusion(bf16[256,8192]{1,0:T(8,128)(2,1)} %param.5), kind=kLoop, calls=%fused_computation.6 | loop fusion | flops 6283264 | bytes 4227072 | tf_op jit(solution)/shard_map/reduce_sum | solution.py:149
  12.8 2.9 %fusion.1.n_ref = bf16[256,8192]{1,0:T(8,128)(2,1)} fusion(bf16[256,8192]{1,0:T(8,128)(2,1)S(1)} %copy-done.2, f32[8192]{0:T(1024)S(1)} %add_sqrt_fusion), kind=kLoop, calls=%fused_computation.7 | loop fusion | flops 6291456 | bytes 8421376 | tf_op jit(solution)/shard_map/convert_element_type | solution.py:149
  16.9 1.6 collective-permute-start.4
  19.7 4.7 %collective-permute-done.3 = f32[128,256]{1,0:T(8,128)S(1)} collective-permute-done((f32[128,256]{1,0:T(8,128)S(1)}, f32[128,256]{1,0:T(8,128)S(1)}, u32[]{:S(2)}, u32[]{:S(2)}) %collective-permute-start.3) | collective-permute-done | bytes 131104 | tf_op jit(solution)/shard_map/ppermute | solution.py:25
  26.5 10.7 %shard_map.58 = (f32[512,8192]{1,0:T(8,128)}, f32[1,8192]{1,0:T(1,128)}, f32[512,1]{1,0:T(8,128)}) custom-call(bf16[512,256]{1,0:T(8,128)(2,1)} %get-tuple-element.9.u_ref, bf16[256,8192]{1,0:T(8,128)(2,1)} %fusion.1.n_ref), custom_call_target="tpu_custom_call" | custom-call | tf_op jit(solution)/shard_map/pallas_call | solution.py:89
  39.9 2.4 collective-permute-start.8
  43.4 1.9 collective-permute-done.8
  45.3 2.1 collective-permute-done.9
  47.4 1.6 collective-permute-start.10
  49.1 2.9 %collective-permute-start.11 = (f32[8192]{0:T(1024)S(1)}, f32[8192]{0:T(1024)S(1)}, u32[]{:S(2)}, u32[]{:S(2)}) collective-permute-start(f32[8192]{0:T(1024)S(1)} %add_add_fusion.2), channel_id=1, source_target_pairs={{0,64},{32,96},{64,0},{96,32},{1,65},{33,97},{65,1},{97,33},{2,66}... | collective-permute-start | bytes 98312 | tf_op jit(solution)/shard_map/ppermute | solution.py:25
  56.5 9.4 %shard_map.59 = f32[512,1]{1,0:T(8,128)} custom-call(f32[512,8192]{1,0:T(8,128)} %get-tuple-element.6.s_ref, f32[1,8192]{1,0:T(1,128)} %bitcast.126), custom_call_target="tpu_custom_call" | custom-call | tf_op jit(solution)/shard_map/pallas_call | solution.py:130
  67.9 3.3 %collective-permute-start.14 = (f32[2,512]{1,0:T(2,128)S(1)}, f32[2,512]{1,0:T(2,128)S(1)}, u32[]{:S(2)}, u32[]{:S(2)}) collective-permute-start(f32[2,512]{1,0:T(2,128)S(1)} %pad_maximum_fusion.1), channel_id=1, source_target_pairs={{0,2},{1,3},{2,0},{3,1},{4,6},{5,7},{6,4},{7,5},{8,10},{9,11},{10,... | collective-permute-start | bytes 12296 | tf_op jit(solution)/shard_map/ppermute | solution.py:25
  73.0 1.8 collective-permute-done.15
  75.7 9.3 %shard_map.60 = f32[1,8192]{1,0:T(1,128)} custom-call(f32[512,8192]{1,0:T(8,128)} %get-tuple-element.6.s_ref, f32[512,1]{1,0:T(8,128)} %copy.13.r_ref), custom_call_target="tpu_custom_call" | custom-call | tf_op jit(solution)/shard_map/pallas_call | solution.py:114
  89.2 1.9 collective-permute-done.17
  91.1 2.1 collective-permute-done.18
  94.0 3.8 %collective-permute-start.21 = (f32[8192]{0:T(1024)S(1)}, f32[8192]{0:T(1024)S(1)}, u32[]{:S(2)}, u32[]{:S(2)}) collective-permute-start(f32[8192]{0:T(1024)S(1)} %add_add_fusion.1), channel_id=1, source_target_pairs={{0,64},{32,96},{64,0},{96,32},{1,65},{33,97},{65,1},{97,33},{2,66}... | collective-permute-start | bytes 98312 | tf_op jit(solution)/shard_map/ppermute | solution.py:25
  100.1 1.7 collective-permute-done.22
  102.4 9.4 %shard_map.61 = f32[512,1]{1,0:T(8,128)} custom-call(f32[512,8192]{1,0:T(8,128)} %get-tuple-element.6.s_ref, f32[1,8192]{1,0:T(1,128)} %bitcast.127), custom_call_target="tpu_custom_call" | custom-call | tf_op jit(solution)/shard_map/pallas_call | solution.py:130
  113.0 2.7 %collective-permute-start.24 = (f32[512]{0:T(512)S(1)}, f32[512]{0:T(512)S(1)}, u32[]{:S(2)}, u32[]{:S(2)}) collective-permute-start(f32[512]{0:T(512)S(1)} %reduce.3), channel_id=1, source_target_pairs={{0,2},{1,3},{2,0},{3,1},{4,6},{5,7},{6,4},{7,5},{8,10},{9,11},{10,... | collective-permute-start | bytes 6152 | tf_op jit(solution)/shard_map/ppermute | solution.py:25
  115.7 1.5 collective-permute-start.25
  120.1 9.3 %shard_map.62 = f32[1,8192]{1,0:T(1,128)} custom-call(f32[512,8192]{1,0:T(8,128)} %get-tuple-element.6.s_ref, f32[512,1]{1,0:T(8,128)} %copy.14.r_ref), custom_call_target="tpu_custom_call" | custom-call | tf_op jit(solution)/shard_map/pallas_call | solution.py:114
  131.6 2.0 collective-permute-start.27
  135.7 3.2 %collective-permute-done.28 = f32[8192]{0:T(1024)S(1)} collective-permute-done((f32[8192]{0:T(1024)S(1)}, f32[8192]{0:T(1024)S(1)}, u32[]{:S(2)}, u32[]{:S(2)}) %collective-permute-start.28) | collective-permute-done | bytes 32800 | tf_op jit(solution)/shard_map/ppermute | solution.py:25
  139.7 2.7 %collective-permute-start.31 = (f32[8192]{0:T(1024)S(1)}, f32[8192]{0:T(1024)S(1)}, u32[]{:S(2)}, u32[]{:S(2)}) collective-permute-start(f32[8192]{0:T(1024)S(1)} %add_add_fusion), channel_id=1, source_target_pairs={{0,64},{32,96},{64,0},{96,32},{1,65},{33,97},{65,1},{97,33},{2,66}... | collective-permute-start | bytes 98312 | tf_op jit(solution)/shard_map/ppermute | solution.py:25
  147.0 9.4 %shard_map.63 = f32[512,1]{1,0:T(8,128)} custom-call(f32[512,8192]{1,0:T(8,128)} %get-tuple-element.6.s_ref, f32[1,8192]{1,0:T(1,128)} %bitcast.119), custom_call_target="tpu_custom_call" | custom-call | tf_op jit(solution)/shard_map/pallas_call | solution.py:130
  157.5 1.5 collective-permute-start.33
  159.0 2.7 %collective-permute-start.34 = (f32[512]{0:T(512)S(1)}, f32[512]{0:T(512)S(1)}, u32[]{:S(2)}, u32[]{:S(2)}) collective-permute-start(f32[512]{0:T(512)S(1)} %reduce.4), channel_id=1, source_target_pairs={{0,2},{1,3},{2,0},{3,1},{4,6},{5,7},{6,4},{7,5},{8,10},{9,11},{10,... | collective-permute-start | bytes 6152 | tf_op jit(solution)/shard_map/ppermute | solution.py:25
  162.4 1.7 collective-permute-done.34
  165.3 10.8 %multiply_convert_fusion = (bf16[512,8192]{1,0:T(8,128)(2,1)S(1)}, bf16[512,8192]{1,0:T(8,128)(2,1)}) fusion(f32[512,8192]{1,0:T(8,128)} %get-tuple-element.6.s_ref, f32[512]{0:T(512)S(1)} %bitcast.138, f32[512]{0:T(512)S(1)} %add_divide_fusion.3, f32[8192]{0:T(1024)S(1)} %copy-done.6), kind=kLoop, calls=%fused_computation.1 | loop fusion | flops 37748736 | bytes 33591296 | tf_op jit(solution)/shard_map/convert_element_type | solution.py:169
  176.1 2.5 fusion.2
  179.0 3.2 %fusion.36 = (bf16[512,256]{1,0:T(8,128)(2,1)}, f32[512,256]{1,0:T(8,128)}) fusion(bf16[512,8192]{1,0:T(8,128)(2,1)S(1)} %get-tuple-element.11, bf16[256,8192]{1,0:T(8,128)(2,1)S(1)} %copy-done.3), kind=kOutput, calls=%fused_computation.92 | convolution fusion | flops 2147614720 | bytes 13369344 | tf_op jit(solution)/shard_map/dot_general | solution.py:174
  182.2 2.7 %collective-permute-start.44 = (bf16[512,256]{1,0:T(8,128)(2,1)}, bf16[512,256]{1,0:T(8,128)(2,1)}, u32[]{:S(2)}, u32[]{:S(2)}) collective-permute-start(bf16[512,256]{1,0:T(8,128)(2,1)} %get-tuple-element.30), channel_id=1, source_target_pairs={{0,2},{1,3},{2,0},{3,1},{4,6},{5,7},{6,4},{7,5},{8,10},{9,11},{10,... | collective-permute-start | bytes 786440 | tf_op jit(solution)/shard_map/ppermute | solution.py:25
  186.4 11.6 %collective-permute-done.43 = bf16[512,256]{1,0:T(8,128)(2,1)S(1)} collective-permute-done((bf16[512,256]{1,0:T(8,128)(2,1)}, bf16[512,256]{1,0:T(8,128)(2,1)S(1)}, u32[]{:S(2)}, u32[]{:S(2)}) %collective-permute-start.43) | collective-permute-done | bytes 262176 | tf_op jit(solution)/shard_map/ppermute | solution.py:25
  200.1 1.8 fusion.10
  202.0 3.2 %bitcast_add_fusion = f32[4,4,8,8192]{3,2,1,0:T(8,128)S(1)} fusion(bf16[4,4,8,8192]{3,2,1,0:T(8,128)(2,1)} %collective-permute-done.36, f32[4,4,2,8,8192]{4,3,2,1,0:T(8,128)} %copy-done.1, s32[]{:T(128)S(6)} %select_n.148), kind=kLoop, calls=%fused_computation.10 | loop fusion | flops 2097152 | bytes 10485764 | tf_op jit(solution)/shard_map/add | solution.py:50
  205.3 1.9 copy-done.4
  211.0 1.9 collective-permute-start.47
  214.3 19.8 %collective-permute-done.47 = bf16[4,8,512]{2,1,0:T(8,128)(2,1)S(1)} collective-permute-done((bf16[4,8,512]{2,1,0:T(8,128)(2,1)S(1)}, bf16[4,8,512]{2,1,0:T(8,128)(2,1)S(1)}, u32[]{:S(2)}, u32[]{:S(2)}) %collective-permute-start.47) | collective-permute-done | bytes 32800 | tf_op jit(solution)/shard_map/ppermute | solution.py:25
  234.1 1.5 collective-permute-done.48
  235.6 3.6 %collective-permute-done.49 = bf16[4,8,512]{2,1,0:T(8,128)(2,1)S(1)} collective-permute-done((bf16[4,8,512]{2,1,0:T(8,128)(2,1)S(1)}, bf16[4,8,512]{2,1,0:T(8,128)(2,1)S(1)}, u32[]{:S(2)}, u32[]{:S(2)}) %collective-permute-start.49) | collective-permute-done | bytes 32800 | tf_op jit(solution)/shard_map/ppermute | solution.py:25
  240.6 2.7 %collective-permute-start.51 = (bf16[8,512]{1,0:T(8,128)(2,1)S(1)}, bf16[8,512]{1,0:T(8,128)(2,1)S(1)}, u32[]{:S(2)}, u32[]{:S(2)}) collective-permute-start(bf16[8,512]{1,0:T(8,128)(2,1)S(1)} %get-tuple-element.27), channel_id=1, source_target_pairs={{0,64},{32,96},{64,0},{96,32},{1,65},{33,97},{65,1},{97,33},{2,66}... | collective-permute-start | bytes 24584 | tf_op jit(solution)/shard_map/ppermute | solution.py:25
  243.5 1.6 fusion.6
  245.2 2.0 collective-permute-start.40
  247.9 1.9 collective-permute-start.42
  251.4 2.2 collective-permute-done.41
  (129 shorter events, 59.6 us)
Async XLA Ops:
  3.1 12.6 %collective-permute-start = (f32[128,256]{1,0:T(8,128)S(1)}, f32[128,256]{1,0:T(8,128)S(1)}, u32[]{:S(2)}, u32[]{:S(2)}) collective-permute-start(f32[128,256]{1,0:T(8,128)S(1)} %get-tuple-element.19), channel_id=1, source_target_pairs={{0,1},{1,2},{2,3},{3,0},{4,5},{5,6},{6,7},{7,4},{8,9},{9,10},{10,1... | collective-permute-start | bytes 393224 | tf_op jit(solution)/shard_map/ppermute | solution.py:25
  5.1 10.6 %collective-permute-start.1 = (f32[128,256]{1,0:T(8,128)S(1)}, f32[128,256]{1,0:T(8,128)S(1)}, u32[]{:S(2)}, u32[]{:S(2)}) collective-permute-start(f32[128,256]{1,0:T(8,128)S(1)} %get-tuple-element.21), channel_id=1, source_target_pairs={{0,2},{1,3},{2,0},{3,1},{4,6},{5,7},{6,4},{7,5},{8,10},{9,11},{10,... | collective-permute-start | bytes 393224 | tf_op jit(solution)/shard_map/ppermute | solution.py:25
  8.7 7.0 %collective-permute-start.2 = (f32[128,256]{1,0:T(8,128)S(1)}, f32[128,256]{1,0:T(8,128)S(1)}, u32[]{:S(2)}, u32[]{:S(2)}) collective-permute-start(f32[128,256]{1,0:T(8,128)S(1)} %get-tuple-element.20), channel_id=1, source_target_pairs={{0,3},{1,0},{2,1},{3,2},{4,7},{5,4},{6,5},{7,6},{8,11},{9,8},{10,9... | collective-permute-start | bytes 393224 | tf_op jit(solution)/shard_map/ppermute | solution.py:25
  15.8 8.7 %collective-permute-start.3 = (f32[128,256]{1,0:T(8,128)S(1)}, f32[128,256]{1,0:T(8,128)S(1)}, u32[]{:S(2)}, u32[]{:S(2)}) collective-permute-start(f32[128,256]{1,0:T(8,128)S(1)} %fusion.20), channel_id=1, source_target_pairs={{0,1},{1,2},{2,3},{3,0},{4,5},{5,6},{6,7},{7,4},{8,9},{9,10},{10,1... | collective-permute-start | bytes 393224 | tf_op jit(solution)/shard_map/ppermute | solution.py:25
  16.9 7.6 %collective-permute-start.4 = (f32[128,256]{1,0:T(8,128)S(1)}, f32[128,256]{1,0:T(8,128)S(1)}, u32[]{:S(2)}, u32[]{:S(2)}) collective-permute-start(f32[128,256]{1,0:T(8,128)S(1)} %fusion.20), channel_id=1, source_target_pairs={{0,2},{1,3},{2,0},{3,1},{4,6},{5,7},{6,4},{7,5},{8,10},{9,11},{10,... | collective-permute-start | bytes 393224 | tf_op jit(solution)/shard_map/ppermute | solution.py:25
  18.4 6.4 %collective-permute-start.5 = (f32[128,256]{1,0:T(8,128)S(1)}, f32[128,256]{1,0:T(8,128)S(1)}, u32[]{:S(2)}, u32[]{:S(2)}) collective-permute-start(f32[128,256]{1,0:T(8,128)S(1)} %fusion.20), channel_id=1, source_target_pairs={{0,3},{1,0},{2,1},{3,2},{4,7},{5,4},{6,5},{7,6},{8,11},{9,8},{10,9... | collective-permute-start | bytes 393224 | tf_op jit(solution)/shard_map/ppermute | solution.py:25
  39.4 4.0 %collective-permute-start.7 = (f32[8192]{0:T(1024)S(1)}, f32[8192]{0:T(1024)S(1)}, u32[]{:S(2)}, u32[]{:S(2)}) collective-permute-start(f32[8192]{0:T(1024)S(1)} %add.349), channel_id=1, source_target_pairs={{0,8},{8,16},{16,24},{24,0},{1,9},{9,17},{17,25},{25,1},{2,10},{10... | collective-permute-start | bytes 98312 | tf_op jit(solution)/shard_map/ppermute | solution.py:25
  39.9 5.4 %collective-permute-start.8 = (f32[8192]{0:T(1024)S(1)}, f32[8192]{0:T(1024)S(1)}, u32[]{:S(2)}, u32[]{:S(2)}) collective-permute-start(f32[8192]{0:T(1024)S(1)} %add.349), channel_id=1, source_target_pairs={{0,16},{8,24},{16,0},{24,8},{1,17},{9,25},{17,1},{25,9},{2,18},{10... | collective-permute-start | bytes 98312 | tf_op jit(solution)/shard_map/ppermute | solution.py:25
  42.3 5.1 %collective-permute-start.9 = (f32[8192]{0:T(1024)S(1)}, f32[8192]{0:T(1024)S(1)}, u32[]{:S(2)}, u32[]{:S(2)}) collective-permute-start(f32[8192]{0:T(1024)S(1)} %add.349), channel_id=1, source_target_pairs={{0,24},{8,0},{16,8},{24,16},{1,25},{9,1},{17,9},{25,17},{2,26},{10... | collective-permute-start | bytes 98312 | tf_op jit(solution)/shard_map/ppermute | solution.py:25
  47.4 7.0 %collective-permute-start.10 = (f32[8192]{0:T(1024)S(1)}, f32[8192]{0:T(1024)S(1)}, u32[]{:S(2)}, u32[]{:S(2)}) collective-permute-start(f32[8192]{0:T(1024)S(1)} %add_add_fusion.2), channel_id=1, source_target_pairs={{0,32},{32,64},{64,96},{96,0},{1,33},{33,65},{65,97},{97,1},{2,34}... | collective-permute-start | bytes 98312 | tf_op jit(solution)/shard_map/ppermute | solution.py:25
  49.1 5.4 %collective-permute-start.11 = (f32[8192]{0:T(1024)S(1)}, f32[8192]{0:T(1024)S(1)}, u32[]{:S(2)}, u32[]{:S(2)}) collective-permute-start(f32[8192]{0:T(1024)S(1)} %add_add_fusion.2), channel_id=1, source_target_pairs={{0,64},{32,96},{64,0},{96,32},{1,65},{33,97},{65,1},{97,33},{2,66}... | collective-permute-start | bytes 98312 | tf_op jit(solution)/shard_map/ppermute | solution.py:25
  52.0 3.9 %collective-permute-start.12 = (f32[8192]{0:T(1024)S(1)}, f32[8192]{0:T(1024)S(1)}, u32[]{:S(2)}, u32[]{:S(2)}) collective-permute-start(f32[8192]{0:T(1024)S(1)} %add_add_fusion.2), channel_id=1, source_target_pairs={{0,96},{32,0},{64,32},{96,64},{1,97},{33,1},{65,33},{97,65},{2,98}... | collective-permute-start | bytes 98312 | tf_op jit(solution)/shard_map/ppermute | solution.py:25
  67.0 4.9 %collective-permute-start.13 = (f32[2,512]{1,0:T(2,128)S(1)}, f32[2,512]{1,0:T(2,128)S(1)}, u32[]{:S(2)}, u32[]{:S(2)}) collective-permute-start(f32[2,512]{1,0:T(2,128)S(1)} %pad_maximum_fusion.1), channel_id=1, source_target_pairs={{0,1},{1,2},{2,3},{3,0},{4,5},{5,6},{6,7},{7,4},{8,9},{9,10},{10,1... | collective-permute-start | bytes 12296 | tf_op jit(solution)/shard_map/ppermute | solution.py:25
  67.9 5.1 %collective-permute-start.14 = (f32[2,512]{1,0:T(2,128)S(1)}, f32[2,512]{1,0:T(2,128)S(1)}, u32[]{:S(2)}, u32[]{:S(2)}) collective-permute-start(f32[2,512]{1,0:T(2,128)S(1)} %pad_maximum_fusion.1), channel_id=1, source_target_pairs={{0,2},{1,3},{2,0},{3,1},{4,6},{5,7},{6,4},{7,5},{8,10},{9,11},{10,... | collective-permute-start | bytes 12296 | tf_op jit(solution)/shard_map/ppermute | solution.py:25
  71.2 3.6 %collective-permute-start.15 = (f32[2,512]{1,0:T(2,128)S(1)}, f32[2,512]{1,0:T(2,128)S(1)}, u32[]{:S(2)}, u32[]{:S(2)}) collective-permute-start(f32[2,512]{1,0:T(2,128)S(1)} %pad_maximum_fusion.1), channel_id=1, source_target_pairs={{0,3},{1,0},{2,1},{3,2},{4,7},{5,4},{6,5},{7,6},{8,11},{9,8},{10,9... | collective-permute-start | bytes 12296 | tf_op jit(solution)/shard_map/ppermute | solution.py:25
  87.2 3.9 %collective-permute-start.17 = (f32[8192]{0:T(1024)S(1)}, f32[8192]{0:T(1024)S(1)}, u32[]{:S(2)}, u32[]{:S(2)}) collective-permute-start(f32[8192]{0:T(1024)S(1)} %add.359), channel_id=1, source_target_pairs={{0,8},{8,16},{16,24},{24,0},{1,9},{9,17},{17,25},{25,1},{2,10},{10... | collective-permute-start | bytes 98312 | tf_op jit(solution)/shard_map/ppermute | solution.py:25
  87.8 5.4 %collective-permute-start.18 = (f32[8192]{0:T(1024)S(1)}, f32[8192]{0:T(1024)S(1)}, u32[]{:S(2)}, u32[]{:S(2)}) collective-permute-start(f32[8192]{0:T(1024)S(1)} %add.359), channel_id=1, source_target_pairs={{0,16},{8,24},{16,0},{24,8},{1,17},{9,25},{17,1},{25,9},{2,18},{10... | collective-permute-start | bytes 98312 | tf_op jit(solution)/shard_map/ppermute | solution.py:25
  88.7 5.1 %collective-permute-start.19 = (f32[8192]{0:T(1024)S(1)}, f32[8192]{0:T(1024)S(1)}, u32[]{:S(2)}, u32[]{:S(2)}) collective-permute-start(f32[8192]{0:T(1024)S(1)} %add.359), channel_id=1, source_target_pairs={{0,24},{8,0},{16,8},{24,16},{1,25},{9,1},{17,9},{25,17},{2,26},{10... | collective-permute-start | bytes 98312 | tf_op jit(solution)/shard_map/ppermute | solution.py:25
  93.8 5.2 %collective-permute-start.20 = (f32[8192]{0:T(1024)S(1)}, f32[8192]{0:T(1024)S(1)}, u32[]{:S(2)}, u32[]{:S(2)}) collective-permute-start(f32[8192]{0:T(1024)S(1)} %add_add_fusion.1), channel_id=1, source_target_pairs={{0,32},{32,64},{64,96},{96,0},{1,33},{33,65},{65,97},{97,1},{2,34}... | collective-permute-start | bytes 98312 | tf_op jit(solution)/shard_map/ppermute | solution.py:25
  94.0 6.1 %collective-permute-start.21 = (f32[8192]{0:T(1024)S(1)}, f32[8192]{0:T(1024)S(1)}, u32[]{:S(2)}, u32[]{:S(2)}) collective-permute-start(f32[8192]{0:T(1024)S(1)} %add_add_fusion.1), channel_id=1, source_target_pairs={{0,64},{32,96},{64,0},{96,32},{1,65},{33,97},{65,1},{97,33},{2,66}... | collective-permute-start | bytes 98312 | tf_op jit(solution)/shard_map/ppermute | solution.py:25
  97.9 3.9 %collective-permute-start.22 = (f32[8192]{0:T(1024)S(1)}, f32[8192]{0:T(1024)S(1)}, u32[]{:S(2)}, u32[]{:S(2)}) collective-permute-start(f32[8192]{0:T(1024)S(1)} %add_add_fusion.1), channel_id=1, source_target_pairs={{0,96},{32,0},{64,32},{96,64},{1,97},{33,1},{65,33},{97,65},{2,98}... | collective-permute-start | bytes 98312 | tf_op jit(solution)/shard_map/ppermute | solution.py:25
  112.9 4.9 %collective-permute-start.23 = (f32[512]{0:T(512)S(1)}, f32[512]{0:T(512)S(1)}, u32[]{:S(2)}, u32[]{:S(2)}) collective-permute-start(f32[512]{0:T(512)S(1)} %reduce.3), channel_id=1, source_target_pairs={{0,1},{1,2},{2,3},{3,0},{4,5},{5,6},{6,7},{7,4},{8,9},{9,10},{10,1... | collective-permute-start | bytes 6152 | tf_op jit(solution)/shard_map/ppermute | solution.py:25
  113.0 5.2 %collective-permute-start.24 = (f32[512]{0:T(512)S(1)}, f32[512]{0:T(512)S(1)}, u32[]{:S(2)}, u32[]{:S(2)}) collective-permute-start(f32[512]{0:T(512)S(1)} %reduce.3), channel_id=1, source_target_pairs={{0,2},{1,3},{2,0},{3,1},{4,6},{5,7},{6,4},{7,5},{8,10},{9,11},{10,... | collective-permute-start | bytes 6152 | tf_op jit(solution)/shard_map/ppermute | solution.py:25
  131.6 4.2 %collective-permute-start.27 = (f32[8192]{0:T(1024)S(1)}, f32[8192]{0:T(1024)S(1)}, u32[]{:S(2)}, u32[]{:S(2)}) collective-permute-start(f32[8192]{0:T(1024)S(1)} %add.369), channel_id=1, source_target_pairs={{0,8},{8,16},{16,24},{24,0},{1,9},{9,17},{17,25},{25,1},{2,10},{10... | collective-permute-start | bytes 98312 | tf_op jit(solution)/shard_map/ppermute | solution.py:25
  133.5 5.4 %collective-permute-start.28 = (f32[8192]{0:T(1024)S(1)}, f32[8192]{0:T(1024)S(1)}, u32[]{:S(2)}, u32[]{:S(2)}) collective-permute-start(f32[8192]{0:T(1024)S(1)} %add.369), channel_id=1, source_target_pairs={{0,16},{8,24},{16,0},{24,8},{1,17},{9,25},{17,1},{25,9},{2,18},{10... | collective-permute-start | bytes 98312 | tf_op jit(solution)/shard_map/ppermute | solution.py:25
  134.4 5.1 %collective-permute-start.29 = (f32[8192]{0:T(1024)S(1)}, f32[8192]{0:T(1024)S(1)}, u32[]{:S(2)}, u32[]{:S(2)}) collective-permute-start(f32[8192]{0:T(1024)S(1)} %add.369), channel_id=1, source_target_pairs={{0,24},{8,0},{16,8},{24,16},{1,25},{9,1},{17,9},{25,17},{2,26},{10... | collective-permute-start | bytes 98312 | tf_op jit(solution)/shard_map/ppermute | solution.py:25
  139.6 5.2 %collective-permute-start.30 = (f32[8192]{0:T(1024)S(1)}, f32[8192]{0:T(1024)S(1)}, u32[]{:S(2)}, u32[]{:S(2)}) collective-permute-start(f32[8192]{0:T(1024)S(1)} %add_add_fusion), channel_id=1, source_target_pairs={{0,32},{32,64},{64,96},{96,0},{1,33},{33,65},{65,97},{97,1},{2,34}... | collective-permute-start | bytes 98312 | tf_op jit(solution)/shard_map/ppermute | solution.py:25
  139.7 5.4 %collective-permute-start.31 = (f32[8192]{0:T(1024)S(1)}, f32[8192]{0:T(1024)S(1)}, u32[]{:S(2)}, u32[]{:S(2)}) collective-permute-start(f32[8192]{0:T(1024)S(1)} %add_add_fusion), channel_id=1, source_target_pairs={{0,64},{32,96},{64,0},{96,32},{1,65},{33,97},{65,1},{97,33},{2,66}... | collective-permute-start | bytes 98312 | tf_op jit(solution)/shard_map/ppermute | solution.py:25
  142.4 3.9 %collective-permute-start.32 = (f32[8192]{0:T(1024)S(1)}, f32[8192]{0:T(1024)S(1)}, u32[]{:S(2)}, u32[]{:S(2)}) collective-permute-start(f32[8192]{0:T(1024)S(1)} %add_add_fusion), channel_id=1, source_target_pairs={{0,96},{32,0},{64,32},{96,64},{1,97},{33,1},{65,33},{97,65},{2,98}... | collective-permute-start | bytes 98312 | tf_op jit(solution)/shard_map/ppermute | solution.py:25
  157.5 4.9 %collective-permute-start.33 = (f32[512]{0:T(512)S(1)}, f32[512]{0:T(512)S(1)}, u32[]{:S(2)}, u32[]{:S(2)}) collective-permute-start(f32[512]{0:T(512)S(1)} %reduce.4), channel_id=1, source_target_pairs={{0,1},{1,2},{2,3},{3,0},{4,5},{5,6},{6,7},{7,4},{8,9},{9,10},{10,1... | collective-permute-start | bytes 6152 | tf_op jit(solution)/shard_map/ppermute | solution.py:25
  159.0 5.1 %collective-permute-start.34 = (f32[512]{0:T(512)S(1)}, f32[512]{0:T(512)S(1)}, u32[]{:S(2)}, u32[]{:S(2)}) collective-permute-start(f32[512]{0:T(512)S(1)} %reduce.4), channel_id=1, source_target_pairs={{0,2},{1,3},{2,0},{3,1},{4,6},{5,7},{6,4},{7,5},{8,10},{9,11},{10,... | collective-permute-start | bytes 6152 | tf_op jit(solution)/shard_map/ppermute | solution.py:25
  178.9 23.2 %collective-permute-start.36 = (bf16[4,4,8,8192]{3,2,1,0:T(8,128)(2,1)S(1)}, bf16[4,4,8,8192]{3,2,1,0:T(8,128)(2,1)}, u32[]{:S(2)}, u32[]{:S(2)}) collective-permute-start(bf16[4,4,8,8192]{3,2,1,0:T(8,128)(2,1)S(1)} %fusion.4), channel_id=1, source_target_pairs={{0,4},{4,0},{1,5},{5,1},{2,6},{6,2},{3,7},{7,3},{8,12},{12,8},{9,1... | collective-permute-start | bytes 6291464 | tf_op jit(solution)/shard_map/ppermute | solution.py:25
  182.2 15.7 %collective-permute-start.43 = (bf16[512,256]{1,0:T(8,128)(2,1)}, bf16[512,256]{1,0:T(8,128)(2,1)S(1)}, u32[]{:S(2)}, u32[]{:S(2)}) collective-permute-start(bf16[512,256]{1,0:T(8,128)(2,1)} %get-tuple-element.30), channel_id=1, source_target_pairs={{0,1},{1,2},{2,3},{3,0},{4,5},{5,6},{6,7},{7,4},{8,9},{9,10},{10,1... | collective-permute-start | bytes 786440 | tf_op jit(solution)/shard_map/ppermute | solution.py:25
  182.2 15.7 %collective-permute-start.44 = (bf16[512,256]{1,0:T(8,128)(2,1)}, bf16[512,256]{1,0:T(8,128)(2,1)}, u32[]{:S(2)}, u32[]{:S(2)}) collective-permute-start(bf16[512,256]{1,0:T(8,128)(2,1)} %get-tuple-element.30), channel_id=1, source_target_pairs={{0,2},{1,3},{2,0},{3,1},{4,6},{5,7},{6,4},{7,5},{8,10},{9,11},{10,... | collective-permute-start | bytes 786440 | tf_op jit(solution)/shard_map/ppermute | solution.py:25
  184.9 13.7 %collective-permute-start.45 = (bf16[512,256]{1,0:T(8,128)(2,1)}, bf16[512,256]{1,0:T(8,128)(2,1)}, u32[]{:S(2)}, u32[]{:S(2)}) collective-permute-start(bf16[512,256]{1,0:T(8,128)(2,1)} %get-tuple-element.30), channel_id=1, source_target_pairs={{0,3},{1,0},{2,1},{3,2},{4,7},{5,4},{6,5},{7,6},{8,11},{9,8},{10,9... | collective-permute-start | bytes 786440 | tf_op jit(solution)/shard_map/ppermute | solution.py:25
  201.9 8.4 %collective-permute-start.46 = (bf16[4,4,8,512]{3,2,0,1:T(8,128)(2,1)S(1)}, bf16[4,4,8,512]{3,2,0,1:T(8,128)(2,1)S(1)}, u32[]{:S(2)}, u32[]{:S(2)}) collective-permute-start(bf16[4,4,8,512]{3,2,0,1:T(8,128)(2,1)S(1)} %fusion.18), channel_id=1, source_target_pairs={{0,4},{4,0},{1,5},{5,1},{2,6},{6,2},{3,7},{7,3},{8,12},{12,8},{9,1... | collective-permute-start | bytes 393224 | tf_op jit(solution)/shard_map/ppermute | solution.py:25
  207.4 35.9 %collective-permute-start.37 = (bf16[4,8,8192]{2,1,0:T(8,128)(2,1)S(1)}, bf16[4,8,8192]{2,1,0:T(8,128)(2,1)S(1)}, u32[]{:S(2)}, u32[]{:S(2)}) collective-permute-start(bf16[4,8,8192]{2,1,0:T(8,128)(2,1)S(1)} %get-tuple-element.13), channel_id=1, source_target_pairs={{0,8},{8,16},{16,24},{24,0},{1,9},{9,17},{17,25},{25,1},{2,10},{10... | collective-permute-start | bytes 1572872 | tf_op jit(solution)/shard_map/ppermute | solution.py:25
  208.1 35.4 %collective-permute-start.38 = (bf16[4,8,8192]{2,1,0:T(8,128)(2,1)S(1)}, bf16[4,8,8192]{2,1,0:T(8,128)(2,1)S(1)}, u32[]{:S(2)}, u32[]{:S(2)}) collective-permute-start(bf16[4,8,8192]{2,1,0:T(8,128)(2,1)S(1)} %get-tuple-element.15), channel_id=1, source_target_pairs={{0,16},{8,24},{16,0},{24,8},{1,17},{9,25},{17,1},{25,9},{2,18},{10... | collective-permute-start | bytes 1572872 | tf_op jit(solution)/shard_map/ppermute | solution.py:25
  209.0 34.5 %collective-permute-start.39 = (bf16[4,8,8192]{2,1,0:T(8,128)(2,1)S(1)}, bf16[4,8,8192]{2,1,0:T(8,128)(2,1)}, u32[]{:S(2)}, u32[]{:S(2)}) collective-permute-start(bf16[4,8,8192]{2,1,0:T(8,128)(2,1)S(1)} %get-tuple-element.14), channel_id=1, source_target_pairs={{0,24},{8,0},{16,8},{24,16},{1,25},{9,1},{17,9},{25,17},{2,26},{10... | collective-permute-start | bytes 1572872 | tf_op jit(solution)/shard_map/ppermute | solution.py:25
  211.0 23.1 %collective-permute-start.47 = (bf16[4,8,512]{2,1,0:T(8,128)(2,1)S(1)}, bf16[4,8,512]{2,1,0:T(8,128)(2,1)S(1)}, u32[]{:S(2)}, u32[]{:S(2)}) collective-permute-start(bf16[4,8,512]{2,1,0:T(8,128)(2,1)S(1)} %get-tuple-element.22), channel_id=1, source_target_pairs={{0,8},{8,16},{16,24},{24,0},{1,9},{9,17},{17,25},{25,1},{2,10},{10... | collective-permute-start | bytes 98312 | tf_op jit(solution)/shard_map/ppermute | solution.py:25
  212.9 22.7 %collective-permute-start.48 = (bf16[4,8,512]{2,1,0:T(8,128)(2,1)}, bf16[4,8,512]{2,1,0:T(8,128)(2,1)S(1)}, u32[]{:S(2)}, u32[]{:S(2)}) collective-permute-start(bf16[4,8,512]{2,1,0:T(8,128)(2,1)} %get-tuple-element.24), channel_id=1, source_target_pairs={{0,16},{8,24},{16,0},{24,8},{1,17},{9,25},{17,1},{25,9},{2,18},{10... | collective-permute-start | bytes 98312 | tf_op jit(solution)/shard_map/ppermute | solution.py:25
  234.1 5.1 %collective-permute-start.49 = (bf16[4,8,512]{2,1,0:T(8,128)(2,1)S(1)}, bf16[4,8,512]{2,1,0:T(8,128)(2,1)S(1)}, u32[]{:S(2)}, u32[]{:S(2)}) collective-permute-start(bf16[4,8,512]{2,1,0:T(8,128)(2,1)S(1)} %get-tuple-element.23), channel_id=1, source_target_pairs={{0,24},{8,0},{16,8},{24,16},{1,25},{9,1},{17,9},{25,17},{2,26},{10... | collective-permute-start | bytes 98312 | tf_op jit(solution)/shard_map/ppermute | solution.py:25
  239.3 8.7 %collective-permute-start.50 = (bf16[8,512]{1,0:T(8,128)(2,1)S(1)}, bf16[8,512]{1,0:T(8,128)(2,1)S(1)}, u32[]{:S(2)}, u32[]{:S(2)}) collective-permute-start(bf16[8,512]{1,0:T(8,128)(2,1)S(1)} %get-tuple-element.25), channel_id=1, source_target_pairs={{0,32},{32,64},{64,96},{96,0},{1,33},{33,65},{65,97},{97,1},{2,34}... | collective-permute-start | bytes 24584 | tf_op jit(solution)/shard_map/ppermute | solution.py:25
  240.6 9.3 %collective-permute-start.51 = (bf16[8,512]{1,0:T(8,128)(2,1)S(1)}, bf16[8,512]{1,0:T(8,128)(2,1)S(1)}, u32[]{:S(2)}, u32[]{:S(2)}) collective-permute-start(bf16[8,512]{1,0:T(8,128)(2,1)S(1)} %get-tuple-element.27), channel_id=1, source_target_pairs={{0,64},{32,96},{64,0},{96,32},{1,65},{33,97},{65,1},{97,33},{2,66}... | collective-permute-start | bytes 24584 | tf_op jit(solution)/shard_map/ppermute | solution.py:25
  243.4 6.5 %collective-permute-start.52 = (bf16[8,512]{1,0:T(8,128)(2,1)S(1)}, bf16[8,512]{1,0:T(8,128)(2,1)S(1)}, u32[]{:S(2)}, u32[]{:S(2)}) collective-permute-start(bf16[8,512]{1,0:T(8,128)(2,1)S(1)} %get-tuple-element.26), channel_id=1, source_target_pairs={{0,96},{32,0},{64,32},{96,64},{1,97},{33,1},{65,33},{97,65},{2,98}... | collective-permute-start | bytes 24584 | tf_op jit(solution)/shard_map/ppermute | solution.py:25
  245.2 6.3 %collective-permute-start.40 = (bf16[8,8192]{1,0:T(8,128)(2,1)S(1)}, bf16[8,8192]{1,0:T(8,128)(2,1)S(1)}, u32[]{:S(2)}, u32[]{:S(2)}) collective-permute-start(bf16[8,8192]{1,0:T(8,128)(2,1)S(1)} %get-tuple-element.16), channel_id=1, source_target_pairs={{0,32},{32,64},{64,96},{96,0},{1,33},{33,65},{65,97},{97,1},{2,34}... | collective-permute-start | bytes 393224 | tf_op jit(solution)/shard_map/ppermute | solution.py:25
  247.1 6.5 %collective-permute-start.41 = (bf16[8,8192]{1,0:T(8,128)(2,1)S(1)}, bf16[8,8192]{1,0:T(8,128)(2,1)S(1)}, u32[]{:S(2)}, u32[]{:S(2)}) collective-permute-start(bf16[8,8192]{1,0:T(8,128)(2,1)S(1)} %get-tuple-element.18), channel_id=1, source_target_pairs={{0,64},{32,96},{64,0},{96,32},{1,65},{33,97},{65,1},{97,33},{2,66}... | collective-permute-start | bytes 393224 | tf_op jit(solution)/shard_map/ppermute | solution.py:25
  247.9 5.7 %collective-permute-start.42 = (bf16[8,8192]{1,0:T(8,128)(2,1)S(1)}, bf16[8,8192]{1,0:T(8,128)(2,1)S(1)}, u32[]{:S(2)}, u32[]{:S(2)}) collective-permute-start(bf16[8,8192]{1,0:T(8,128)(2,1)S(1)} %get-tuple-element.17), channel_id=1, source_target_pairs={{0,96},{32,0},{64,32},{96,64},{1,97},{33,1},{65,33},{97,65},{2,98}... | collective-permute-start | bytes 393224 | tf_op jit(solution)/shard_map/ppermute | solution.py:25
  (12 other events, 65.2 us)

commit v3 on v2

--- a/solution.py
+++ b/solution.py
@@ -5,7 +5,6 @@
 from jax import lax
 from jax.experimental import pallas as pl
 from jax.sharding import Mesh
-
 from jax.sharding import PartitionSpec as P
 
 PROTOS = 32768
@@ -69,12 +68,14 @@
     return a
 
 
-def _score_kernel(u_ref, n_ref, s_ref, col_ref, rs_ref):
+def _score_kernel(u_ref, n_ref, s_ref, k_ref, col_ref, rs_ref):
     j = pl.program_id(0)
     sc = jnp.dot(u_ref[...], n_ref[...], preferred_element_type=F32)
     s = jnp.exp(sc * (1.0 / soft_temp))
     s_ref[...] = s
-    col_ref[...] = jnp.sum(s * s, axis=0, keepdims=True)
+    k = s * s
+    k_ref[...] = k.astype(BF16)
+    col_ref[...] = jnp.sum(k, axis=0, keepdims=True)
 
     @pl.when(j == 0)
     def _():
@@ -86,27 +87,29 @@
 def _scores(unit_b, normed, bp=1024):
     T, E = unit_b.shape
     Pn = normed.shape[1]
-    soft, col, rs = pl.pallas_call(
+    soft, kb, col, rs = pl.pallas_call(
         _score_kernel,
         grid=(Pn // bp,),
         in_specs=[pl.BlockSpec((T, E), lambda j: (0, 0)), pl.BlockSpec((E, bp), lambda j: (0, j))],
         out_specs=[
+            pl.BlockSpec((T, bp), lambda j: (0, j)),
             pl.BlockSpec((T, bp), lambda j: (0, j)),
             pl.BlockSpec((1, bp), lambda j: (0, j)),
             pl.BlockSpec((T, 1), lambda j: (0, 0)),
         ],
         out_shape=[
             jax.ShapeDtypeStruct((T, Pn), F32),
+            jax.ShapeDtypeStruct((T, Pn), BF16),
             jax.ShapeDtypeStruct((1, Pn), F32),
             jax.ShapeDtypeStruct((T, 1), F32),
         ],
     )(unit_b, normed)
-    return soft, col[0], rs[:, 0]
+    return soft, kb, col[0], rs[:, 0]
 
 
-def _col_kernel(s_ref, r_ref, o_ref):
-    s = s_ref[...]
-    o_ref[...] = jnp.sum(s * s * r_ref[...], axis=0, keepdims=True)
+def _col_kernel(k_ref, r_ref, o_ref):
+    k = k_ref[...].astype(F32)
+    o_ref[...] = jnp.sum(k * r_ref[...], axis=0, keepdims=True)
 
 
 def _colpass(soft, r, bp=1024):
@@ -120,9 +123,9 @@
     )(soft, r.reshape(T, 1))[0]
 
 
-def _row_kernel(s_ref, c_ref, o_ref):
-    s = s_ref[...]
-    o_ref[...] = jnp.sum(s * s * c_ref[...], axis=1, keepdims=True)
+def _row_kernel(k_ref, c_ref, o_ref):
+    k = k_ref[...].astype(F32)
+    o_ref[...] = jnp.sum(k * c_ref[...], axis=1, keepdims=True)
 
 
 def _rowpass(soft, c, bt=64):
@@ -147,14 +150,14 @@
     unit_b = unit.astype(BF16)
     proto_f = prototypes.astype(F32)
     normed = (proto_f / jnp.sqrt(jnp.sum(proto_f * proto_f, axis=0, keepdims=True) + 1e-06)).astype(BF16)
-    soft, col0, soft_local = _scores(unit_b, normed)
+    soft, kern_b, col0, soft_local = _scores(unit_b, normed)
     kern = soft * soft
     r = None
     soft_total = None
     for step in range(ITERS):
-        colpart = col0 if r is None else _colpass(soft, r)
+        colpart = col0 if r is None else _colpass(kern_b, r)
         c = 1.0 / _allsum_dp(colpart)
-        rowpart = _rowpass(soft, c)
+        rowpart = _rowpass(kern_b, c)
         if step == 0:
             both = _allsum(jnp.stack([rowpart, soft_local]), "z")
             row, soft_total = both[0], both[1]

time: 256 us -> 249 us (0.973)
  Pallas kernels: 57.4 us -> 49.9 us
    pallas_call x3, Pallas kernels: 28.2 us -> 23.1 us  [_rowpass(): pl.pallas_call(_row_kernel, grid=(T // bt,), in_specs=[pl.BlockSpec((bt,...]
    pallas_call x2, Pallas kernels: 18.5 us -> 15.1 us  [_colpass(): pl.pallas_call(_col_kernel, grid=(Pn // bp,), in_specs=[pl.BlockSpec((T,...]
where the time goes in v3:
time: 249 us; the launch traced here: 247 us
  waiting for transfers between devices  81.5 us (33%)
  starting transfers between devices  64.9 us (26%)
  Pallas kernels  49.9 us (20%)
  other arithmetic  34.2 us (14%)
  matrix products  8.88 us (4%)
  local copies, waits for them, and re-layouts  6.61 us (3%)
    ppermute x53, waiting for transfers between devices, _shift(): return lax.ppermute(v, ax, [(i, (i + k) % n) for i in range(n)])  81.5 us
    ppermute x53, starting transfers between devices, _shift(): return lax.ppermute(v, ax, [(i, (i + k) % n) for i in range(n)])  64.9 us
    pallas_call x3, Pallas kernels, _rowpass(): pl.pallas_call(_row_kernel, grid=(T // bt,), in_specs=[pl.BlockSpec((bt,...  23.1 us
    pallas_call x2, Pallas kernels, _colpass(): pl.pallas_call(_col_kernel, grid=(Pn // bp,), in_specs=[pl.BlockSpec((T,...  15.1 us
    pallas_call x1, Pallas kernels, _scores(): pl.pallas_call(_score_kernel, grid=(Pn // bp,), in_specs=[pl.BlockSpec((T...  11.7 us
    convert_element_type x1, other arithmetic, on_device(): dscore = ((probs - plan) * factor).astype(BF16)  10.8 us
    add x7, other arithmetic, _rs(): acc = acc + _shift(blk, ax, k).astype(a.dtype)  6.29 us
  transfers between devices with their start and end apart: 53, of which 39 were waited for; matrix products, arithmetic and copies ran while one was open for 8% of the time, Pallas kernels for 0%

profile of v3, /device:TPU:6, one launch (start us, length us, event | category | flops | bytes accessed | tf_op | source)
XLA Modules:
  0.0 246.9 jit_solution(11843285518509509206)
XLA Ops:
  3.1 2.0 collective-permute-start
  5.1 3.6 %collective-permute-start.1 = (f32[128,256]{1,0:T(8,128)S(1)}, f32[128,256]{1,0:T(8,128)S(1)}, u32[]{:S(2)}, u32[]{:S(2)}) collective-permute-start(f32[128,256]{1,0:T(8,128)S(1)} %get-tuple-element.23), channel_id=1, source_target_pairs={{0,2},{1,3},{2,0},{3,1},{4,6},{5,7},{6,4},{7,5},{8,10},{9,11},{10,... | collective-permute-start | bytes 393224 | tf_op jit(solution)/shard_map/ppermute | solution.py:24
  9.7 3.1 %fusion = f32[8192]{0:T(1024)S(1)} fusion(bf16[256,8192]{1,0:T(8,128)(2,1)} %param.5), kind=kLoop, calls=%fused_computation.6 | loop fusion | flops 6283264 | bytes 4227072 | tf_op jit(solution)/shard_map/reduce_sum | solution.py:152
  12.8 2.9 %fusion.1.n_ref = bf16[256,8192]{1,0:T(8,128)(2,1)} fusion(bf16[256,8192]{1,0:T(8,128)(2,1)S(1)} %copy-done.2, f32[8192]{0:T(1024)S(1)} %add_sqrt_fusion), kind=kLoop, calls=%fused_computation.7 | loop fusion | flops 6291456 | bytes 8421376 | tf_op jit(solution)/shard_map/convert_element_type | solution.py:152
  16.9 1.6 collective-permute-start.4
  19.7 4.7 %collective-permute-done.3 = f32[128,256]{1,0:T(8,128)S(1)} collective-permute-done((f32[128,256]{1,0:T(8,128)S(1)}, f32[128,256]{1,0:T(8,128)S(1)}, u32[]{:S(2)}, u32[]{:S(2)}) %collective-permute-start.3) | collective-permute-done | bytes 131104 | tf_op jit(solution)/shard_map/ppermute | solution.py:24
  26.5 11.7 %shard_map.58 = (f32[512,8192]{1,0:T(8,128)}, bf16[512,8192]{1,0:T(8,128)(2,1)}, f32[1,8192]{1,0:T(1,128)}, f32[512,1]{1,0:T(8,128)}) custom-call(bf16[512,256]{1,0:T(8,128)(2,1)} %get-tuple-element.11.u_ref, bf16[256,8192]{1,0:T(8,128)(2,1)} %fusion.1.n_ref), custom_call_target="tpu_custom_call" | custom-call | tf_op jit(solution)/shard_map/pallas_call | solution.py:90
  41.0 2.4 collective-permute-start.8
  44.5 1.9 collective-permute-done.8
  46.4 2.1 collective-permute-done.9
  48.5 1.6 collective-permute-start.10
  50.2 2.9 %collective-permute-start.11 = (f32[8192]{0:T(1024)S(1)}, f32[8192]{0:T(1024)S(1)}, u32[]{:S(2)}, u32[]{:S(2)}) collective-permute-start(f32[8192]{0:T(1024)S(1)} %add_add_fusion.2), channel_id=1, source_target_pairs={{0,64},{32,96},{64,0},{96,32},{1,65},{33,97},{65,1},{97,33},{2,66}... | collective-permute-start | bytes 98312 | tf_op jit(solution)/shard_map/ppermute | solution.py:24
  57.6 7.7 %shard_map.59 = f32[512,1]{1,0:T(8,128)} custom-call(bf16[512,8192]{1,0:T(8,128)(2,1)} %get-tuple-element.8.k_ref, f32[1,8192]{1,0:T(1,128)} %bitcast.126), custom_call_target="tpu_custom_call" | custom-call | tf_op jit(solution)/shard_map/pallas_call | solution.py:133
  67.3 3.3 %collective-permute-start.14 = (f32[2,512]{1,0:T(2,128)S(1)}, f32[2,512]{1,0:T(2,128)S(1)}, u32[]{:S(2)}, u32[]{:S(2)}) collective-permute-start(f32[2,512]{1,0:T(2,128)S(1)} %pad_maximum_fusion.1), channel_id=1, source_target_pairs={{0,2},{1,3},{2,0},{3,1},{4,6},{5,7},{6,4},{7,5},{8,10},{9,11},{10,... | collective-permute-start | bytes 12296 | tf_op jit(solution)/shard_map/ppermute | solution.py:24
  72.4 1.8 collective-permute-done.15
  75.1 7.5 %shard_map.60 = f32[1,8192]{1,0:T(1,128)} custom-call(bf16[512,8192]{1,0:T(8,128)(2,1)} %get-tuple-element.8.k_ref, f32[512,1]{1,0:T(8,128)} %copy.13.r_ref), custom_call_target="tpu_custom_call" | custom-call | tf_op jit(solution)/shard_map/pallas_call | solution.py:117
  86.8 1.9 collective-permute-done.17
  88.7 2.1 collective-permute-done.18
  91.7 3.8 %collective-permute-start.21 = (f32[8192]{0:T(1024)S(1)}, f32[8192]{0:T(1024)S(1)}, u32[]{:S(2)}, u32[]{:S(2)}) collective-permute-start(f32[8192]{0:T(1024)S(1)} %add_add_fusion.1), channel_id=1, source_target_pairs={{0,64},{32,96},{64,0},{96,32},{1,65},{33,97},{65,1},{97,33},{2,66}... | collective-permute-start | bytes 98312 | tf_op jit(solution)/shard_map/ppermute | solution.py:24
  97.7 1.7 collective-permute-done.22
  100.0 7.7 %shard_map.61 = f32[512,1]{1,0:T(8,128)} custom-call(bf16[512,8192]{1,0:T(8,128)(2,1)} %get-tuple-element.8.k_ref, f32[1,8192]{1,0:T(1,128)} %bitcast.127), custom_call_target="tpu_custom_call" | custom-call | tf_op jit(solution)/shard_map/pallas_call | solution.py:133
  108.8 2.7 %collective-permute-start.24 = (f32[512]{0:T(512)S(1)}, f32[512]{0:T(512)S(1)}, u32[]{:S(2)}, u32[]{:S(2)}) collective-permute-start(f32[512]{0:T(512)S(1)} %reduce.3), channel_id=1, source_target_pairs={{0,2},{1,3},{2,0},{3,1},{4,6},{5,7},{6,4},{7,5},{8,10},{9,11},{10,... | collective-permute-start | bytes 6152 | tf_op jit(solution)/shard_map/ppermute | solution.py:24
  111.5 1.5 collective-permute-start.25
  116.0 7.6 %shard_map.62 = f32[1,8192]{1,0:T(1,128)} custom-call(bf16[512,8192]{1,0:T(8,128)(2,1)} %get-tuple-element.8.k_ref, f32[512,1]{1,0:T(8,128)} %copy.14.r_ref), custom_call_target="tpu_custom_call" | custom-call | tf_op jit(solution)/shard_map/pallas_call | solution.py:117
  125.7 2.0 collective-permute-start.27
  129.9 3.2 %collective-permute-done.28 = f32[8192]{0:T(1024)S(1)} collective-permute-done((f32[8192]{0:T(1024)S(1)}, f32[8192]{0:T(1024)S(1)}, u32[]{:S(2)}, u32[]{:S(2)}) %collective-permute-start.28) | collective-permute-done | bytes 32800 | tf_op jit(solution)/shard_map/ppermute | solution.py:24
  133.9 2.7 %collective-permute-start.31 = (f32[8192]{0:T(1024)S(1)}, f32[8192]{0:T(1024)S(1)}, u32[]{:S(2)}, u32[]{:S(2)}) collective-permute-start(f32[8192]{0:T(1024)S(1)} %add_add_fusion), channel_id=1, source_target_pairs={{0,64},{32,96},{64,0},{96,32},{1,65},{33,97},{65,1},{97,33},{2,66}... | collective-permute-start | bytes 98312 | tf_op jit(solution)/shard_map/ppermute | solution.py:24
  141.1 7.8 %shard_map.63 = f32[512,1]{1,0:T(8,128)} custom-call(bf16[512,8192]{1,0:T(8,128)(2,1)} %get-tuple-element.8.k_ref, f32[1,8192]{1,0:T(1,128)} %bitcast.119), custom_call_target="tpu_custom_call" | custom-call | tf_op jit(solution)/shard_map/pallas_call | solution.py:133
  150.0 1.5 collective-permute-start.33
  151.5 2.7 %collective-permute-start.34 = (f32[512]{0:T(512)S(1)}, f32[512]{0:T(512)S(1)}, u32[]{:S(2)}, u32[]{:S(2)}) collective-permute-start(f32[512]{0:T(512)S(1)} %reduce.4), channel_id=1, source_target_pairs={{0,2},{1,3},{2,0},{3,1},{4,6},{5,7},{6,4},{7,5},{8,10},{9,11},{10,... | collective-permute-start | bytes 6152 | tf_op jit(solution)/shard_map/ppermute | solution.py:24
  154.9 1.7 collective-permute-done.34
  157.8 10.8 %multiply_convert_fusion = (bf16[512,8192]{1,0:T(8,128)(2,1)S(1)}, bf16[512,8192]{1,0:T(8,128)(2,1)}) fusion(f32[512,8192]{1,0:T(8,128)} %get-tuple-element.7, f32[512]{0:T(512)S(1)} %bitcast.138, f32[512]{0:T(512)S(1)} %add_divide_fusion.3, f32[8192]{0:T(1024)S(1)} %copy-done.6), kind=kLoop, calls=%fused_computation.1 | loop fusion | flops 37748736 | bytes 33591296 | tf_op jit(solution)/shard_map/convert_element_type | solution.py:172
  168.6 2.5 fusion.2
  171.5 3.2 %fusion.36 = (bf16[512,256]{1,0:T(8,128)(2,1)}, f32[512,256]{1,0:T(8,128)}) fusion(bf16[512,8192]{1,0:T(8,128)(2,1)S(1)} %get-tuple-element.13, bf16[256,8192]{1,0:T(8,128)(2,1)S(1)} %copy-done.3), kind=kOutput, calls=%fused_computation.92 | convolution fusion | flops 2147614720 | bytes 13369344 | tf_op jit(solution)/shard_map/dot_general | solution.py:177
  174.7 2.7 %collective-permute-start.44 = (bf16[512,256]{1,0:T(8,128)(2,1)}, bf16[512,256]{1,0:T(8,128)(2,1)}, u32[]{:S(2)}, u32[]{:S(2)}) collective-permute-start(bf16[512,256]{1,0:T(8,128)(2,1)} %get-tuple-element.32), channel_id=1, source_target_pairs={{0,2},{1,3},{2,0},{3,1},{4,6},{5,7},{6,4},{7,5},{8,10},{9,11},{10,... | collective-permute-start | bytes 786440 | tf_op jit(solution)/shard_map/ppermute | solution.py:24
  178.9 11.6 %collective-permute-done.43 = bf16[512,256]{1,0:T(8,128)(2,1)S(1)} collective-permute-done((bf16[512,256]{1,0:T(8,128)(2,1)}, bf16[512,256]{1,0:T(8,128)(2,1)S(1)}, u32[]{:S(2)}, u32[]{:S(2)}) %collective-permute-start.43) | collective-permute-done | bytes 262176 | tf_op jit(solution)/shard_map/ppermute | solution.py:24
  192.6 1.8 fusion.10
  194.5 3.2 %bitcast_add_fusion = f32[4,4,8,8192]{3,2,1,0:T(8,128)S(1)} fusion(bf16[4,4,8,8192]{3,2,1,0:T(8,128)(2,1)} %collective-permute-done.36, f32[4,4,2,8,8192]{4,3,2,1,0:T(8,128)} %copy-done.1, s32[]{:T(128)S(6)} %select_n.148), kind=kLoop, calls=%fused_computation.10 | loop fusion | flops 2097152 | bytes 10485764 | tf_op jit(solution)/shard_map/add | solution.py:49
  197.8 1.9 copy-done.4
  203.5 1.9 collective-permute-start.47
  206.8 19.8 %collective-permute-done.47 = bf16[4,8,512]{2,1,0:T(8,128)(2,1)S(1)} collective-permute-done((bf16[4,8,512]{2,1,0:T(8,128)(2,1)S(1)}, bf16[4,8,512]{2,1,0:T(8,128)(2,1)S(1)}, u32[]{:S(2)}, u32[]{:S(2)}) %collective-permute-start.47) | collective-permute-done | bytes 32800 | tf_op jit(solution)/shard_map/ppermute | solution.py:24
  226.6 1.5 collective-permute-done.48
  228.1 3.6 %collective-permute-done.49 = bf16[4,8,512]{2,1,0:T(8,128)(2,1)S(1)} collective-permute-done((bf16[4,8,512]{2,1,0:T(8,128)(2,1)S(1)}, bf16[4,8,512]{2,1,0:T(8,128)(2,1)S(1)}, u32[]{:S(2)}, u32[]{:S(2)}) %collective-permute-start.49) | collective-permute-done | bytes 32800 | tf_op jit(solution)/shard_map/ppermute | solution.py:24
  233.1 2.7 %collective-permute-start.51 = (bf16[8,512]{1,0:T(8,128)(2,1)S(1)}, bf16[8,512]{1,0:T(8,128)(2,1)S(1)}, u32[]{:S(2)}, u32[]{:S(2)}) collective-permute-start(bf16[8,512]{1,0:T(8,128)(2,1)S(1)} %get-tuple-element.29), channel_id=1, source_target_pairs={{0,64},{32,96},{64,0},{96,32},{1,65},{33,97},{65,1},{97,33},{2,66}... | collective-permute-start | bytes 24584 | tf_op jit(solution)/shard_map/ppermute | solution.py:24
  236.0 1.6 fusion.6
  237.6 2.0 collective-permute-start.40
  240.4 1.9 collective-permute-start.42
  243.9 2.2 collective-permute-done.41
  (129 shorter events, 59.6 us)
Async XLA Ops:
  3.1 12.6 %collective-permute-start = (f32[128,256]{1,0:T(8,128)S(1)}, f32[128,256]{1,0:T(8,128)S(1)}, u32[]{:S(2)}, u32[]{:S(2)}) collective-permute-start(f32[128,256]{1,0:T(8,128)S(1)} %get-tuple-element.21), channel_id=1, source_target_pairs={{0,1},{1,2},{2,3},{3,0},{4,5},{5,6},{6,7},{7,4},{8,9},{9,10},{10,1... | collective-permute-start | bytes 393224 | tf_op jit(solution)/shard_map/ppermute | solution.py:24
  5.1 10.6 %collective-permute-start.1 = (f32[128,256]{1,0:T(8,128)S(1)}, f32[128,256]{1,0:T(8,128)S(1)}, u32[]{:S(2)}, u32[]{:S(2)}) collective-permute-start(f32[128,256]{1,0:T(8,128)S(1)} %get-tuple-element.23), channel_id=1, source_target_pairs={{0,2},{1,3},{2,0},{3,1},{4,6},{5,7},{6,4},{7,5},{8,10},{9,11},{10,... | collective-permute-start | bytes 393224 | tf_op jit(solution)/shard_map/ppermute | solution.py:24
  8.7 7.0 %collective-permute-start.2 = (f32[128,256]{1,0:T(8,128)S(1)}, f32[128,256]{1,0:T(8,128)S(1)}, u32[]{:S(2)}, u32[]{:S(2)}) collective-permute-start(f32[128,256]{1,0:T(8,128)S(1)} %get-tuple-element.22), channel_id=1, source_target_pairs={{0,3},{1,0},{2,1},{3,2},{4,7},{5,4},{6,5},{7,6},{8,11},{9,8},{10,9... | collective-permute-start | bytes 393224 | tf_op jit(solution)/shard_map/ppermute | solution.py:24
  15.8 8.7 %collective-permute-start.3 = (f32[128,256]{1,0:T(8,128)S(1)}, f32[128,256]{1,0:T(8,128)S(1)}, u32[]{:S(2)}, u32[]{:S(2)}) collective-permute-start(f32[128,256]{1,0:T(8,128)S(1)} %fusion.20), channel_id=1, source_target_pairs={{0,1},{1,2},{2,3},{3,0},{4,5},{5,6},{6,7},{7,4},{8,9},{9,10},{10,1... | collective-permute-start | bytes 393224 | tf_op jit(solution)/shard_map/ppermute | solution.py:24
  16.9 7.6 %collective-permute-start.4 = (f32[128,256]{1,0:T(8,128)S(1)}, f32[128,256]{1,0:T(8,128)S(1)}, u32[]{:S(2)}, u32[]{:S(2)}) collective-permute-start(f32[128,256]{1,0:T(8,128)S(1)} %fusion.20), channel_id=1, source_target_pairs={{0,2},{1,3},{2,0},{3,1},{4,6},{5,7},{6,4},{7,5},{8,10},{9,11},{10,... | collective-permute-start | bytes 393224 | tf_op jit(solution)/shard_map/ppermute | solution.py:24
  18.4 6.4 %collective-permute-start.5 = (f32[128,256]{1,0:T(8,128)S(1)}, f32[128,256]{1,0:T(8,128)S(1)}, u32[]{:S(2)}, u32[]{:S(2)}) collective-permute-start(f32[128,256]{1,0:T(8,128)S(1)} %fusion.20), channel_id=1, source_target_pairs={{0,3},{1,0},{2,1},{3,2},{4,7},{5,4},{6,5},{7,6},{8,11},{9,8},{10,9... | collective-permute-start | bytes 393224 | tf_op jit(solution)/shard_map/ppermute | solution.py:24
  40.5 4.0 %collective-permute-start.7 = (f32[8192]{0:T(1024)S(1)}, f32[8192]{0:T(1024)S(1)}, u32[]{:S(2)}, u32[]{:S(2)}) collective-permute-start(f32[8192]{0:T(1024)S(1)} %add.349), channel_id=1, source_target_pairs={{0,8},{8,16},{16,24},{24,0},{1,9},{9,17},{17,25},{25,1},{2,10},{10... | collective-permute-start | bytes 98312 | tf_op jit(solution)/shard_map/ppermute | solution.py:24
  41.0 5.4 %collective-permute-start.8 = (f32[8192]{0:T(1024)S(1)}, f32[8192]{0:T(1024)S(1)}, u32[]{:S(2)}, u32[]{:S(2)}) collective-permute-start(f32[8192]{0:T(1024)S(1)} %add.349), channel_id=1, source_target_pairs={{0,16},{8,24},{16,0},{24,8},{1,17},{9,25},{17,1},{25,9},{2,18},{10... | collective-permute-start | bytes 98312 | tf_op jit(solution)/shard_map/ppermute | solution.py:24
  43.4 5.1 %collective-permute-start.9 = (f32[8192]{0:T(1024)S(1)}, f32[8192]{0:T(1024)S(1)}, u32[]{:S(2)}, u32[]{:S(2)}) collective-permute-start(f32[8192]{0:T(1024)S(1)} %add.349), channel_id=1, source_target_pairs={{0,24},{8,0},{16,8},{24,16},{1,25},{9,1},{17,9},{25,17},{2,26},{10... | collective-permute-start | bytes 98312 | tf_op jit(solution)/shard_map/ppermute | solution.py:24
  48.5 7.0 %collective-permute-start.10 = (f32[8192]{0:T(1024)S(1)}, f32[8192]{0:T(1024)S(1)}, u32[]{:S(2)}, u32[]{:S(2)}) collective-permute-start(f32[8192]{0:T(1024)S(1)} %add_add_fusion.2), channel_id=1, source_target_pairs={{0,32},{32,64},{64,96},{96,0},{1,33},{33,65},{65,97},{97,1},{2,34}... | collective-permute-start | bytes 98312 | tf_op jit(solution)/shard_map/ppermute | solution.py:24
  50.2 5.4 %collective-permute-start.11 = (f32[8192]{0:T(1024)S(1)}, f32[8192]{0:T(1024)S(1)}, u32[]{:S(2)}, u32[]{:S(2)}) collective-permute-start(f32[8192]{0:T(1024)S(1)} %add_add_fusion.2), channel_id=1, source_target_pairs={{0,64},{32,96},{64,0},{96,32},{1,65},{33,97},{65,1},{97,33},{2,66}... | collective-permute-start | bytes 98312 | tf_op jit(solution)/shard_map/ppermute | solution.py:24
  53.1 3.9 %collective-permute-start.12 = (f32[8192]{0:T(1024)S(1)}, f32[8192]{0:T(1024)S(1)}, u32[]{:S(2)}, u32[]{:S(2)}) collective-permute-start(f32[8192]{0:T(1024)S(1)} %add_add_fusion.2), channel_id=1, source_target_pairs={{0,96},{32,0},{64,32},{96,64},{1,97},{33,1},{65,33},{97,65},{2,98}... | collective-permute-start | bytes 98312 | tf_op jit(solution)/shard_map/ppermute | solution.py:24
  66.4 4.9 %collective-permute-start.13 = (f32[2,512]{1,0:T(2,128)S(1)}, f32[2,512]{1,0:T(2,128)S(1)}, u32[]{:S(2)}, u32[]{:S(2)}) collective-permute-start(f32[2,512]{1,0:T(2,128)S(1)} %pad_maximum_fusion.1), channel_id=1, source_target_pairs={{0,1},{1,2},{2,3},{3,0},{4,5},{5,6},{6,7},{7,4},{8,9},{9,10},{10,1... | collective-permute-start | bytes 12296 | tf_op jit(solution)/shard_map/ppermute | solution.py:24
  67.3 5.1 %collective-permute-start.14 = (f32[2,512]{1,0:T(2,128)S(1)}, f32[2,512]{1,0:T(2,128)S(1)}, u32[]{:S(2)}, u32[]{:S(2)}) collective-permute-start(f32[2,512]{1,0:T(2,128)S(1)} %pad_maximum_fusion.1), channel_id=1, source_target_pairs={{0,2},{1,3},{2,0},{3,1},{4,6},{5,7},{6,4},{7,5},{8,10},{9,11},{10,... | collective-permute-start | bytes 12296 | tf_op jit(solution)/shard_map/ppermute | solution.py:24
  70.6 3.6 %collective-permute-start.15 = (f32[2,512]{1,0:T(2,128)S(1)}, f32[2,512]{1,0:T(2,128)S(1)}, u32[]{:S(2)}, u32[]{:S(2)}) collective-permute-start(f32[2,512]{1,0:T(2,128)S(1)} %pad_maximum_fusion.1), channel_id=1, source_target_pairs={{0,3},{1,0},{2,1},{3,2},{4,7},{5,4},{6,5},{7,6},{8,11},{9,8},{10,9... | collective-permute-start | bytes 12296 | tf_op jit(solution)/shard_map/ppermute | solution.py:24
  84.8 3.9 %collective-permute-start.17 = (f32[8192]{0:T(1024)S(1)}, f32[8192]{0:T(1024)S(1)}, u32[]{:S(2)}, u32[]{:S(2)}) collective-permute-start(f32[8192]{0:T(1024)S(1)} %add.359), channel_id=1, source_target_pairs={{0,8},{8,16},{16,24},{24,0},{1,9},{9,17},{17,25},{25,1},{2,10},{10... | collective-permute-start | bytes 98312 | tf_op jit(solution)/shard_map/ppermute | solution.py:24
  85.4 5.4 %collective-permute-start.18 = (f32[8192]{0:T(1024)S(1)}, f32[8192]{0:T(1024)S(1)}, u32[]{:S(2)}, u32[]{:S(2)}) collective-permute-start(f32[8192]{0:T(1024)S(1)} %add.359), channel_id=1, source_target_pairs={{0,16},{8,24},{16,0},{24,8},{1,17},{9,25},{17,1},{25,9},{2,18},{10... | collective-permute-start | bytes 98312 | tf_op jit(solution)/shard_map/ppermute | solution.py:24
  86.3 5.1 %collective-permute-start.19 = (f32[8192]{0:T(1024)S(1)}, f32[8192]{0:T(1024)S(1)}, u32[]{:S(2)}, u32[]{:S(2)}) collective-permute-start(f32[8192]{0:T(1024)S(1)} %add.359), channel_id=1, source_target_pairs={{0,24},{8,0},{16,8},{24,16},{1,25},{9,1},{17,9},{25,17},{2,26},{10... | collective-permute-start | bytes 98312 | tf_op jit(solution)/shard_map/ppermute | solution.py:24
  91.4 5.2 %collective-permute-start.20 = (f32[8192]{0:T(1024)S(1)}, f32[8192]{0:T(1024)S(1)}, u32[]{:S(2)}, u32[]{:S(2)}) collective-permute-start(f32[8192]{0:T(1024)S(1)} %add_add_fusion.1), channel_id=1, source_target_pairs={{0,32},{32,64},{64,96},{96,0},{1,33},{33,65},{65,97},{97,1},{2,34}... | collective-permute-start | bytes 98312 | tf_op jit(solution)/shard_map/ppermute | solution.py:24
  91.7 6.1 %collective-permute-start.21 = (f32[8192]{0:T(1024)S(1)}, f32[8192]{0:T(1024)S(1)}, u32[]{:S(2)}, u32[]{:S(2)}) collective-permute-start(f32[8192]{0:T(1024)S(1)} %add_add_fusion.1), channel_id=1, source_target_pairs={{0,64},{32,96},{64,0},{96,32},{1,65},{33,97},{65,1},{97,33},{2,66}... | collective-permute-start | bytes 98312 | tf_op jit(solution)/shard_map/ppermute | solution.py:24
  95.5 3.9 %collective-permute-start.22 = (f32[8192]{0:T(1024)S(1)}, f32[8192]{0:T(1024)S(1)}, u32[]{:S(2)}, u32[]{:S(2)}) collective-permute-start(f32[8192]{0:T(1024)S(1)} %add_add_fusion.1), channel_id=1, source_target_pairs={{0,96},{32,0},{64,32},{96,64},{1,97},{33,1},{65,33},{97,65},{2,98}... | collective-permute-start | bytes 98312 | tf_op jit(solution)/shard_map/ppermute | solution.py:24
  108.8 4.9 %collective-permute-start.23 = (f32[512]{0:T(512)S(1)}, f32[512]{0:T(512)S(1)}, u32[]{:S(2)}, u32[]{:S(2)}) collective-permute-start(f32[512]{0:T(512)S(1)} %reduce.3), channel_id=1, source_target_pairs={{0,1},{1,2},{2,3},{3,0},{4,5},{5,6},{6,7},{7,4},{8,9},{9,10},{10,1... | collective-permute-start | bytes 6152 | tf_op jit(solution)/shard_map/ppermute | solution.py:24
  108.8 5.2 %collective-permute-start.24 = (f32[512]{0:T(512)S(1)}, f32[512]{0:T(512)S(1)}, u32[]{:S(2)}, u32[]{:S(2)}) collective-permute-start(f32[512]{0:T(512)S(1)} %reduce.3), channel_id=1, source_target_pairs={{0,2},{1,3},{2,0},{3,1},{4,6},{5,7},{6,4},{7,5},{8,10},{9,11},{10,... | collective-permute-start | bytes 6152 | tf_op jit(solution)/shard_map/ppermute | solution.py:24
  125.7 4.2 %collective-permute-start.27 = (f32[8192]{0:T(1024)S(1)}, f32[8192]{0:T(1024)S(1)}, u32[]{:S(2)}, u32[]{:S(2)}) collective-permute-start(f32[8192]{0:T(1024)S(1)} %add.369), channel_id=1, source_target_pairs={{0,8},{8,16},{16,24},{24,0},{1,9},{9,17},{17,25},{25,1},{2,10},{10... | collective-permute-start | bytes 98312 | tf_op jit(solution)/shard_map/ppermute | solution.py:24
  127.7 5.4 %collective-permute-start.28 = (f32[8192]{0:T(1024)S(1)}, f32[8192]{0:T(1024)S(1)}, u32[]{:S(2)}, u32[]{:S(2)}) collective-permute-start(f32[8192]{0:T(1024)S(1)} %add.369), channel_id=1, source_target_pairs={{0,16},{8,24},{16,0},{24,8},{1,17},{9,25},{17,1},{25,9},{2,18},{10... | collective-permute-start | bytes 98312 | tf_op jit(solution)/shard_map/ppermute | solution.py:24
  128.6 5.1 %collective-permute-start.29 = (f32[8192]{0:T(1024)S(1)}, f32[8192]{0:T(1024)S(1)}, u32[]{:S(2)}, u32[]{:S(2)}) collective-permute-start(f32[8192]{0:T(1024)S(1)} %add.369), channel_id=1, source_target_pairs={{0,24},{8,0},{16,8},{24,16},{1,25},{9,1},{17,9},{25,17},{2,26},{10... | collective-permute-start | bytes 98312 | tf_op jit(solution)/shard_map/ppermute | solution.py:24
  133.7 5.2 %collective-permute-start.30 = (f32[8192]{0:T(1024)S(1)}, f32[8192]{0:T(1024)S(1)}, u32[]{:S(2)}, u32[]{:S(2)}) collective-permute-start(f32[8192]{0:T(1024)S(1)} %add_add_fusion), channel_id=1, source_target_pairs={{0,32},{32,64},{64,96},{96,0},{1,33},{33,65},{65,97},{97,1},{2,34}... | collective-permute-start | bytes 98312 | tf_op jit(solution)/shard_map/ppermute | solution.py:24
  133.9 5.4 %collective-permute-start.31 = (f32[8192]{0:T(1024)S(1)}, f32[8192]{0:T(1024)S(1)}, u32[]{:S(2)}, u32[]{:S(2)}) collective-permute-start(f32[8192]{0:T(1024)S(1)} %add_add_fusion), channel_id=1, source_target_pairs={{0,64},{32,96},{64,0},{96,32},{1,65},{33,97},{65,1},{97,33},{2,66}... | collective-permute-start | bytes 98312 | tf_op jit(solution)/shard_map/ppermute | solution.py:24
  136.6 3.9 %collective-permute-start.32 = (f32[8192]{0:T(1024)S(1)}, f32[8192]{0:T(1024)S(1)}, u32[]{:S(2)}, u32[]{:S(2)}) collective-permute-start(f32[8192]{0:T(1024)S(1)} %add_add_fusion), channel_id=1, source_target_pairs={{0,96},{32,0},{64,32},{96,64},{1,97},{33,1},{65,33},{97,65},{2,98}... | collective-permute-start | bytes 98312 | tf_op jit(solution)/shard_map/ppermute | solution.py:24
  150.0 4.9 %collective-permute-start.33 = (f32[512]{0:T(512)S(1)}, f32[512]{0:T(512)S(1)}, u32[]{:S(2)}, u32[]{:S(2)}) collective-permute-start(f32[512]{0:T(512)S(1)} %reduce.4), channel_id=1, source_target_pairs={{0,1},{1,2},{2,3},{3,0},{4,5},{5,6},{6,7},{7,4},{8,9},{9,10},{10,1... | collective-permute-start | bytes 6152 | tf_op jit(solution)/shard_map/ppermute | solution.py:24
  151.5 5.1 %collective-permute-start.34 = (f32[512]{0:T(512)S(1)}, f32[512]{0:T(512)S(1)}, u32[]{:S(2)}, u32[]{:S(2)}) collective-permute-start(f32[512]{0:T(512)S(1)} %reduce.4), channel_id=1, source_target_pairs={{0,2},{1,3},{2,0},{3,1},{4,6},{5,7},{6,4},{7,5},{8,10},{9,11},{10,... | collective-permute-start | bytes 6152 | tf_op jit(solution)/shard_map/ppermute | solution.py:24
  171.4 23.2 %collective-permute-start.36 = (bf16[4,4,8,8192]{3,2,1,0:T(8,128)(2,1)S(1)}, bf16[4,4,8,8192]{3,2,1,0:T(8,128)(2,1)}, u32[]{:S(2)}, u32[]{:S(2)}) collective-permute-start(bf16[4,4,8,8192]{3,2,1,0:T(8,128)(2,1)S(1)} %fusion.4), channel_id=1, source_target_pairs={{0,4},{4,0},{1,5},{5,1},{2,6},{6,2},{3,7},{7,3},{8,12},{12,8},{9,1... | collective-permute-start | bytes 6291464 | tf_op jit(solution)/shard_map/ppermute | solution.py:24
  174.7 15.7 %collective-permute-start.43 = (bf16[512,256]{1,0:T(8,128)(2,1)}, bf16[512,256]{1,0:T(8,128)(2,1)S(1)}, u32[]{:S(2)}, u32[]{:S(2)}) collective-permute-start(bf16[512,256]{1,0:T(8,128)(2,1)} %get-tuple-element.32), channel_id=1, source_target_pairs={{0,1},{1,2},{2,3},{3,0},{4,5},{5,6},{6,7},{7,4},{8,9},{9,10},{10,1... | collective-permute-start | bytes 786440 | tf_op jit(solution)/shard_map/ppermute | solution.py:24
  174.7 15.7 %collective-permute-start.44 = (bf16[512,256]{1,0:T(8,128)(2,1)}, bf16[512,256]{1,0:T(8,128)(2,1)}, u32[]{:S(2)}, u32[]{:S(2)}) collective-permute-start(bf16[512,256]{1,0:T(8,128)(2,1)} %get-tuple-element.32), channel_id=1, source_target_pairs={{0,2},{1,3},{2,0},{3,1},{4,6},{5,7},{6,4},{7,5},{8,10},{9,11},{10,... | collective-permute-start | bytes 786440 | tf_op jit(solution)/shard_map/ppermute | solution.py:24
  177.4 13.7 %collective-permute-start.45 = (bf16[512,256]{1,0:T(8,128)(2,1)}, bf16[512,256]{1,0:T(8,128)(2,1)}, u32[]{:S(2)}, u32[]{:S(2)}) collective-permute-start(bf16[512,256]{1,0:T(8,128)(2,1)} %get-tuple-element.32), channel_id=1, source_target_pairs={{0,3},{1,0},{2,1},{3,2},{4,7},{5,4},{6,5},{7,6},{8,11},{9,8},{10,9... | collective-permute-start | bytes 786440 | tf_op jit(solution)/shard_map/ppermute | solution.py:24
  194.4 8.4 %collective-permute-start.46 = (bf16[4,4,8,512]{3,2,0,1:T(8,128)(2,1)S(1)}, bf16[4,4,8,512]{3,2,0,1:T(8,128)(2,1)S(1)}, u32[]{:S(2)}, u32[]{:S(2)}) collective-permute-start(bf16[4,4,8,512]{3,2,0,1:T(8,128)(2,1)S(1)} %fusion.18), channel_id=1, source_target_pairs={{0,4},{4,0},{1,5},{5,1},{2,6},{6,2},{3,7},{7,3},{8,12},{12,8},{9,1... | collective-permute-start | bytes 393224 | tf_op jit(solution)/shard_map/ppermute | solution.py:24
  199.9 35.9 %collective-permute-start.37 = (bf16[4,8,8192]{2,1,0:T(8,128)(2,1)S(1)}, bf16[4,8,8192]{2,1,0:T(8,128)(2,1)S(1)}, u32[]{:S(2)}, u32[]{:S(2)}) collective-permute-start(bf16[4,8,8192]{2,1,0:T(8,128)(2,1)S(1)} %get-tuple-element.15), channel_id=1, source_target_pairs={{0,8},{8,16},{16,24},{24,0},{1,9},{9,17},{17,25},{25,1},{2,10},{10... | collective-permute-start | bytes 1572872 | tf_op jit(solution)/shard_map/ppermute | solution.py:24
  200.6 35.4 %collective-permute-start.38 = (bf16[4,8,8192]{2,1,0:T(8,128)(2,1)S(1)}, bf16[4,8,8192]{2,1,0:T(8,128)(2,1)S(1)}, u32[]{:S(2)}, u32[]{:S(2)}) collective-permute-start(bf16[4,8,8192]{2,1,0:T(8,128)(2,1)S(1)} %get-tuple-element.17), channel_id=1, source_target_pairs={{0,16},{8,24},{16,0},{24,8},{1,17},{9,25},{17,1},{25,9},{2,18},{10... | collective-permute-start | bytes 1572872 | tf_op jit(solution)/shard_map/ppermute | solution.py:24
  201.5 34.5 %collective-permute-start.39 = (bf16[4,8,8192]{2,1,0:T(8,128)(2,1)S(1)}, bf16[4,8,8192]{2,1,0:T(8,128)(2,1)}, u32[]{:S(2)}, u32[]{:S(2)}) collective-permute-start(bf16[4,8,8192]{2,1,0:T(8,128)(2,1)S(1)} %get-tuple-element.16), channel_id=1, source_target_pairs={{0,24},{8,0},{16,8},{24,16},{1,25},{9,1},{17,9},{25,17},{2,26},{10... | collective-permute-start | bytes 1572872 | tf_op jit(solution)/shard_map/ppermute | solution.py:24
  203.5 23.1 %collective-permute-start.47 = (bf16[4,8,512]{2,1,0:T(8,128)(2,1)S(1)}, bf16[4,8,512]{2,1,0:T(8,128)(2,1)S(1)}, u32[]{:S(2)}, u32[]{:S(2)}) collective-permute-start(bf16[4,8,512]{2,1,0:T(8,128)(2,1)S(1)} %get-tuple-element.24), channel_id=1, source_target_pairs={{0,8},{8,16},{16,24},{24,0},{1,9},{9,17},{17,25},{25,1},{2,10},{10... | collective-permute-start | bytes 98312 | tf_op jit(solution)/shard_map/ppermute | solution.py:24
  205.4 22.7 %collective-permute-start.48 = (bf16[4,8,512]{2,1,0:T(8,128)(2,1)}, bf16[4,8,512]{2,1,0:T(8,128)(2,1)S(1)}, u32[]{:S(2)}, u32[]{:S(2)}) collective-permute-start(bf16[4,8,512]{2,1,0:T(8,128)(2,1)} %get-tuple-element.26), channel_id=1, source_target_pairs={{0,16},{8,24},{16,0},{24,8},{1,17},{9,25},{17,1},{25,9},{2,18},{10... | collective-permute-start | bytes 98312 | tf_op jit(solution)/shard_map/ppermute | solution.py:24
  226.6 5.1 %collective-permute-start.49 = (bf16[4,8,512]{2,1,0:T(8,128)(2,1)S(1)}, bf16[4,8,512]{2,1,0:T(8,128)(2,1)S(1)}, u32[]{:S(2)}, u32[]{:S(2)}) collective-permute-start(bf16[4,8,512]{2,1,0:T(8,128)(2,1)S(1)} %get-tuple-element.25), channel_id=1, source_target_pairs={{0,24},{8,0},{16,8},{24,16},{1,25},{9,1},{17,9},{25,17},{2,26},{10... | collective-permute-start | bytes 98312 | tf_op jit(solution)/shard_map/ppermute | solution.py:24
  231.8 8.7 %collective-permute-start.50 = (bf16[8,512]{1,0:T(8,128)(2,1)S(1)}, bf16[8,512]{1,0:T(8,128)(2,1)S(1)}, u32[]{:S(2)}, u32[]{:S(2)}) collective-permute-start(bf16[8,512]{1,0:T(8,128)(2,1)S(1)} %get-tuple-element.27), channel_id=1, source_target_pairs={{0,32},{32,64},{64,96},{96,0},{1,33},{33,65},{65,97},{97,1},{2,34}... | collective-permute-start | bytes 24584 | tf_op jit(solution)/shard_map/ppermute | solution.py:24
  233.1 9.3 %collective-permute-start.51 = (bf16[8,512]{1,0:T(8,128)(2,1)S(1)}, bf16[8,512]{1,0:T(8,128)(2,1)S(1)}, u32[]{:S(2)}, u32[]{:S(2)}) collective-permute-start(bf16[8,512]{1,0:T(8,128)(2,1)S(1)} %get-tuple-element.29), channel_id=1, source_target_pairs={{0,64},{32,96},{64,0},{96,32},{1,65},{33,97},{65,1},{97,33},{2,66}... | collective-permute-start | bytes 24584 | tf_op jit(solution)/shard_map/ppermute | solution.py:24
  235.8 6.5 %collective-permute-start.52 = (bf16[8,512]{1,0:T(8,128)(2,1)S(1)}, bf16[8,512]{1,0:T(8,128)(2,1)S(1)}, u32[]{:S(2)}, u32[]{:S(2)}) collective-permute-start(bf16[8,512]{1,0:T(8,128)(2,1)S(1)} %get-tuple-element.28), channel_id=1, source_target_pairs={{0,96},{32,0},{64,32},{96,64},{1,97},{33,1},{65,33},{97,65},{2,98}... | collective-permute-start | bytes 24584 | tf_op jit(solution)/shard_map/ppermute | solution.py:24
  237.6 6.2 %collective-permute-start.40 = (bf16[8,8192]{1,0:T(8,128)(2,1)S(1)}, bf16[8,8192]{1,0:T(8,128)(2,1)S(1)}, u32[]{:S(2)}, u32[]{:S(2)}) collective-permute-start(bf16[8,8192]{1,0:T(8,128)(2,1)S(1)} %get-tuple-element.18), channel_id=1, source_target_pairs={{0,32},{32,64},{64,96},{96,0},{1,33},{33,65},{65,97},{97,1},{2,34}... | collective-permute-start | bytes 393224 | tf_op jit(solution)/shard_map/ppermute | solution.py:24
  239.6 6.5 %collective-permute-start.41 = (bf16[8,8192]{1,0:T(8,128)(2,1)S(1)}, bf16[8,8192]{1,0:T(8,128)(2,1)S(1)}, u32[]{:S(2)}, u32[]{:S(2)}) collective-permute-start(bf16[8,8192]{1,0:T(8,128)(2,1)S(1)} %get-tuple-element.20), channel_id=1, source_target_pairs={{0,64},{32,96},{64,0},{96,32},{1,65},{33,97},{65,1},{97,33},{2,66}... | collective-permute-start | bytes 393224 | tf_op jit(solution)/shard_map/ppermute | solution.py:24
  240.4 5.7 %collective-permute-start.42 = (bf16[8,8192]{1,0:T(8,128)(2,1)S(1)}, bf16[8,8192]{1,0:T(8,128)(2,1)S(1)}, u32[]{:S(2)}, u32[]{:S(2)}) collective-permute-start(bf16[8,8192]{1,0:T(8,128)(2,1)S(1)} %get-tuple-element.19), channel_id=1, source_target_pairs={{0,96},{32,0},{64,32},{96,64},{1,97},{33,1},{65,33},{97,65},{2,98}... | collective-permute-start | bytes 393224 | tf_op jit(solution)/shard_map/ppermute | solution.py:24
  (12 other events, 87.0 us)

commit v4 on v3

--- a/solution.py
+++ b/solution.py
@@ -4,6 +4,7 @@
 import jax.numpy as jnp
 from jax import lax
 from jax.experimental import pallas as pl
+from jax.experimental.pallas import tpu as pltpu
 from jax.sharding import Mesh
 from jax.sharding import PartitionSpec as P
 
@@ -74,7 +75,7 @@
     s = jnp.exp(sc * (1.0 / soft_temp))
     s_ref[...] = s
     k = s * s
-    k_ref[...] = k.astype(BF16)
+    k_ref[:, pl.ds(pl.multiple_of(j * s.shape[1], s.shape[1]), s.shape[1])] = k.astype(BF16)
     col_ref[...] = jnp.sum(k, axis=0, keepdims=True)
 
     @pl.when(j == 0)
@@ -93,7 +94,7 @@
         in_specs=[pl.BlockSpec((T, E), lambda j: (0, 0)), pl.BlockSpec((E, bp), lambda j: (0, j))],
         out_specs=[
             pl.BlockSpec((T, bp), lambda j: (0, j)),
-            pl.BlockSpec((T, bp), lambda j: (0, j)),
+            pl.BlockSpec(memory_space=pltpu.VMEM),
             pl.BlockSpec((1, bp), lambda j: (0, j)),
             pl.BlockSpec((T, 1), lambda j: (0, 0)),
         ],
@@ -108,35 +109,52 @@
 
 
 def _col_kernel(k_ref, r_ref, o_ref):
-    k = k_ref[...].astype(F32)
-    o_ref[...] = jnp.sum(k * r_ref[...], axis=0, keepdims=True)
-
-
-def _colpass(soft, r, bp=1024):
-    T, Pn = soft.shape
+    _, Pn = k_ref.shape
+    w = 512
+
+    def body(j, carry):
+        sl = pl.ds(pl.multiple_of(j * w, w), w)
+        k = k_ref[:, sl].astype(F32)
+        o_ref[:, sl] = jnp.sum(k * r_ref[...], axis=0, keepdims=True)
+        return carry
+
+    lax.fori_loop(0, Pn // w, body, 0)
+
+
+_VMEM = pl.BlockSpec(memory_space=pltpu.VMEM)
+
+
+def _colpass(kern_b, r):
+    T, Pn = kern_b.shape
     return pl.pallas_call(
         _col_kernel,
-        grid=(Pn // bp,),
-        in_specs=[pl.BlockSpec((T, bp), lambda j: (0, j)), pl.BlockSpec((T, 1), lambda j: (0, 0))],
-        out_specs=pl.BlockSpec((1, bp), lambda j: (0, j)),
+        in_specs=[_VMEM, _VMEM],
+        out_specs=_VMEM,
         out_shape=jax.ShapeDtypeStruct((1, Pn), F32),
-    )(soft, r.reshape(T, 1))[0]
+    )(kern_b, r.reshape(T, 1))[0]
 
 
 def _row_kernel(k_ref, c_ref, o_ref):
-    k = k_ref[...].astype(F32)
-    o_ref[...] = jnp.sum(k * c_ref[...], axis=1, keepdims=True)
-
-
-def _rowpass(soft, c, bt=64):
-    T, Pn = soft.shape
+    T, _ = k_ref.shape
+    h = 32
+
+    def body(i, carry):
+        sl = pl.ds(pl.multiple_of(i * h, h), h)
+        k = k_ref[sl, :].astype(F32)
+        o_ref[sl, :] = jnp.sum(k * c_ref[...], axis=1, keepdims=True)
+        return carry
+
+    lax.fori_loop(0, T // h, body, 0)
+
+
+def _rowpass(kern_b, c):
+    T, Pn = kern_b.shape
     return pl.pallas_call(
         _row_kernel,
-        grid=(T // bt,),
-        in_specs=[pl.BlockSpec((bt, Pn), lambda i: (i, 0)), pl.BlockSpec((1, Pn), lambda i: (0, 0))],
-        out_specs=pl.BlockSpec((bt, 1), lambda i: (i, 0)),
+        in_specs=[_VMEM, _VMEM],
+        out_specs=_VMEM,
         out_shape=jax.ShapeDtypeStruct((T, 1), F32),
-    )(soft, c.reshape(1, Pn))[:, 0]
+    )(kern_b, c.reshape(1, Pn))[:, 0]
 
 
 def on_device(features, head_weight, prototypes):

time: 249 us -> 248 us (level)
  no operation moved by 1% of the time
where the time goes in v4:
time: 248 us; the launch traced here: 247 us
  waiting for transfers between devices  81.5 us (33%)
  starting transfers between devices  64.9 us (26%)
  Pallas kernels  50.1 us (20%)
  other arithmetic  34.2 us (14%)
  matrix products  8.88 us (4%)
  local copies, waits for them, and re-layouts  6.61 us (3%)
    ppermute x53, waiting for transfers between devices, _shift(): return lax.ppermute(v, ax, [(i, (i + k) % n) for i in range(n)])  81.5 us
    ppermute x53, starting transfers between devices, _shift(): return lax.ppermute(v, ax, [(i, (i + k) % n) for i in range(n)])  64.9 us
    pallas_call x3, Pallas kernels, _rowpass(): pl.pallas_call(_row_kernel, in_specs=[_VMEM, _VMEM], out_specs=_VMEM, out...  22.7 us
    pallas_call x2, Pallas kernels, _colpass(): pl.pallas_call(_col_kernel, in_specs=[_VMEM, _VMEM], out_specs=_VMEM, out...  13.9 us
    pallas_call x1, Pallas kernels, _scores(): pl.pallas_call(_score_kernel, grid=(Pn // bp,), in_specs=[pl.BlockSpec((T...  13.5 us
    convert_element_type x1, other arithmetic, on_device(): dscore = ((probs - plan) * factor).astype(BF16)  10.8 us
    add x7, other arithmetic, _rs(): acc = acc + _shift(blk, ax, k).astype(a.dtype)  6.29 us
  transfers between devices with their start and end apart: 53, of which 39 were waited for; matrix products, arithmetic and copies ran while one was open for 8% of the time, Pallas kernels for 0%

profile of v4, /device:TPU:6, one launch (start us, length us, event | category | flops | bytes accessed | tf_op | source)
XLA Modules:
  0.0 247.2 jit_solution(1363028737196998582)
XLA Ops:
  3.1 2.0 collective-permute-start
  5.1 3.6 %collective-permute-start.1 = (f32[128,256]{1,0:T(8,128)S(1)}, f32[128,256]{1,0:T(8,128)S(1)}, u32[]{:S(2)}, u32[]{:S(2)}) collective-permute-start(f32[128,256]{1,0:T(8,128)S(1)} %get-tuple-element.23), channel_id=1, source_target_pairs={{0,2},{1,3},{2,0},{3,1},{4,6},{5,7},{6,4},{7,5},{8,10},{9,11},{10,... | collective-permute-start | bytes 393224 | tf_op jit(solution)/shard_map/ppermute | solution.py:25
  9.7 3.1 %fusion = f32[8192]{0:T(1024)S(1)} fusion(bf16[256,8192]{1,0:T(8,128)(2,1)} %param.5), kind=kLoop, calls=%fused_computation.6 | loop fusion | flops 6283264 | bytes 4227072 | tf_op jit(solution)/shard_map/reduce_sum | solution.py:170
  12.8 2.9 %fusion.1.n_ref = bf16[256,8192]{1,0:T(8,128)(2,1)} fusion(bf16[256,8192]{1,0:T(8,128)(2,1)S(1)} %copy-done.2, f32[8192]{0:T(1024)S(1)} %add_sqrt_fusion), kind=kLoop, calls=%fused_computation.7 | loop fusion | flops 6291456 | bytes 8421376 | tf_op jit(solution)/shard_map/convert_element_type | solution.py:170
  16.9 1.6 collective-permute-start.4
  19.7 4.7 %collective-permute-done.3 = f32[128,256]{1,0:T(8,128)S(1)} collective-permute-done((f32[128,256]{1,0:T(8,128)S(1)}, f32[128,256]{1,0:T(8,128)S(1)}, u32[]{:S(2)}, u32[]{:S(2)}) %collective-permute-start.3) | collective-permute-done | bytes 131104 | tf_op jit(solution)/shard_map/ppermute | solution.py:25
  26.5 13.5 %shard_map.58 = (f32[512,8192]{1,0:T(8,128)}, bf16[512,8192]{1,0:T(8,128)(2,1)}, f32[1,8192]{1,0:T(1,128)}, f32[512,1]{1,0:T(8,128)}) custom-call(bf16[512,256]{1,0:T(8,128)(2,1)} %get-tuple-element.11.u_ref, bf16[256,8192]{1,0:T(8,128)(2,1)} %fusion.1.n_ref), custom_call_target="tpu_custom_call" | custom-call | tf_op jit(solution)/shard_map/pallas_call | solution.py:91
  42.8 2.4 collective-permute-start.8
  46.3 1.9 collective-permute-done.8
  48.2 2.1 collective-permute-done.9
  50.3 1.6 collective-permute-start.10
  52.0 2.9 %collective-permute-start.11 = (f32[8192]{0:T(1024)S(1)}, f32[8192]{0:T(1024)S(1)}, u32[]{:S(2)}, u32[]{:S(2)}) collective-permute-start(f32[8192]{0:T(1024)S(1)} %add_add_fusion.2), channel_id=1, source_target_pairs={{0,64},{32,96},{64,0},{96,32},{1,65},{33,97},{65,1},{97,33},{2,66}... | collective-permute-start | bytes 98312 | tf_op jit(solution)/shard_map/ppermute | solution.py:25
  59.4 7.6 %shard_map.59 = f32[512,1]{1,0:T(8,128)} custom-call(bf16[512,8192]{1,0:T(8,128)(2,1)} %get-tuple-element.8.k_ref, f32[1,8192]{1,0:T(1,128)} %bitcast.126), custom_call_target="tpu_custom_call" | custom-call | tf_op jit(solution)/shard_map/pallas_call | solution.py:152
  69.0 3.3 %collective-permute-start.14 = (f32[2,512]{1,0:T(2,128)S(1)}, f32[2,512]{1,0:T(2,128)S(1)}, u32[]{:S(2)}, u32[]{:S(2)}) collective-permute-start(f32[2,512]{1,0:T(2,128)S(1)} %pad_maximum_fusion.1), channel_id=1, source_target_pairs={{0,2},{1,3},{2,0},{3,1},{4,6},{5,7},{6,4},{7,5},{8,10},{9,11},{10,... | collective-permute-start | bytes 12296 | tf_op jit(solution)/shard_map/ppermute | solution.py:25
  74.1 1.8 collective-permute-done.15
  76.8 6.9 %shard_map.60 = f32[1,8192]{1,0:T(1,128)} custom-call(bf16[512,8192]{1,0:T(8,128)(2,1)} %get-tuple-element.8.k_ref, f32[512,1]{1,0:T(8,128)} %copy.13.r_ref), custom_call_target="tpu_custom_call" | custom-call | tf_op jit(solution)/shard_map/pallas_call | solution.py:129
  87.9 1.9 collective-permute-done.17
  89.8 2.1 collective-permute-done.18
  92.8 3.8 %collective-permute-start.21 = (f32[8192]{0:T(1024)S(1)}, f32[8192]{0:T(1024)S(1)}, u32[]{:S(2)}, u32[]{:S(2)}) collective-permute-start(f32[8192]{0:T(1024)S(1)} %add_add_fusion.1), channel_id=1, source_target_pairs={{0,64},{32,96},{64,0},{96,32},{1,65},{33,97},{65,1},{97,33},{2,66}... | collective-permute-start | bytes 98312 | tf_op jit(solution)/shard_map/ppermute | solution.py:25
  98.9 1.7 collective-permute-done.22
  101.2 7.6 %shard_map.61 = f32[512,1]{1,0:T(8,128)} custom-call(bf16[512,8192]{1,0:T(8,128)(2,1)} %get-tuple-element.8.k_ref, f32[1,8192]{1,0:T(1,128)} %bitcast.127), custom_call_target="tpu_custom_call" | custom-call | tf_op jit(solution)/shard_map/pallas_call | solution.py:152
  109.9 2.7 %collective-permute-start.24 = (f32[512]{0:T(512)S(1)}, f32[512]{0:T(512)S(1)}, u32[]{:S(2)}, u32[]{:S(2)}) collective-permute-start(f32[512]{0:T(512)S(1)} %reduce.3), channel_id=1, source_target_pairs={{0,2},{1,3},{2,0},{3,1},{4,6},{5,7},{6,4},{7,5},{8,10},{9,11},{10,... | collective-permute-start | bytes 6152 | tf_op jit(solution)/shard_map/ppermute | solution.py:25
  112.6 1.5 collective-permute-start.25
  117.0 7.0 %shard_map.62 = f32[1,8192]{1,0:T(1,128)} custom-call(bf16[512,8192]{1,0:T(8,128)(2,1)} %get-tuple-element.8.k_ref, f32[512,1]{1,0:T(8,128)} %copy.14.r_ref), custom_call_target="tpu_custom_call" | custom-call | tf_op jit(solution)/shard_map/pallas_call | solution.py:129
  126.2 2.0 collective-permute-start.27
  130.3 3.2 %collective-permute-done.28 = f32[8192]{0:T(1024)S(1)} collective-permute-done((f32[8192]{0:T(1024)S(1)}, f32[8192]{0:T(1024)S(1)}, u32[]{:S(2)}, u32[]{:S(2)}) %collective-permute-start.28) | collective-permute-done | bytes 32800 | tf_op jit(solution)/shard_map/ppermute | solution.py:25
  134.3 2.7 %collective-permute-start.31 = (f32[8192]{0:T(1024)S(1)}, f32[8192]{0:T(1024)S(1)}, u32[]{:S(2)}, u32[]{:S(2)}) collective-permute-start(f32[8192]{0:T(1024)S(1)} %add_add_fusion), channel_id=1, source_target_pairs={{0,64},{32,96},{64,0},{96,32},{1,65},{33,97},{65,1},{97,33},{2,66}... | collective-permute-start | bytes 98312 | tf_op jit(solution)/shard_map/ppermute | solution.py:25
  141.6 7.6 %shard_map.63 = f32[512,1]{1,0:T(8,128)} custom-call(bf16[512,8192]{1,0:T(8,128)(2,1)} %get-tuple-element.8.k_ref, f32[1,8192]{1,0:T(1,128)} %bitcast.119), custom_call_target="tpu_custom_call" | custom-call | tf_op jit(solution)/shard_map/pallas_call | solution.py:152
  150.3 1.5 collective-permute-start.33
  151.8 2.7 %collective-permute-start.34 = (f32[512]{0:T(512)S(1)}, f32[512]{0:T(512)S(1)}, u32[]{:S(2)}, u32[]{:S(2)}) collective-permute-start(f32[512]{0:T(512)S(1)} %reduce.4), channel_id=1, source_target_pairs={{0,2},{1,3},{2,0},{3,1},{4,6},{5,7},{6,4},{7,5},{8,10},{9,11},{10,... | collective-permute-start | bytes 6152 | tf_op jit(solution)/shard_map/ppermute | solution.py:25
  155.1 1.7 collective-permute-done.34
  158.1 10.8 %multiply_convert_fusion = (bf16[512,8192]{1,0:T(8,128)(2,1)S(1)}, bf16[512,8192]{1,0:T(8,128)(2,1)}) fusion(f32[512,8192]{1,0:T(8,128)} %get-tuple-element.7, f32[512]{0:T(512)S(1)} %bitcast.138, f32[512]{0:T(512)S(1)} %add_divide_fusion.3, f32[8192]{0:T(1024)S(1)} %copy-done.6), kind=kLoop, calls=%fused_computation.1 | loop fusion | flops 37748736 | bytes 33591296 | tf_op jit(solution)/shard_map/convert_element_type | solution.py:190
  168.9 2.5 fusion.2
  171.7 3.2 %fusion.36 = (bf16[512,256]{1,0:T(8,128)(2,1)}, f32[512,256]{1,0:T(8,128)}) fusion(bf16[512,8192]{1,0:T(8,128)(2,1)S(1)} %get-tuple-element.13, bf16[256,8192]{1,0:T(8,128)(2,1)S(1)} %copy-done.3), kind=kOutput, calls=%fused_computation.92 | convolution fusion | flops 2147614720 | bytes 13369344 | tf_op jit(solution)/shard_map/dot_general | solution.py:195
  175.0 2.7 %collective-permute-start.44 = (bf16[512,256]{1,0:T(8,128)(2,1)}, bf16[512,256]{1,0:T(8,128)(2,1)}, u32[]{:S(2)}, u32[]{:S(2)}) collective-permute-start(bf16[512,256]{1,0:T(8,128)(2,1)} %get-tuple-element.32), channel_id=1, source_target_pairs={{0,2},{1,3},{2,0},{3,1},{4,6},{5,7},{6,4},{7,5},{8,10},{9,11},{10,... | collective-permute-start | bytes 786440 | tf_op jit(solution)/shard_map/ppermute | solution.py:25
  179.1 11.6 %collective-permute-done.43 = bf16[512,256]{1,0:T(8,128)(2,1)S(1)} collective-permute-done((bf16[512,256]{1,0:T(8,128)(2,1)}, bf16[512,256]{1,0:T(8,128)(2,1)S(1)}, u32[]{:S(2)}, u32[]{:S(2)}) %collective-permute-start.43) | collective-permute-done | bytes 262176 | tf_op jit(solution)/shard_map/ppermute | solution.py:25
  192.8 1.8 fusion.10
  194.8 3.2 %bitcast_add_fusion = f32[4,4,8,8192]{3,2,1,0:T(8,128)S(1)} fusion(bf16[4,4,8,8192]{3,2,1,0:T(8,128)(2,1)} %collective-permute-done.36, f32[4,4,2,8,8192]{4,3,2,1,0:T(8,128)} %copy-done.1, s32[]{:T(128)S(6)} %select_n.148), kind=kLoop, calls=%fused_computation.10 | loop fusion | flops 2097152 | bytes 10485764 | tf_op jit(solution)/shard_map/add | solution.py:50
  198.0 1.9 copy-done.4
  203.8 1.9 collective-permute-start.47
  207.1 19.8 %collective-permute-done.47 = bf16[4,8,512]{2,1,0:T(8,128)(2,1)S(1)} collective-permute-done((bf16[4,8,512]{2,1,0:T(8,128)(2,1)S(1)}, bf16[4,8,512]{2,1,0:T(8,128)(2,1)S(1)}, u32[]{:S(2)}, u32[]{:S(2)}) %collective-permute-start.47) | collective-permute-done | bytes 32800 | tf_op jit(solution)/shard_map/ppermute | solution.py:25
  226.9 1.5 collective-permute-done.48
  228.4 3.6 %collective-permute-done.49 = bf16[4,8,512]{2,1,0:T(8,128)(2,1)S(1)} collective-permute-done((bf16[4,8,512]{2,1,0:T(8,128)(2,1)S(1)}, bf16[4,8,512]{2,1,0:T(8,128)(2,1)S(1)}, u32[]{:S(2)}, u32[]{:S(2)}) %collective-permute-start.49) | collective-permute-done | bytes 32800 | tf_op jit(solution)/shard_map/ppermute | solution.py:25
  233.4 2.7 %collective-permute-start.51 = (bf16[8,512]{1,0:T(8,128)(2,1)S(1)}, bf16[8,512]{1,0:T(8,128)(2,1)S(1)}, u32[]{:S(2)}, u32[]{:S(2)}) collective-permute-start(bf16[8,512]{1,0:T(8,128)(2,1)S(1)} %get-tuple-element.29), channel_id=1, source_target_pairs={{0,64},{32,96},{64,0},{96,32},{1,65},{33,97},{65,1},{97,33},{2,66}... | collective-permute-start | bytes 24584 | tf_op jit(solution)/shard_map/ppermute | solution.py:25
  236.2 1.6 fusion.6
  237.9 2.0 collective-permute-start.40
  240.7 2.0 collective-permute-start.42
  244.2 2.2 collective-permute-done.41
  (129 shorter events, 59.5 us)
Async XLA Ops:
  3.1 12.6 %collective-permute-start = (f32[128,256]{1,0:T(8,128)S(1)}, f32[128,256]{1,0:T(8,128)S(1)}, u32[]{:S(2)}, u32[]{:S(2)}) collective-permute-start(f32[128,256]{1,0:T(8,128)S(1)} %get-tuple-element.21), channel_id=1, source_target_pairs={{0,1},{1,2},{2,3},{3,0},{4,5},{5,6},{6,7},{7,4},{8,9},{9,10},{10,1... | collective-permute-start | bytes 393224 | tf_op jit(solution)/shard_map/ppermute | solution.py:25
  5.1 10.6 %collective-permute-start.1 = (f32[128,256]{1,0:T(8,128)S(1)}, f32[128,256]{1,0:T(8,128)S(1)}, u32[]{:S(2)}, u32[]{:S(2)}) collective-permute-start(f32[128,256]{1,0:T(8,128)S(1)} %get-tuple-element.23), channel_id=1, source_target_pairs={{0,2},{1,3},{2,0},{3,1},{4,6},{5,7},{6,4},{7,5},{8,10},{9,11},{10,... | collective-permute-start | bytes 393224 | tf_op jit(solution)/shard_map/ppermute | solution.py:25
  8.7 7.0 %collective-permute-start.2 = (f32[128,256]{1,0:T(8,128)S(1)}, f32[128,256]{1,0:T(8,128)S(1)}, u32[]{:S(2)}, u32[]{:S(2)}) collective-permute-start(f32[128,256]{1,0:T(8,128)S(1)} %get-tuple-element.22), channel_id=1, source_target_pairs={{0,3},{1,0},{2,1},{3,2},{4,7},{5,4},{6,5},{7,6},{8,11},{9,8},{10,9... | collective-permute-start | bytes 393224 | tf_op jit(solution)/shard_map/ppermute | solution.py:25
  15.8 8.7 %collective-permute-start.3 = (f32[128,256]{1,0:T(8,128)S(1)}, f32[128,256]{1,0:T(8,128)S(1)}, u32[]{:S(2)}, u32[]{:S(2)}) collective-permute-start(f32[128,256]{1,0:T(8,128)S(1)} %fusion.20), channel_id=1, source_target_pairs={{0,1},{1,2},{2,3},{3,0},{4,5},{5,6},{6,7},{7,4},{8,9},{9,10},{10,1... | collective-permute-start | bytes 393224 | tf_op jit(solution)/shard_map/ppermute | solution.py:25
  16.9 7.6 %collective-permute-start.4 = (f32[128,256]{1,0:T(8,128)S(1)}, f32[128,256]{1,0:T(8,128)S(1)}, u32[]{:S(2)}, u32[]{:S(2)}) collective-permute-start(f32[128,256]{1,0:T(8,128)S(1)} %fusion.20), channel_id=1, source_target_pairs={{0,2},{1,3},{2,0},{3,1},{4,6},{5,7},{6,4},{7,5},{8,10},{9,11},{10,... | collective-permute-start | bytes 393224 | tf_op jit(solution)/shard_map/ppermute | solution.py:25
  18.4 6.4 %collective-permute-start.5 = (f32[128,256]{1,0:T(8,128)S(1)}, f32[128,256]{1,0:T(8,128)S(1)}, u32[]{:S(2)}, u32[]{:S(2)}) collective-permute-start(f32[128,256]{1,0:T(8,128)S(1)} %fusion.20), channel_id=1, source_target_pairs={{0,3},{1,0},{2,1},{3,2},{4,7},{5,4},{6,5},{7,6},{8,11},{9,8},{10,9... | collective-permute-start | bytes 393224 | tf_op jit(solution)/shard_map/ppermute | solution.py:25
  42.3 4.0 %collective-permute-start.7 = (f32[8192]{0:T(1024)S(1)}, f32[8192]{0:T(1024)S(1)}, u32[]{:S(2)}, u32[]{:S(2)}) collective-permute-start(f32[8192]{0:T(1024)S(1)} %add.349), channel_id=1, source_target_pairs={{0,8},{8,16},{16,24},{24,0},{1,9},{9,17},{17,25},{25,1},{2,10},{10... | collective-permute-start | bytes 98312 | tf_op jit(solution)/shard_map/ppermute | solution.py:25
  42.8 5.4 %collective-permute-start.8 = (f32[8192]{0:T(1024)S(1)}, f32[8192]{0:T(1024)S(1)}, u32[]{:S(2)}, u32[]{:S(2)}) collective-permute-start(f32[8192]{0:T(1024)S(1)} %add.349), channel_id=1, source_target_pairs={{0,16},{8,24},{16,0},{24,8},{1,17},{9,25},{17,1},{25,9},{2,18},{10... | collective-permute-start | bytes 98312 | tf_op jit(solution)/shard_map/ppermute | solution.py:25
  45.2 5.1 %collective-permute-start.9 = (f32[8192]{0:T(1024)S(1)}, f32[8192]{0:T(1024)S(1)}, u32[]{:S(2)}, u32[]{:S(2)}) collective-permute-start(f32[8192]{0:T(1024)S(1)} %add.349), channel_id=1, source_target_pairs={{0,24},{8,0},{16,8},{24,16},{1,25},{9,1},{17,9},{25,17},{2,26},{10... | collective-permute-start | bytes 98312 | tf_op jit(solution)/shard_map/ppermute | solution.py:25
  50.3 7.0 %collective-permute-start.10 = (f32[8192]{0:T(1024)S(1)}, f32[8192]{0:T(1024)S(1)}, u32[]{:S(2)}, u32[]{:S(2)}) collective-permute-start(f32[8192]{0:T(1024)S(1)} %add_add_fusion.2), channel_id=1, source_target_pairs={{0,32},{32,64},{64,96},{96,0},{1,33},{33,65},{65,97},{97,1},{2,34}... | collective-permute-start | bytes 98312 | tf_op jit(solution)/shard_map/ppermute | solution.py:25
  52.0 5.4 %collective-permute-start.11 = (f32[8192]{0:T(1024)S(1)}, f32[8192]{0:T(1024)S(1)}, u32[]{:S(2)}, u32[]{:S(2)}) collective-permute-start(f32[8192]{0:T(1024)S(1)} %add_add_fusion.2), channel_id=1, source_target_pairs={{0,64},{32,96},{64,0},{96,32},{1,65},{33,97},{65,1},{97,33},{2,66}... | collective-permute-start | bytes 98312 | tf_op jit(solution)/shard_map/ppermute | solution.py:25
  54.9 3.9 %collective-permute-start.12 = (f32[8192]{0:T(1024)S(1)}, f32[8192]{0:T(1024)S(1)}, u32[]{:S(2)}, u32[]{:S(2)}) collective-permute-start(f32[8192]{0:T(1024)S(1)} %add_add_fusion.2), channel_id=1, source_target_pairs={{0,96},{32,0},{64,32},{96,64},{1,97},{33,1},{65,33},{97,65},{2,98}... | collective-permute-start | bytes 98312 | tf_op jit(solution)/shard_map/ppermute | solution.py:25
  68.1 4.9 %collective-permute-start.13 = (f32[2,512]{1,0:T(2,128)S(1)}, f32[2,512]{1,0:T(2,128)S(1)}, u32[]{:S(2)}, u32[]{:S(2)}) collective-permute-start(f32[2,512]{1,0:T(2,128)S(1)} %pad_maximum_fusion.1), channel_id=1, source_target_pairs={{0,1},{1,2},{2,3},{3,0},{4,5},{5,6},{6,7},{7,4},{8,9},{9,10},{10,1... | collective-permute-start | bytes 12296 | tf_op jit(solution)/shard_map/ppermute | solution.py:25
  69.0 5.1 %collective-permute-start.14 = (f32[2,512]{1,0:T(2,128)S(1)}, f32[2,512]{1,0:T(2,128)S(1)}, u32[]{:S(2)}, u32[]{:S(2)}) collective-permute-start(f32[2,512]{1,0:T(2,128)S(1)} %pad_maximum_fusion.1), channel_id=1, source_target_pairs={{0,2},{1,3},{2,0},{3,1},{4,6},{5,7},{6,4},{7,5},{8,10},{9,11},{10,... | collective-permute-start | bytes 12296 | tf_op jit(solution)/shard_map/ppermute | solution.py:25
  72.3 3.6 %collective-permute-start.15 = (f32[2,512]{1,0:T(2,128)S(1)}, f32[2,512]{1,0:T(2,128)S(1)}, u32[]{:S(2)}, u32[]{:S(2)}) collective-permute-start(f32[2,512]{1,0:T(2,128)S(1)} %pad_maximum_fusion.1), channel_id=1, source_target_pairs={{0,3},{1,0},{2,1},{3,2},{4,7},{5,4},{6,5},{7,6},{8,11},{9,8},{10,9... | collective-permute-start | bytes 12296 | tf_op jit(solution)/shard_map/ppermute | solution.py:25
  85.9 3.9 %collective-permute-start.17 = (f32[8192]{0:T(1024)S(1)}, f32[8192]{0:T(1024)S(1)}, u32[]{:S(2)}, u32[]{:S(2)}) collective-permute-start(f32[8192]{0:T(1024)S(1)} %add.359), channel_id=1, source_target_pairs={{0,8},{8,16},{16,24},{24,0},{1,9},{9,17},{17,25},{25,1},{2,10},{10... | collective-permute-start | bytes 98312 | tf_op jit(solution)/shard_map/ppermute | solution.py:25
  86.5 5.4 %collective-permute-start.18 = (f32[8192]{0:T(1024)S(1)}, f32[8192]{0:T(1024)S(1)}, u32[]{:S(2)}, u32[]{:S(2)}) collective-permute-start(f32[8192]{0:T(1024)S(1)} %add.359), channel_id=1, source_target_pairs={{0,16},{8,24},{16,0},{24,8},{1,17},{9,25},{17,1},{25,9},{2,18},{10... | collective-permute-start | bytes 98312 | tf_op jit(solution)/shard_map/ppermute | solution.py:25
  87.4 5.1 %collective-permute-start.19 = (f32[8192]{0:T(1024)S(1)}, f32[8192]{0:T(1024)S(1)}, u32[]{:S(2)}, u32[]{:S(2)}) collective-permute-start(f32[8192]{0:T(1024)S(1)} %add.359), channel_id=1, source_target_pairs={{0,24},{8,0},{16,8},{24,16},{1,25},{9,1},{17,9},{25,17},{2,26},{10... | collective-permute-start | bytes 98312 | tf_op jit(solution)/shard_map/ppermute | solution.py:25
  92.5 5.2 %collective-permute-start.20 = (f32[8192]{0:T(1024)S(1)}, f32[8192]{0:T(1024)S(1)}, u32[]{:S(2)}, u32[]{:S(2)}) collective-permute-start(f32[8192]{0:T(1024)S(1)} %add_add_fusion.1), channel_id=1, source_target_pairs={{0,32},{32,64},{64,96},{96,0},{1,33},{33,65},{65,97},{97,1},{2,34}... | collective-permute-start | bytes 98312 | tf_op jit(solution)/shard_map/ppermute | solution.py:25
  92.8 6.1 %collective-permute-start.21 = (f32[8192]{0:T(1024)S(1)}, f32[8192]{0:T(1024)S(1)}, u32[]{:S(2)}, u32[]{:S(2)}) collective-permute-start(f32[8192]{0:T(1024)S(1)} %add_add_fusion.1), channel_id=1, source_target_pairs={{0,64},{32,96},{64,0},{96,32},{1,65},{33,97},{65,1},{97,33},{2,66}... | collective-permute-start | bytes 98312 | tf_op jit(solution)/shard_map/ppermute | solution.py:25
  96.6 3.9 %collective-permute-start.22 = (f32[8192]{0:T(1024)S(1)}, f32[8192]{0:T(1024)S(1)}, u32[]{:S(2)}, u32[]{:S(2)}) collective-permute-start(f32[8192]{0:T(1024)S(1)} %add_add_fusion.1), channel_id=1, source_target_pairs={{0,96},{32,0},{64,32},{96,64},{1,97},{33,1},{65,33},{97,65},{2,98}... | collective-permute-start | bytes 98312 | tf_op jit(solution)/shard_map/ppermute | solution.py:25
  109.8 4.9 %collective-permute-start.23 = (f32[512]{0:T(512)S(1)}, f32[512]{0:T(512)S(1)}, u32[]{:S(2)}, u32[]{:S(2)}) collective-permute-start(f32[512]{0:T(512)S(1)} %reduce.3), channel_id=1, source_target_pairs={{0,1},{1,2},{2,3},{3,0},{4,5},{5,6},{6,7},{7,4},{8,9},{9,10},{10,1... | collective-permute-start | bytes 6152 | tf_op jit(solution)/shard_map/ppermute | solution.py:25
  109.9 5.2 %collective-permute-start.24 = (f32[512]{0:T(512)S(1)}, f32[512]{0:T(512)S(1)}, u32[]{:S(2)}, u32[]{:S(2)}) collective-permute-start(f32[512]{0:T(512)S(1)} %reduce.3), channel_id=1, source_target_pairs={{0,2},{1,3},{2,0},{3,1},{4,6},{5,7},{6,4},{7,5},{8,10},{9,11},{10,... | collective-permute-start | bytes 6152 | tf_op jit(solution)/shard_map/ppermute | solution.py:25
  126.2 4.2 %collective-permute-start.27 = (f32[8192]{0:T(1024)S(1)}, f32[8192]{0:T(1024)S(1)}, u32[]{:S(2)}, u32[]{:S(2)}) collective-permute-start(f32[8192]{0:T(1024)S(1)} %add.369), channel_id=1, source_target_pairs={{0,8},{8,16},{16,24},{24,0},{1,9},{9,17},{17,25},{25,1},{2,10},{10... | collective-permute-start | bytes 98312 | tf_op jit(solution)/shard_map/ppermute | solution.py:25
  128.2 5.4 %collective-permute-start.28 = (f32[8192]{0:T(1024)S(1)}, f32[8192]{0:T(1024)S(1)}, u32[]{:S(2)}, u32[]{:S(2)}) collective-permute-start(f32[8192]{0:T(1024)S(1)} %add.369), channel_id=1, source_target_pairs={{0,16},{8,24},{16,0},{24,8},{1,17},{9,25},{17,1},{25,9},{2,18},{10... | collective-permute-start | bytes 98312 | tf_op jit(solution)/shard_map/ppermute | solution.py:25
  129.1 5.1 %collective-permute-start.29 = (f32[8192]{0:T(1024)S(1)}, f32[8192]{0:T(1024)S(1)}, u32[]{:S(2)}, u32[]{:S(2)}) collective-permute-start(f32[8192]{0:T(1024)S(1)} %add.369), channel_id=1, source_target_pairs={{0,24},{8,0},{16,8},{24,16},{1,25},{9,1},{17,9},{25,17},{2,26},{10... | collective-permute-start | bytes 98312 | tf_op jit(solution)/shard_map/ppermute | solution.py:25
  134.2 5.2 %collective-permute-start.30 = (f32[8192]{0:T(1024)S(1)}, f32[8192]{0:T(1024)S(1)}, u32[]{:S(2)}, u32[]{:S(2)}) collective-permute-start(f32[8192]{0:T(1024)S(1)} %add_add_fusion), channel_id=1, source_target_pairs={{0,32},{32,64},{64,96},{96,0},{1,33},{33,65},{65,97},{97,1},{2,34}... | collective-permute-start | bytes 98312 | tf_op jit(solution)/shard_map/ppermute | solution.py:25
  134.3 5.4 %collective-permute-start.31 = (f32[8192]{0:T(1024)S(1)}, f32[8192]{0:T(1024)S(1)}, u32[]{:S(2)}, u32[]{:S(2)}) collective-permute-start(f32[8192]{0:T(1024)S(1)} %add_add_fusion), channel_id=1, source_target_pairs={{0,64},{32,96},{64,0},{96,32},{1,65},{33,97},{65,1},{97,33},{2,66}... | collective-permute-start | bytes 98312 | tf_op jit(solution)/shard_map/ppermute | solution.py:25
  137.1 3.9 %collective-permute-start.32 = (f32[8192]{0:T(1024)S(1)}, f32[8192]{0:T(1024)S(1)}, u32[]{:S(2)}, u32[]{:S(2)}) collective-permute-start(f32[8192]{0:T(1024)S(1)} %add_add_fusion), channel_id=1, source_target_pairs={{0,96},{32,0},{64,32},{96,64},{1,97},{33,1},{65,33},{97,65},{2,98}... | collective-permute-start | bytes 98312 | tf_op jit(solution)/shard_map/ppermute | solution.py:25
  150.3 4.9 %collective-permute-start.33 = (f32[512]{0:T(512)S(1)}, f32[512]{0:T(512)S(1)}, u32[]{:S(2)}, u32[]{:S(2)}) collective-permute-start(f32[512]{0:T(512)S(1)} %reduce.4), channel_id=1, source_target_pairs={{0,1},{1,2},{2,3},{3,0},{4,5},{5,6},{6,7},{7,4},{8,9},{9,10},{10,1... | collective-permute-start | bytes 6152 | tf_op jit(solution)/shard_map/ppermute | solution.py:25
  151.8 5.1 %collective-permute-start.34 = (f32[512]{0:T(512)S(1)}, f32[512]{0:T(512)S(1)}, u32[]{:S(2)}, u32[]{:S(2)}) collective-permute-start(f32[512]{0:T(512)S(1)} %reduce.4), channel_id=1, source_target_pairs={{0,2},{1,3},{2,0},{3,1},{4,6},{5,7},{6,4},{7,5},{8,10},{9,11},{10,... | collective-permute-start | bytes 6152 | tf_op jit(solution)/shard_map/ppermute | solution.py:25
  171.6 23.2 %collective-permute-start.36 = (bf16[4,4,8,8192]{3,2,1,0:T(8,128)(2,1)S(1)}, bf16[4,4,8,8192]{3,2,1,0:T(8,128)(2,1)}, u32[]{:S(2)}, u32[]{:S(2)}) collective-permute-start(bf16[4,4,8,8192]{3,2,1,0:T(8,128)(2,1)S(1)} %fusion.4), channel_id=1, source_target_pairs={{0,4},{4,0},{1,5},{5,1},{2,6},{6,2},{3,7},{7,3},{8,12},{12,8},{9,1... | collective-permute-start | bytes 6291464 | tf_op jit(solution)/shard_map/ppermute | solution.py:25
  175.0 15.7 %collective-permute-start.43 = (bf16[512,256]{1,0:T(8,128)(2,1)}, bf16[512,256]{1,0:T(8,128)(2,1)S(1)}, u32[]{:S(2)}, u32[]{:S(2)}) collective-permute-start(bf16[512,256]{1,0:T(8,128)(2,1)} %get-tuple-element.32), channel_id=1, source_target_pairs={{0,1},{1,2},{2,3},{3,0},{4,5},{5,6},{6,7},{7,4},{8,9},{9,10},{10,1... | collective-permute-start | bytes 786440 | tf_op jit(solution)/shard_map/ppermute | solution.py:25
  175.0 15.7 %collective-permute-start.44 = (bf16[512,256]{1,0:T(8,128)(2,1)}, bf16[512,256]{1,0:T(8,128)(2,1)}, u32[]{:S(2)}, u32[]{:S(2)}) collective-permute-start(bf16[512,256]{1,0:T(8,128)(2,1)} %get-tuple-element.32), channel_id=1, source_target_pairs={{0,2},{1,3},{2,0},{3,1},{4,6},{5,7},{6,4},{7,5},{8,10},{9,11},{10,... | collective-permute-start | bytes 786440 | tf_op jit(solution)/shard_map/ppermute | solution.py:25
  177.7 13.7 %collective-permute-start.45 = (bf16[512,256]{1,0:T(8,128)(2,1)}, bf16[512,256]{1,0:T(8,128)(2,1)}, u32[]{:S(2)}, u32[]{:S(2)}) collective-permute-start(bf16[512,256]{1,0:T(8,128)(2,1)} %get-tuple-element.32), channel_id=1, source_target_pairs={{0,3},{1,0},{2,1},{3,2},{4,7},{5,4},{6,5},{7,6},{8,11},{9,8},{10,9... | collective-permute-start | bytes 786440 | tf_op jit(solution)/shard_map/ppermute | solution.py:25
  194.7 8.4 %collective-permute-start.46 = (bf16[4,4,8,512]{3,2,0,1:T(8,128)(2,1)S(1)}, bf16[4,4,8,512]{3,2,0,1:T(8,128)(2,1)S(1)}, u32[]{:S(2)}, u32[]{:S(2)}) collective-permute-start(bf16[4,4,8,512]{3,2,0,1:T(8,128)(2,1)S(1)} %fusion.18), channel_id=1, source_target_pairs={{0,4},{4,0},{1,5},{5,1},{2,6},{6,2},{3,7},{7,3},{8,12},{12,8},{9,1... | collective-permute-start | bytes 393224 | tf_op jit(solution)/shard_map/ppermute | solution.py:25
  200.2 35.9 %collective-permute-start.37 = (bf16[4,8,8192]{2,1,0:T(8,128)(2,1)S(1)}, bf16[4,8,8192]{2,1,0:T(8,128)(2,1)S(1)}, u32[]{:S(2)}, u32[]{:S(2)}) collective-permute-start(bf16[4,8,8192]{2,1,0:T(8,128)(2,1)S(1)} %get-tuple-element.15), channel_id=1, source_target_pairs={{0,8},{8,16},{16,24},{24,0},{1,9},{9,17},{17,25},{25,1},{2,10},{10... | collective-permute-start | bytes 1572872 | tf_op jit(solution)/shard_map/ppermute | solution.py:25
  200.8 35.4 %collective-permute-start.38 = (bf16[4,8,8192]{2,1,0:T(8,128)(2,1)S(1)}, bf16[4,8,8192]{2,1,0:T(8,128)(2,1)S(1)}, u32[]{:S(2)}, u32[]{:S(2)}) collective-permute-start(bf16[4,8,8192]{2,1,0:T(8,128)(2,1)S(1)} %get-tuple-element.17), channel_id=1, source_target_pairs={{0,16},{8,24},{16,0},{24,8},{1,17},{9,25},{17,1},{25,9},{2,18},{10... | collective-permute-start | bytes 1572872 | tf_op jit(solution)/shard_map/ppermute | solution.py:25
  201.8 34.5 %collective-permute-start.39 = (bf16[4,8,8192]{2,1,0:T(8,128)(2,1)S(1)}, bf16[4,8,8192]{2,1,0:T(8,128)(2,1)}, u32[]{:S(2)}, u32[]{:S(2)}) collective-permute-start(bf16[4,8,8192]{2,1,0:T(8,128)(2,1)S(1)} %get-tuple-element.16), channel_id=1, source_target_pairs={{0,24},{8,0},{16,8},{24,16},{1,25},{9,1},{17,9},{25,17},{2,26},{10... | collective-permute-start | bytes 1572872 | tf_op jit(solution)/shard_map/ppermute | solution.py:25
  203.8 23.1 %collective-permute-start.47 = (bf16[4,8,512]{2,1,0:T(8,128)(2,1)S(1)}, bf16[4,8,512]{2,1,0:T(8,128)(2,1)S(1)}, u32[]{:S(2)}, u32[]{:S(2)}) collective-permute-start(bf16[4,8,512]{2,1,0:T(8,128)(2,1)S(1)} %get-tuple-element.24), channel_id=1, source_target_pairs={{0,8},{8,16},{16,24},{24,0},{1,9},{9,17},{17,25},{25,1},{2,10},{10... | collective-permute-start | bytes 98312 | tf_op jit(solution)/shard_map/ppermute | solution.py:25
  205.7 22.7 %collective-permute-start.48 = (bf16[4,8,512]{2,1,0:T(8,128)(2,1)}, bf16[4,8,512]{2,1,0:T(8,128)(2,1)S(1)}, u32[]{:S(2)}, u32[]{:S(2)}) collective-permute-start(bf16[4,8,512]{2,1,0:T(8,128)(2,1)} %get-tuple-element.26), channel_id=1, source_target_pairs={{0,16},{8,24},{16,0},{24,8},{1,17},{9,25},{17,1},{25,9},{2,18},{10... | collective-permute-start | bytes 98312 | tf_op jit(solution)/shard_map/ppermute | solution.py:25
  226.9 5.1 %collective-permute-start.49 = (bf16[4,8,512]{2,1,0:T(8,128)(2,1)S(1)}, bf16[4,8,512]{2,1,0:T(8,128)(2,1)S(1)}, u32[]{:S(2)}, u32[]{:S(2)}) collective-permute-start(bf16[4,8,512]{2,1,0:T(8,128)(2,1)S(1)} %get-tuple-element.25), channel_id=1, source_target_pairs={{0,24},{8,0},{16,8},{24,16},{1,25},{9,1},{17,9},{25,17},{2,26},{10... | collective-permute-start | bytes 98312 | tf_op jit(solution)/shard_map/ppermute | solution.py:25
  232.0 8.7 %collective-permute-start.50 = (bf16[8,512]{1,0:T(8,128)(2,1)S(1)}, bf16[8,512]{1,0:T(8,128)(2,1)S(1)}, u32[]{:S(2)}, u32[]{:S(2)}) collective-permute-start(bf16[8,512]{1,0:T(8,128)(2,1)S(1)} %get-tuple-element.27), channel_id=1, source_target_pairs={{0,32},{32,64},{64,96},{96,0},{1,33},{33,65},{65,97},{97,1},{2,34}... | collective-permute-start | bytes 24584 | tf_op jit(solution)/shard_map/ppermute | solution.py:25
  233.4 9.3 %collective-permute-start.51 = (bf16[8,512]{1,0:T(8,128)(2,1)S(1)}, bf16[8,512]{1,0:T(8,128)(2,1)S(1)}, u32[]{:S(2)}, u32[]{:S(2)}) collective-permute-start(bf16[8,512]{1,0:T(8,128)(2,1)S(1)} %get-tuple-element.29), channel_id=1, source_target_pairs={{0,64},{32,96},{64,0},{96,32},{1,65},{33,97},{65,1},{97,33},{2,66}... | collective-permute-start | bytes 24584 | tf_op jit(solution)/shard_map/ppermute | solution.py:25
  236.1 6.5 %collective-permute-start.52 = (bf16[8,512]{1,0:T(8,128)(2,1)S(1)}, bf16[8,512]{1,0:T(8,128)(2,1)S(1)}, u32[]{:S(2)}, u32[]{:S(2)}) collective-permute-start(bf16[8,512]{1,0:T(8,128)(2,1)S(1)} %get-tuple-element.28), channel_id=1, source_target_pairs={{0,96},{32,0},{64,32},{96,64},{1,97},{33,1},{65,33},{97,65},{2,98}... | collective-permute-start | bytes 24584 | tf_op jit(solution)/shard_map/ppermute | solution.py:25
  237.9 6.3 %collective-permute-start.40 = (bf16[8,8192]{1,0:T(8,128)(2,1)S(1)}, bf16[8,8192]{1,0:T(8,128)(2,1)S(1)}, u32[]{:S(2)}, u32[]{:S(2)}) collective-permute-start(bf16[8,8192]{1,0:T(8,128)(2,1)S(1)} %get-tuple-element.18), channel_id=1, source_target_pairs={{0,32},{32,64},{64,96},{96,0},{1,33},{33,65},{65,97},{97,1},{2,34}... | collective-permute-start | bytes 393224 | tf_op jit(solution)/shard_map/ppermute | solution.py:25
  239.9 6.5 %collective-permute-start.41 = (bf16[8,8192]{1,0:T(8,128)(2,1)S(1)}, bf16[8,8192]{1,0:T(8,128)(2,1)S(1)}, u32[]{:S(2)}, u32[]{:S(2)}) collective-permute-start(bf16[8,8192]{1,0:T(8,128)(2,1)S(1)} %get-tuple-element.20), channel_id=1, source_target_pairs={{0,64},{32,96},{64,0},{96,32},{1,65},{33,97},{65,1},{97,33},{2,66}... | collective-permute-start | bytes 393224 | tf_op jit(solution)/shard_map/ppermute | solution.py:25
  240.7 5.7 %collective-permute-start.42 = (bf16[8,8192]{1,0:T(8,128)(2,1)S(1)}, bf16[8,8192]{1,0:T(8,128)(2,1)S(1)}, u32[]{:S(2)}, u32[]{:S(2)}) collective-permute-start(bf16[8,8192]{1,0:T(8,128)(2,1)S(1)} %get-tuple-element.19), channel_id=1, source_target_pairs={{0,96},{32,0},{64,32},{96,64},{1,97},{33,1},{65,33},{97,65},{2,98}... | collective-permute-start | bytes 393224 | tf_op jit(solution)/shard_map/ppermute | solution.py:25
  (12 other events, 86.0 us)
